TPU v7x, 32 devices: a whole 2x2x4 slice. The times are simulated.
32 devices in a mesh: groups: 2 (over y), gx: 4 (over z), gy: 2 (over x), gz: 2 (over core).
Axes of the slice: x: 2, y: 2, z: 4, core: 2. Of those that a mesh axis runs over, the one named last changes fastest.
Arguments:
- coarse: bfloat16 [64, 16, 1024], P(('groups', 'gx'), ('gy', 'gz')), parts along dimension 0, may hold values from -6 to 6
- coarse_mask: int32 [64, 16, 16], P(('groups', 'gx'), ('gy', 'gz')), parts along dimension 0, may hold values 0 or 1
- brick_live: int32 [8, 2, 2], P(('groups', 'gx'), 'gy', 'gz'), parts along dimension 0, may hold values 0 or 1
- field: bfloat16 [128, 32, 2048], P(('groups', 'gx'), 'gy', 'gz'), parts along dimension 0, may hold values from -6 to 6
- coarse_weight: bfloat16 [64, 1728], replicated, may hold values from -0.15625 to 0.15625
- fine_weight_a: bfloat16 [64, 1728], replicated, may hold values from -0.15625 to 0.15625
- fine_weight_b: bfloat16 [64, 1728], replicated, may hold values from -0.15625 to 0.15625
- mod_weight: bfloat16 [64, 128], replicated, may hold values from -0.75 to 0.75
Outputs:
- decoded: bfloat16 [128, 32, 2048], P(('groups', 'gx'), 'gy', 'gz'), parts along dimension 0
There are 2 independent parts, one for each index of `groups`. A program takes and returns all parts, laid end to end along the dimension named above; an argument that names none is the same for every part. Nothing has to cross between parts.
All inputs are finite; a program needn't handle non-finite values. No bound on the sum of `coarse_mask` or of `brick_live` on one device may be relied on, other than what follows from the above.
Results may differ from a plain program's by a relative error of at most 0.0057.
Values may be sent and summed in bfloat16 or wider, within the bound.
No kernel may reach another device: no remote copies, remote signals or barrier semaphores. Data moves between devices by JAX's collectives and lax.ppermute only.
A program may use at most 64 MiB of HBM per device.

v0:
```python
import jax
import jax.numpy as jnp
from jax import lax
from jax.sharding import PartitionSpec as P

conv_layout = ("NDHWC", "DHWIO", "NDHWC")


def convolve(padded, weight):
    channels = weight.shape[0]
    kernel = weight.reshape(channels, 3, 3, 3, channels).transpose(1, 2, 3, 0, 4)
    result = lax.conv_general_dilated(
        padded[None],
        kernel,
        (1, 1, 1),
        "VALID",
        dimension_numbers=conv_layout,
        preferred_element_type=jnp.float32,
    )
    return result[0]


def shift_pairs(count, up):
    if up:
        return [(k, k + 1) for k in range(count - 1)]
    return [(k + 1, k) for k in range(count - 1)]


def grow(cells, axis, dim, width):
    count = lax.axis_size(axis)
    size = cells.shape[dim]
    head = lax.slice_in_dim(cells, 0, width, axis=dim)
    tail = lax.slice_in_dim(cells, size - width, size, axis=dim)
    low = lax.ppermute(tail, axis, shift_pairs(count, True))
    high = lax.ppermute(head, axis, shift_pairs(count, False))
    return jnp.concatenate([low, cells, high], axis=dim)


def doubled(volume):
    size_x, size_y, size_z, channels = volume.shape
    spread = jnp.broadcast_to(
        volume[:, None, :, None, :, None, :], (size_x, 2, size_y, 2, size_z, 2, channels)
    )
    return spread.reshape(2 * size_x, 2 * size_y, 2 * size_z, channels)


def body(
    coarse, coarse_mask, brick_live, field, coarse_weight, fine_weight_a, fine_weight_b, mod_weight
):
    channels = coarse_weight.shape[0]
    rows_x, rows_y, flat_z = coarse.shape
    cells_z = flat_z // channels
    edge = field.shape[0]
    half = edge // 2
    assert lax.axis_size("gz") == 2 and rows_x == half and 2 * rows_y == half
    lanes = 128
    zside = lax.axis_index("gz")
    first = zside == 0
    live = brick_live.reshape(())

    extra = jnp.concatenate(
        [
            coarse_mask.astype(jnp.bfloat16),
            jnp.broadcast_to(live.astype(jnp.bfloat16), (rows_x, rows_y, 1)),
            jnp.zeros((rows_x, rows_y, lanes - cells_z - 1), jnp.bfloat16),
        ],
        axis=2,
    )
    mine = jnp.concatenate([coarse, extra], axis=2)
    theirs = lax.ppermute(mine, "gz", [(0, 1), (1, 0)])
    column = jnp.where(first, jnp.concatenate([mine, theirs], 1), jnp.concatenate([theirs, mine], 1))
    live_other = theirs[0, 0, flat_z + cells_z]
    live_mine = live.astype(jnp.bfloat16)
    live_low = jnp.where(first, live_mine, live_other)
    live_high = jnp.where(first, live_other, live_mine)
    zcoarse = lax.broadcasted_iota(jnp.int32, (1, 1, cells_z), 2)
    live_z = jnp.where(zcoarse < half, live_low, live_high)
    keep = column[:, :, flat_z : flat_z + cells_z] * live_z
    packed = jnp.concatenate(
        [
            column[:, :, :flat_z],
            keep,
            jnp.zeros((rows_x, 2 * rows_y, lanes - cells_z), jnp.bfloat16),
        ],
        axis=2,
    )

    region = grow(grow(packed, "gy", 1, 2), "gx", 0, 2)
    size = region.shape[0]
    volume = region[:, :, :flat_z].reshape(size, size, cells_z, channels)
    volume = jnp.pad(volume, ((0, 0), (0, 0), (2, 2), (0, 0)))
    volume = lax.dynamic_slice_in_dim(volume, zside * half, half + 4, axis=2)
    keep = jnp.pad(region[:, :, flat_z : flat_z + cells_z], ((0, 0), (0, 0), (2, 2)))
    keep = lax.dynamic_slice_in_dim(keep, zside * half + 1, half + 2, axis=2)[1:-1, 1:-1]
    activity = convolve(volume, coarse_weight)
    centre = volume[1:-1, 1:-1, 1:-1].astype(jnp.float32)
    hidden = ((centre + jax.nn.silu(activity)) * keep[..., None].astype(jnp.float32)).astype(
        jnp.bfloat16
    )
    fine_input = doubled(hidden)

    product = jnp.dot(
        field.reshape(-1, channels), mod_weight, preferred_element_type=jnp.float32
    )
    gates = jax.nn.sigmoid(product).reshape(edge, edge, edge, 2 * channels) * live.astype(
        jnp.float32
    )
    gate_a = gates[..., :channels]
    gate_b = gates[..., channels:]
    face = jnp.where(first, gate_a[:, :, -1], gate_a[:, :, 0])
    face = lax.ppermute(face, "gz", [(0, 1), (1, 0)])[:, :, None]
    blank = jnp.zeros_like(face)
    gate_a = jnp.where(
        first,
        jnp.concatenate([blank, gate_a, face], 2),
        jnp.concatenate([face, gate_a, blank], 2),
    )
    gate_a = grow(grow(gate_a, "gy", 1, 1), "gx", 0, 1)

    first_act = convolve(fine_input, fine_weight_a)
    level_one = (
        fine_input[1:-1, 1:-1, 1:-1].astype(jnp.float32) + jax.nn.silu(first_act) * gate_a
    ).astype(jnp.bfloat16)
    second_act = convolve(level_one, fine_weight_b)
    result = (
        level_one[1:-1, 1:-1, 1:-1].astype(jnp.float32) + jax.nn.silu(second_act) * gate_b
    ).astype(jnp.bfloat16)
    return result.reshape(edge, edge, edge * channels)


def solution(mesh):
    in_specs = (
        P(("groups", "gx"), ("gy", "gz"), None),
        P(("groups", "gx"), ("gy", "gz"), None),
        P(("groups", "gx"), "gy", "gz"),
        P(("groups", "gx"), "gy", "gz"),
        P(),
        P(),
        P(),
        P(),
    )
    out_specs = P(("groups", "gx"), "gy", "gz")
    return jax.shard_map(body, mesh=mesh, in_specs=in_specs, out_specs=out_specs, check_vma=False)
```

profile of v0, /device:TPU:0, one launch (start us, length us, event | category | flops | bytes accessed | tf_op | source)
XLA Modules:
  0.0 120.7 jit_solution(11879110977698894161)
XLA Ops:
  2.9 1.8 %reshape.43 = bf16[4096,64]{1,0:T(8,128)(2,1)S(1)} reshape(bf16[16,16,1024]{2,1,0:T(8,128)(2,1)} %param.11) | data formatting | bytes 1048576 | tf_op jit(solution)/shard_map/reshape | solution.py:103
  7.8 2.2 %reshape.42 = bf16[64,3,3,3,64]{4,3,2,1,0:T(4,128)(2,1)} reshape(bf16[64,1728]{1,0:T(8,128)(2,1)} %param.13) | data formatting | bytes 442368 | tf_op jit(solution)/shard_map/reshape | solution.py:11
  10.0 2.2 %reshape.44 = bf16[64,3,3,3,64]{4,3,2,1,0:T(4,128)(2,1)} reshape(bf16[64,1728]{1,0:T(8,128)(2,1)} %param.14) | data formatting | bytes 442368 | tf_op jit(solution)/shard_map/reshape | solution.py:11
  13.6 2.6 %fusion.23 = f32[16,16,18,64]{3,2,1,0:T(8,128)S(1)} fusion(f32[16,16,16,64]{3,2,1,0:T(8,128)} %bitcast.59, f32[16,16,1,64]{3,2,1,0:T(1,128)} %bitcast.62, f32[16,16,1,64]{3,2,1,0:T(1,128)S(1)} %broadcast_in_dim.43, pred[]{:T(512)S(6)} %eq.3), kind=kLoop, calls=%fused_computation.28 | loop fusion | flops 1474560 | bytes 2359297 | tf_op jit(solution)/shard_map/jit(_where)/select_n | solution.py:113
  18.5 4.6 %collective-permute-start.1 = (bf16[8,2,1152]{2,1,0:T(2,128)(2,1)S(1)}, bf16[8,2,1152]{2,1,0:T(2,128)(2,1)S(1)}, u32[]{:S(2)}, u32[]{:S(2)}) collective-permute-start(bf16[8,2,1152]{2,1,0:T(2,128)(2,1)S(1)} %get-tuple-element.11), channel_id=1, source_target_pairs={{0,2},{1,3},{4,6},{5,7},{8,10},{9,11},{12,14},{13,15},{16,18},{17,... | collective-permute-start | bytes 110600 | tf_op jit(solution)/shard_map/ppermute | solution.py:34
  24.4 4.6 %collective-permute-start.6 = (f32[16,1,18,64]{3,2,1,0:T(8,128)S(1)}, f32[16,1,18,64]{3,2,1,0:T(8,128)S(1)}, u32[]{:S(2)}, u32[]{:S(2)}) collective-permute-start(f32[16,1,18,64]{3,2,1,0:T(8,128)S(1)} %get-tuple-element.7), channel_id=1, source_target_pairs={{0,2},{1,3},{4,6},{5,7},{8,10},{9,11},{12,14},{13,15},{16,18},{17,... | collective-permute-start | bytes 221192 | tf_op jit(solution)/shard_map/ppermute | solution.py:34
  30.3 3.5 %collective-permute-start.3 = (bf16[2,12,1152]{2,1,0:T(8,128)(2,1)S(1)}, bf16[2,12,1152]{2,1,0:T(8,128)(2,1)S(1)}, u32[]{:S(2)}, u32[]{:S(2)}) collective-permute-start(bf16[2,12,1152]{2,1,0:T(8,128)(2,1)S(1)} %get-tuple-element.9), channel_id=1, source_target_pairs={{0,4},{4,8},{8,12},{1,5},{5,9},{9,13},{2,6},{6,10},{10,14},{3,7},{... | collective-permute-start | bytes 165896 | tf_op jit(solution)/shard_map/ppermute | solution.py:34
  35.2 1.9 %collective-permute-done.7 = f32[16,1,18,64]{3,2,1,0:T(8,128)S(1)} collective-permute-done((f32[16,1,18,64]{3,2,1,0:T(8,128)S(1)}, f32[16,1,18,64]{3,2,1,0:T(8,128)S(1)}, u32[]{:S(2)}, u32[]{:S(2)}) %collective-permute-start.7) | collective-permute-done | bytes 73760 | tf_op jit(solution)/shard_map/ppermute | solution.py:35
  37.9 4.2 %collective-permute-start.8 = (f32[1,18,18,64]{3,2,1,0:T(8,128)}, f32[1,18,18,64]{3,2,1,0:T(8,128)}, u32[]{:S(2)}, u32[]{:S(2)}) collective-permute-start(f32[1,18,18,64]{3,2,1,0:T(8,128)} %get-tuple-element.5), channel_id=1, source_target_pairs={{0,4},{4,8},{8,12},{1,5},{5,9},{9,13},{2,6},{6,10},{10,14},{3,7},{... | collective-permute-start | bytes 248840 | tf_op jit(solution)/shard_map/ppermute | solution.py:34
  42.1 1.5 %collective-permute-start.9 = (f32[1,18,18,64]{3,2,1,0:T(8,128)}, f32[1,18,18,64]{3,2,1,0:T(8,128)}, u32[]{:S(2)}, u32[]{:S(2)}) collective-permute-start(f32[1,18,18,64]{3,2,1,0:T(8,128)} %get-tuple-element.6), channel_id=1, source_target_pairs={{4,0},{8,4},{12,8},{5,1},{9,5},{13,9},{6,2},{10,6},{14,10},{7,3},{... | collective-permute-start | bytes 248840 | tf_op jit(solution)/shard_map/ppermute | solution.py:35
  45.1 2.3 %reshape.39 = bf16[12,12,16,64]{3,2,1,0:T(8,128)(2,1)} reshape(bf16[12,12,1024]{2,1,0:T(8,128)(2,1)} %slice.95) | data formatting | bytes 589824 | tf_op jit(solution)/shard_map/reshape | solution.py:90
  48.8 5.4 %fusion.34 = f32[1,10,10,10,64]{4,0,3,2,1:T(1,128)S(1)} fusion(bf16[1,12,12,12,64]{4,3,2,1,0:T(8,128)(2,1)S(1)} %fusion.40, bf16[64,3,3,3,64]{4,3,2,1,0:T(4,128)(2,1)} %reshape.40), kind=kOutput, calls=%fused_computation.40 | convolution fusion | flops 221184000 | bytes 698368 | tf_op jit(solution)/shard_map/conv_general_dilated | solution.py:12
  55.1 2.4 %broadcast_in_dim.42 = bf16[10,2,10,2,10,2,64]{6,5,4,3,2,1,0:T(2,128)(2,1)} broadcast(bf16[10,10,10,64]{3,2,1,0:T(8,128)(2,1)S(1)} %multiply_convert_fusion), dimensions={0,2,4,6} | broadcast | bytes 1152000 | tf_op jit(solution)/shard_map/broadcast_in_dim | solution.py:41
  57.5 5.7 %reshape.74 = bf16[20,20,1,20,64]{4,3,1,0,2:T(8,128)(2,1)} reshape(bf16[10,2,10,2,10,2,64]{6,5,4,3,2,1,0:T(2,128)(2,1)} %broadcast_in_dim.42) | data formatting | bytes 2048000 | tf_op jit(solution)/shard_map/broadcast_in_dim;reshape | solution.py:13
  63.2 2.1 %copy.28 = bf16[20,20,1,20,64]{4,1,3,0,2:T(8,128)(2,1)S(1)} copy(bf16[20,20,1,20,64]{4,3,1,0,2:T(8,128)(2,1)} %reshape.74) | data formatting | bytes 2048000 | tf_op jit(solution)/shard_map/broadcast_in_dim;reshape | solution.py:13
  67.1 9.1 %broadcast_select_fusion = f32[18,18,8,3,64]{4,2,3,1,0:T(8,128)} fusion(pred[8,3]{0,1:T(4,128)(4,1)S(1)} %copy-done.21, bf16[20,20,1,7,2,64]{5,3,4,1,0,2:T(8,128)(2,1)S(1)} %slice.98, bf16[20,20,1,8,3,64]{5,3,4,1,0,2:T(8,128)(2,1)S(1)} %copy.18, bf16[64,3,3,3,64]{4,3,2,1,0:T(4,128)(2,1)S(1)} %copy-done.8), kind=kOutput, calls=%fused_computation.35 | convolution fusion | flops 1726568448 | bytes 4157464 | tf_op jit(solution)/shard_map/conv_general_dilated | solution.py:12
  76.2 5.7 %reshape.41 = bf16[20,20,20,64]{3,2,1,0:T(8,128)(2,1)} reshape(bf16[10,2,10,2,10,2,64]{6,5,4,3,2,1,0:T(2,128)(2,1)} %broadcast_in_dim.42) | data formatting | bytes 2048000 | tf_op jit(solution)/shard_map/reshape | solution.py:44
  81.9 6.1 %copy.20 = f32[18,18,8,3,64]{4,3,2,1,0:T(4,128)} copy(f32[18,18,8,3,64]{4,2,3,1,0:T(8,128)} %broadcast_select_fusion) | data formatting | bytes 3981312 | tf_op jit(solution)/shard_map/conv_general_dilated | solution.py:12
  88.0 7.3 %reshape.52 = f32[18,18,1,24,64]{4,3,1,0,2:T(8,128)} reshape(f32[18,18,8,3,64]{4,3,2,1,0:T(4,128)} %copy.20) | data formatting | bytes 3981312 | tf_op jit(solution)/shard_map/conv_general_dilated | solution.py:12
  95.3 4.3 %fusion.14 = bf16[18,18,18,64]{3,2,1,0:T(8,128)(2,1)S(1)} fusion(f32[1,18,18,64]{3,2,1,0:T(8,128)} %collective-permute-done.9, f32[16,1,18,64]{3,2,1,0:T(8,128)} %copy-done.6, f32[16,16,18,64]{3,2,1,0:T(8,128)S(1)} %fusion.23, f32[16,1,18,64]{3,2,1,0:T(8,128)S(1)} %collective-permute-done.6, f32[1,18,18,64]{3,2,1,0:T(8,128)} %collective-permute-done.8, ...), kind=kLoop, calls=%fused_computation.18 | loop fusion | flops 4478976 | bytes 4478976 | tf_op jit(solution)/shard_map/convert_element_type | solution.py:123
  100.9 1.7 %pad.12 = bf16[18,18,1,24,64]{4,3,1,0,2:T(8,128)(2,1)} pad(bf16[18,18,1,18,64]{4,3,1,0,2:T(8,128)(2,1)S(1)} %bitcast.56, bf16[]{:T(256)} %constant.11.clone.1), padding=0_0x0_0x0_0x0_6x0_0 | pad | bytes 1741826 | tf_op jit(solution)/shard_map/broadcast_in_dim | solution.py:13
  102.6 5.1 %reshape.55 = bf16[18,18,1,8,3,64]{5,4,3,1,0,2:T(4,128)(2,1)S(1)} reshape(bf16[18,18,1,24,64]{4,3,1,0,2:T(8,128)(2,1)} %pad.12) | data formatting | bytes 1990656 | tf_op jit(solution)/shard_map/conv_general_dilated | solution.py:12
  108.8 6.3 %fusion.30 = f32[16,16,8,3,64]{4,2,3,1,0:T(8,128)S(1)} fusion(bf16[18,18,1,7,2,64]{5,3,4,1,0,2:T(8,128)(2,1)S(1)} %slice.106, bf16[18,18,1,8,3,64]{5,3,4,1,0,2:T(8,128)(2,1)S(1)} %copy.24, pred[8,3]{0,1:T(4,128)(4,1)S(1)} %copy-done.20, bf16[64,3,3,3,64]{4,3,2,1,0:T(4,128)(2,1)S(1)} %copy-done.7), kind=kOutput, calls=%fused_computation.36 | convolution fusion | flops 1364324352 | bytes 3370008 | tf_op jit(solution)/shard_map/conv_general_dilated | solution.py:12
  119.2 1.5 %reshape.45 = bf16[16,16,1024]{2,1,0:T(8,128)(2,1)} reshape(bf16[16,16,16,64]{3,2,1,0:T(8,128)(2,1)S(1)} %fusion.26) | data formatting | bytes 1048576 | tf_op jit(solution)/shard_map/reshape | solution.py:128
  (92 shorter events, 24.3 us)
Async XLA Ops:
  0.0 4.6 %copy-start = (bf16[64,128]{1,0:T(8,128)(2,1)S(1)}, bf16[64,128]{1,0:T(8,128)(2,1)}, u32[]{:S(2)}) copy-start(bf16[64,128]{1,0:T(8,128)(2,1)} %param.15) | copy-start | bytes 49156
  2.4 13.8 %collective-permute-start = (bf16[8,4,1152]{2,1,0:T(4,128)(2,1)S(1)}, bf16[8,4,1152]{2,1,0:T(4,128)(2,1)S(1)}, u32[]{:S(2)}, u32[]{:S(2)}) collective-permute-start(bf16[8,4,1152]{2,1,0:T(4,128)(2,1)S(1)} %concatenate.30), channel_id=1, source_target_pairs={{0,1},{1,0},{2,3},{3,2},{4,5},{5,4},{6,7},{7,6},{8,9},{9,8},{10,11... | collective-permute-start | bytes 221192 | tf_op jit(solution)/shard_map/ppermute | solution.py:70
  4.7 2.0 %copy-start.16 = (bf16[64,1728]{1,0:T(8,128)(2,1)S(1)}, bf16[64,1728]{1,0:T(8,128)(2,1)}, u32[]{:S(2)}) copy-start(bf16[64,1728]{1,0:T(8,128)(2,1)} %param.12) | copy-start | bytes 663556
  5.4 7.5 %copy-start.3 = (f32[4096,128]{1,0:T(8,128)}, f32[4096,128]{1,0:T(8,128)S(1)}, u32[]{:S(2)}) copy-start(f32[4096,128]{1,0:T(8,128)S(1)} %fusion.5) | copy-start | bytes 6291460
  5.5 7.3 %collective-permute-start.5 = (f32[16,16,64]{2,1,0:T(8,128)S(1)}, f32[16,16,64]{2,1,0:T(8,128)S(1)}, u32[]{:S(2)}, u32[]{:S(2)}) collective-permute-start(f32[16,16,64]{2,1,0:T(8,128)S(1)} %bitcast.63), channel_id=1, source_target_pairs={{0,1},{1,0},{2,3},{3,2},{4,5},{5,4},{6,7},{7,6},{8,9},{9,8},{10,11... | collective-permute-start | bytes 196616 | tf_op jit(solution)/shard_map/ppermute | solution.py:111
  18.5 11.8 %collective-permute-start.1 = (bf16[8,2,1152]{2,1,0:T(2,128)(2,1)S(1)}, bf16[8,2,1152]{2,1,0:T(2,128)(2,1)S(1)}, u32[]{:S(2)}, u32[]{:S(2)}) collective-permute-start(bf16[8,2,1152]{2,1,0:T(2,128)(2,1)S(1)} %get-tuple-element.11), channel_id=1, source_target_pairs={{0,2},{1,3},{4,6},{5,7},{8,10},{9,11},{12,14},{13,15},{16,18},{17,... | collective-permute-start | bytes 110600 | tf_op jit(solution)/shard_map/ppermute | solution.py:34
  23.0 7.2 %collective-permute-start.2 = (bf16[8,2,1152]{2,1,0:T(2,128)(2,1)S(1)}, bf16[8,2,1152]{2,1,0:T(2,128)(2,1)S(1)}, u32[]{:S(2)}, u32[]{:S(2)}) collective-permute-start(bf16[8,2,1152]{2,1,0:T(2,128)(2,1)S(1)} %get-tuple-element.12), channel_id=1, source_target_pairs={{2,0},{3,1},{6,4},{7,5},{10,8},{11,9},{14,12},{15,13},{18,16},{19,... | collective-permute-start | bytes 110600 | tf_op jit(solution)/shard_map/ppermute | solution.py:35
  24.4 10.8 %collective-permute-start.6 = (f32[16,1,18,64]{3,2,1,0:T(8,128)S(1)}, f32[16,1,18,64]{3,2,1,0:T(8,128)S(1)}, u32[]{:S(2)}, u32[]{:S(2)}) collective-permute-start(f32[16,1,18,64]{3,2,1,0:T(8,128)S(1)} %get-tuple-element.7), channel_id=1, source_target_pairs={{0,2},{1,3},{4,6},{5,7},{8,10},{9,11},{12,14},{13,15},{16,18},{17,... | collective-permute-start | bytes 221192 | tf_op jit(solution)/shard_map/ppermute | solution.py:34
  28.9 8.1 %collective-permute-start.7 = (f32[16,1,18,64]{3,2,1,0:T(8,128)S(1)}, f32[16,1,18,64]{3,2,1,0:T(8,128)S(1)}, u32[]{:S(2)}, u32[]{:S(2)}) collective-permute-start(f32[16,1,18,64]{3,2,1,0:T(8,128)S(1)} %get-tuple-element.8), channel_id=1, source_target_pairs={{2,0},{3,1},{6,4},{7,5},{10,8},{11,9},{14,12},{15,13},{18,16},{19,... | collective-permute-start | bytes 221192 | tf_op jit(solution)/shard_map/ppermute | solution.py:35
  30.3 13.4 %copy-start.9 = (bf16[8,2,1152]{2,1,0:T(2,128)(2,1)}, bf16[8,2,1152]{2,1,0:T(2,128)(2,1)S(1)}, u32[]{:S(2)}) copy-start(bf16[8,2,1152]{2,1,0:T(2,128)(2,1)S(1)} %collective-permute-done.2) | copy-start | bytes 110596
  30.3 13.2 %collective-permute-start.3 = (bf16[2,12,1152]{2,1,0:T(8,128)(2,1)S(1)}, bf16[2,12,1152]{2,1,0:T(8,128)(2,1)S(1)}, u32[]{:S(2)}, u32[]{:S(2)}) collective-permute-start(bf16[2,12,1152]{2,1,0:T(8,128)(2,1)S(1)} %get-tuple-element.9), channel_id=1, source_target_pairs={{0,4},{4,8},{8,12},{1,5},{5,9},{9,13},{2,6},{6,10},{10,14},{3,7},{... | collective-permute-start | bytes 165896 | tf_op jit(solution)/shard_map/ppermute | solution.py:34
  33.8 9.8 %collective-permute-start.4 = (bf16[2,12,1152]{2,1,0:T(8,128)(2,1)S(1)}, bf16[2,12,1152]{2,1,0:T(8,128)(2,1)S(1)}, u32[]{:S(2)}, u32[]{:S(2)}) collective-permute-start(bf16[2,12,1152]{2,1,0:T(8,128)(2,1)S(1)} %get-tuple-element.10), channel_id=1, source_target_pairs={{4,0},{8,4},{12,8},{5,1},{9,5},{13,9},{6,2},{10,6},{14,10},{7,3},{... | collective-permute-start | bytes 165896 | tf_op jit(solution)/shard_map/ppermute | solution.py:35
  37.1 6.5 %copy-start.6 = (f32[16,1,18,64]{3,2,1,0:T(8,128)}, f32[16,1,18,64]{3,2,1,0:T(8,128)S(1)}, u32[]{:S(2)}) copy-start(f32[16,1,18,64]{3,2,1,0:T(8,128)S(1)} %collective-permute-done.7) | copy-start | bytes 221188
  37.9 57.4 %collective-permute-start.8 = (f32[1,18,18,64]{3,2,1,0:T(8,128)}, f32[1,18,18,64]{3,2,1,0:T(8,128)}, u32[]{:S(2)}, u32[]{:S(2)}) collective-permute-start(f32[1,18,18,64]{3,2,1,0:T(8,128)} %get-tuple-element.5), channel_id=1, source_target_pairs={{0,4},{4,8},{8,12},{1,5},{5,9},{9,13},{2,6},{6,10},{10,14},{3,7},{... | collective-permute-start | bytes 248840 | tf_op jit(solution)/shard_map/ppermute | solution.py:34
  42.1 53.2 %collective-permute-start.9 = (f32[1,18,18,64]{3,2,1,0:T(8,128)}, f32[1,18,18,64]{3,2,1,0:T(8,128)}, u32[]{:S(2)}, u32[]{:S(2)}) collective-permute-start(f32[1,18,18,64]{3,2,1,0:T(8,128)} %get-tuple-element.6), channel_id=1, source_target_pairs={{4,0},{8,4},{12,8},{5,1},{9,5},{13,9},{6,2},{10,6},{14,10},{7,3},{... | collective-permute-start | bytes 248840 | tf_op jit(solution)/shard_map/ppermute | solution.py:35
  48.7 5.5 %copy-start.10 = (bf16[8,2,1152]{2,1,0:T(2,128)(2,1)S(1)}, bf16[8,2,1152]{2,1,0:T(2,128)(2,1)}, u32[]{:S(2)}) copy-start(bf16[8,2,1152]{2,1,0:T(2,128)(2,1)} %copy-done.9) | copy-start | bytes 110596
  48.7 5.5 %copy-start.11 = (s32[12,12,10]{2,1,0:T(8,128)S(1)}, s32[12,12,10]{2,1,0:T(8,128)}, u32[]{:S(2)}) copy-start(s32[12,12,10]{2,1,0:T(8,128)} %iota_add_fusion) | copy-start | bytes 17284
  48.7 5.5 %copy-start.13 = (bf16[2,12,1152]{2,1,0:T(8,128)(2,1)S(1)}, bf16[2,12,1152]{2,1,0:T(8,128)(2,1)}, u32[]{:S(2)}) copy-start(bf16[2,12,1152]{2,1,0:T(8,128)(2,1)} %copy-done.12) | copy-start | bytes 165892
  48.7 5.5 %copy-start.15 = (bf16[2,12,1152]{2,1,0:T(8,128)(2,1)S(1)}, bf16[2,12,1152]{2,1,0:T(8,128)(2,1)}, u32[]{:S(2)}) copy-start(bf16[2,12,1152]{2,1,0:T(8,128)(2,1)} %copy-done.14) | copy-start | bytes 165892
  48.7 5.5 %copy-start.18 = (pred[12,12,20]{2,1,0:T(8,128)(4,1)S(1)}, pred[12,12,20]{2,1,0:T(8,128)(4,1)}, u32[]{:S(2)}) copy-start(pred[12,12,20]{2,1,0:T(8,128)(4,1)} %get-tuple-element.13) | copy-start | bytes 8644
  48.8 5.5 %copy-start.19 = (pred[12,12,20]{2,1,0:T(8,128)(4,1)S(1)}, pred[12,12,20]{2,1,0:T(8,128)(4,1)}, u32[]{:S(2)}) copy-start(pred[12,12,20]{2,1,0:T(8,128)(4,1)} %get-tuple-element.14) | copy-start | bytes 8644
  48.8 5.9 %copy-start.5 = (bf16[12,12,16,64]{3,2,1,0:T(8,128)(2,1)S(1)}, bf16[12,12,16,64]{3,2,1,0:T(8,128)(2,1)}, u32[]{:S(2)}) copy-start(bf16[12,12,16,64]{3,2,1,0:T(8,128)(2,1)} %reshape.39) | copy-start | bytes 884740
  115.6 1.6 %copy-start.2 = (bf16[18,18,18,64]{3,2,1,0:T(8,128)(2,1)S(1)}, bf16[18,18,18,64]{3,2,1,0:T(8,128)(2,1)}, u32[]{:S(2)}) copy-start(bf16[18,18,18,64]{3,2,1,0:T(8,128)(2,1)} %copy-done.1) | copy-start | bytes 2239492
  115.6 2.2 %copy-start.4 = (f32[4096,128]{1,0:T(8,128)S(1)}, f32[4096,128]{1,0:T(8,128)}, u32[]{:S(2)}) copy-start(f32[4096,128]{1,0:T(8,128)} %copy-done.3) | copy-start | bytes 6291460
  (8 other events, 7.5 us)
where the time goes:
time: 122 us; the launch traced here: 121 us
  local copies, waits for them, and re-layouts  59.1 us (48%)
  starting transfers between devices  22.8 us (19%)
  matrix products  21.5 us (18%)
  other arithmetic  12.9 us (11%)
  between operations  2.55 us (2%)
  waiting for transfers between devices  1.94 us (2%)
    conv_general_dilated x3, matrix products, convolve(): lax.conv_general_dilated(padded[None], kernel, (1, 1, 1), 'VALID', dimens...  20.8 us
    conv_general_dilated x9, local copies, waits for them, and re-layouts, convolve(): lax.conv_general_dilated(padded[None], kernel, (1, 1, 1), 'VALID', dimens...  20.6 us
    ppermute x4, starting transfers between devices, grow(): low = lax.ppermute(tail, axis, shift_pairs(count, True))  16.8 us
    another operation x3, local copies, waits for them, and re-layouts, convolve(): padded[None]  8.52 us
    reshape x1, local copies, waits for them, and re-layouts, doubled(): return spread.reshape(2 * size_x, 2 * size_y, 2 * size_z, channels)  5.71 us
    reshape x3, local copies, waits for them, and re-layouts, convolve(): weight.reshape(channels, 3, 3, 3, channels).transpose(1, 2, 3, 0, 4)  5.55 us
    ppermute x4, starting transfers between devices, grow(): high = lax.ppermute(head, axis, shift_pairs(count, False))  5.34 us
    unnamed x44, local copies, waits for them, and re-layouts  5.12 us
  transfers between devices with their start and end apart: 10, of which 1 were waited for; matrix products, arithmetic and copies ran while one was open for 53% of the time, Pallas kernels for 0%

commit v1 on v0

--- a/solution.py
+++ b/solution.py
@@ -1,9 +1,81 @@
 import jax
 import jax.numpy as jnp
 from jax import lax
+from jax.experimental import pallas as pl
+from jax.experimental.pallas import tpu as pltpu
 from jax.sharding import PartitionSpec as P
 
 conv_layout = ("NDHWC", "DHWIO", "NDHWC")
+
+STRIDE = 24
+ROWS_C = 112
+ROWS_F = 488
+ROWS_A = 432
+ROWS_B = 384
+ROWS_L = 440
+LANES_F = 1408
+LANES_A = 1280
+LANES_B = 1024
+
+
+def bands(weight):
+    channels = weight.shape[0]
+    cells = weight.astype(jnp.float32).reshape(channels, 3, 3, 3, channels)
+    pick = (
+        jnp.arange(6)[:, None, None] - jnp.arange(4)[None, :, None] == jnp.arange(3)[None, None, :]
+    ).astype(jnp.float32)
+    band = jnp.einsum("abd,ixydo->xyaibo", pick, cells, precision=lax.Precision.HIGHEST)
+    return band.reshape(9, 6 * channels, 4 * channels).astype(jnp.bfloat16)
+
+
+def silu(v):
+    return v / (1.0 + jnp.exp(-v))
+
+
+def fine_kernel(hid_ref, spread_ref, ga_ref, gb_ref, wa_ref, wb_ref, out_ref, fin_ref, lvl_ref):
+    wide_c = hid_ref.shape[1]
+    i = lax.broadcasted_iota(jnp.int32, (wide_c, LANES_F), 0)
+    j = lax.broadcasted_iota(jnp.int32, (wide_c, LANES_F), 1)
+    zup = (((i >> 6) == (j >> 7)) & ((i & 63) == (j & 63)) & (j < LANES_A)).astype(jnp.bfloat16)
+    deep = jnp.dot(hid_ref[...], zup, preferred_element_type=jnp.float32).astype(jnp.bfloat16)
+    fin_ref[...] = jnp.dot(spread_ref[...], deep, preferred_element_type=jnp.float32)
+    r = lax.broadcasted_iota(jnp.int32, (384, 256), 0)
+    c = lax.broadcasted_iota(jnp.int32, (384, 256), 1)
+    shift = (r == c + 64).astype(jnp.bfloat16)
+    lvl_ref[ROWS_A:, :] = jnp.zeros((ROWS_L - ROWS_A, LANES_A), jnp.float32)
+
+    def conv(src, weights, rows, chunk):
+        acc = jnp.zeros((rows, 256), jnp.float32)
+        centre = None
+        for t in range(9):
+            dx, dy = divmod(t, 3)
+            off = dx * STRIDE + dy
+            a = src[off : off + rows, 256 * chunk : 256 * chunk + 384].astype(jnp.bfloat16)
+            acc = acc + jnp.dot(a, weights[t], preferred_element_type=jnp.float32)
+            if t == 4:
+                centre = jnp.dot(a, shift, preferred_element_type=jnp.float32)
+        return centre, acc
+
+    for k in range(LANES_A // 256):
+        centre, acc = conv(fin_ref, wa_ref, ROWS_A, k)
+        lanes = slice(256 * k, 256 * k + 256)
+        step = centre + silu(acc) * ga_ref[:, lanes]
+        lvl_ref[:ROWS_A, lanes] = step.astype(jnp.bfloat16).astype(jnp.float32)
+    for k in range(LANES_B // 256):
+        centre, acc = conv(lvl_ref, wb_ref, ROWS_B, k)
+        lanes = slice(256 * k, 256 * k + 256)
+        out_ref[:, lanes] = (centre + silu(acc) * gb_ref[:, lanes]).astype(out_ref.dtype)
+
+
+def fine_stage(hid, spread, gate_a, gate_b, band_a, band_b):
+    return pl.pallas_call(
+        fine_kernel,
+        out_shape=jax.ShapeDtypeStruct((ROWS_B, LANES_B), jnp.bfloat16),
+        scratch_shapes=[
+            pltpu.VMEM((ROWS_F, LANES_F), jnp.float32),
+            pltpu.VMEM((ROWS_L, LANES_A), jnp.float32),
+        ],
+    )(hid, spread, gate_a, gate_b, band_a, band_b)
 
 
 def convolve(padded, weight):
@@ -34,14 +106,6 @@
     low = lax.ppermute(tail, axis, shift_pairs(count, True))
     high = lax.ppermute(head, axis, shift_pairs(count, False))
     return jnp.concatenate([low, cells, high], axis=dim)
-
-
-def doubled(volume):
-    size_x, size_y, size_z, channels = volume.shape
-    spread = jnp.broadcast_to(
-        volume[:, None, :, None, :, None, :], (size_x, 2, size_y, 2, size_z, 2, channels)
-    )
-    return spread.reshape(2 * size_x, 2 * size_y, 2 * size_z, channels)
 
 
 def body(
@@ -97,35 +161,50 @@
     hidden = ((centre + jax.nn.silu(activity)) * keep[..., None].astype(jnp.float32)).astype(
         jnp.bfloat16
     )
-    fine_input = doubled(hidden)
-
-    product = jnp.dot(
-        field.reshape(-1, channels), mod_weight, preferred_element_type=jnp.float32
-    )
-    gates = jax.nn.sigmoid(product).reshape(edge, edge, edge, 2 * channels) * live.astype(
-        jnp.float32
-    )
-    gate_a = gates[..., :channels]
-    gate_b = gates[..., channels:]
-    face = jnp.where(first, gate_a[:, :, -1], gate_a[:, :, 0])
-    face = lax.ppermute(face, "gz", [(0, 1), (1, 0)])[:, :, None]
+    cells = hidden.shape[0] * hidden.shape[1]
+    hid = jnp.pad(hidden.reshape(cells, -1), ((0, ROWS_C - cells), (0, 0)))
+
+    eye = jnp.eye(edge, dtype=jnp.float32)
+    flat_w = mod_weight.astype(jnp.float32)
+
+    def gate(part):
+        block = (eye[:, None, :, None] * part[None, :, None, :]).reshape(
+            edge * channels, edge * channels
+        )
+        return jax.nn.sigmoid(
+            jnp.einsum(
+                "xyl,lm->xym", field, block.astype(jnp.bfloat16), preferred_element_type=jnp.float32
+            )
+        ) * live.astype(jnp.float32)
+
+    gate_a = gate(flat_w[:, :channels])
+    gate_b = gate(flat_w[:, channels:])
+    width = edge * channels
+    face = jnp.where(first, gate_a[:, :, width - channels :], gate_a[:, :, :channels])
+    face = lax.ppermute(face, "gz", [(0, 1), (1, 0)])
     blank = jnp.zeros_like(face)
-    gate_a = jnp.where(
-        first,
-        jnp.concatenate([blank, gate_a, face], 2),
-        jnp.concatenate([face, gate_a, blank], 2),
+    gate_a = jnp.concatenate(
+        [
+            jnp.where(first, blank, face),
+            gate_a,
+            jnp.where(first, face, blank),
+            jnp.zeros((edge, edge, 2 * channels), jnp.float32),
+        ],
+        axis=2,
     )
     gate_a = grow(grow(gate_a, "gy", 1, 1), "gx", 0, 1)
-
-    first_act = convolve(fine_input, fine_weight_a)
-    level_one = (
-        fine_input[1:-1, 1:-1, 1:-1].astype(jnp.float32) + jax.nn.silu(first_act) * gate_a
-    ).astype(jnp.bfloat16)
-    second_act = convolve(level_one, fine_weight_b)
-    result = (
-        level_one[1:-1, 1:-1, 1:-1].astype(jnp.float32) + jax.nn.silu(second_act) * gate_b
-    ).astype(jnp.bfloat16)
-    return result.reshape(edge, edge, edge * channels)
+    gate_a = jnp.pad(gate_a, ((0, 0), (0, STRIDE - edge - 2), (0, 0))).reshape(-1, gate_a.shape[2])
+    gate_b = jnp.pad(gate_b, ((0, 0), (0, STRIDE - edge), (0, 0))).reshape(-1, width)
+
+    rows = jnp.arange(ROWS_F)
+    fx, fy = rows // STRIDE, rows % STRIDE
+    inside = (fx < edge + 4) & (fy < edge + 4)
+    source = (fx // 2) * (half + 2) + fy // 2
+    spread = (inside[:, None] & (source[:, None] == jnp.arange(ROWS_C)[None, :])).astype(
+        jnp.bfloat16
+    )
+    out = fine_stage(hid, spread, gate_a, gate_b, bands(fine_weight_a), bands(fine_weight_b))
+    return out.reshape(edge, STRIDE, width)[:, :edge]
 
 
 def solution(mesh):

time: 122 us -> 115 us (0.943)
  Pallas kernels: 0 us -> 15.6 us
  local copies, waits for them, and re-layouts: 59.1 us -> 44.9 us
  matrix products: 21.5 us -> 10.6 us
  other arithmetic: 12.9 us -> 16 us
  waiting for transfers between devices: 1.94 us -> 0.13 us
    convert_element_type x0 -> x6, local copies, waits for them, and re-layouts: none -> 32.5 us  [the longest x4 21.6 us: bands(): return band.reshape(9, 6 * channels, 4 * channels).astype(jnp.bfloat16)]
    conv_general_dilated x9 -> x0, local copies, waits for them, and re-layouts: 20.6 us -> none  [convolve(): lax.conv_general_dilated(padded[None], kernel, (1, 1, 1), 'VALID', dimens...]
    conv_general_dilated x3 -> x1, matrix products: 20.8 us -> 4.25 us  [convolve(): lax.conv_general_dilated(padded[None], kernel, (1, 1, 1), 'VALID', dimens...]
    pallas_call x0 -> x1, Pallas kernels: none -> 15.6 us  [fine_stage(): pl.pallas_call(fine_kernel, out_shape=jax.ShapeDtypeStruct((ROWS_B, LANES...]
    another operation x3 -> x0, local copies, waits for them, and re-layouts: 8.52 us -> none  [convolve(): padded[None]]
    reshape x3, local copies, waits for them, and re-layouts: 8.98 us -> 0.91 us  [the longest x2 0.67 us: bands(): cells = weight.astype(jnp.float32).reshape(channels, 3, 3, 3, channels)]
    dot_general x1 -> x4, matrix products: 0.7 us -> 6.37 us  [the longest x2 3.57 us: bands(): jnp.einsum('abd,ixydo->xyaibo', pick, cells, precision=lax.Precision.HIGH...]
    reshape x3 -> x1, local copies, waits for them, and re-layouts: 5.55 us -> 0.34 us  [convolve(): weight.reshape(channels, 3, 3, 3, channels).transpose(1, 2, 3, 0, 4)]
  transfers between devices with their start and end apart: 10 -> 10, of which waited for: 1 -> 1; matrix products, arithmetic and copies ran while one was open for 53% -> 44% of each run, Pallas kernels for 0% -> 0%
where the time goes in v1:
time: 115 us; the launch traced here: 113 us
  local copies, waits for them, and re-layouts  44.9 us (39%)
  starting transfers between devices  23.7 us (21%)
  other arithmetic  16 us (14%)
  Pallas kernels  15.6 us (14%)
  matrix products  10.6 us (9%)
  between operations  2.56 us (2%)
    convert_element_type x4, local copies, waits for them, and re-layouts, bands(): return band.reshape(9, 6 * channels, 4 * channels).astype(jnp.bfloat16)  21.6 us
    ppermute x4, starting transfers between devices, grow(): low = lax.ppermute(tail, axis, shift_pairs(count, True))  18 us
    pallas_call x1, Pallas kernels, fine_stage(): pl.pallas_call(fine_kernel, out_shape=jax.ShapeDtypeStruct((ROWS_B, LANES...  15.6 us
    convert_element_type x2, local copies, waits for them, and re-layouts, gate(): block.astype(jnp.bfloat16)  11 us
    convert_element_type x1, other arithmetic, gate(): block.astype(jnp.bfloat16)  5.3 us
    ppermute x4, starting transfers between devices, grow(): high = lax.ppermute(head, axis, shift_pairs(count, False))  5.16 us
    conv_general_dilated x1, matrix products, convolve(): lax.conv_general_dilated(padded[None], kernel, (1, 1, 1), 'VALID', dimens...  4.25 us
    dot_general x2, matrix products, bands(): jnp.einsum('abd,ixydo->xyaibo', pick, cells, precision=lax.Precision.HIGH...  3.57 us
  transfers between devices with their start and end apart: 10, of which 1 were waited for; matrix products, arithmetic and copies ran while one was open for 44% of the time, Pallas kernels for 0%

profile of v1, /device:TPU:0, one launch (start us, length us, event | category | flops | bytes accessed | tf_op | source)
XLA Modules:
  0.0 113.5 jit_solution(15065767663033513003)
XLA Ops:
  0.9 5.3 %multiply_convert_fusion = (bf16[16,64,16,64]{3,2,1,0:T(8,128)(2,1)}, bf16[16,64,16,64]{3,2,1,0:T(8,128)(2,1)}) fusion(f32[64,64]{1,0:T(8,128)S(1)} %get-tuple-element.15, f32[16,16]{1,0:T(8,128)S(1)} %fusion.37, f32[64,64]{1,0:T(8,128)S(1)} %get-tuple-element.16), kind=kLoop, calls=%fused_computation | loop fusion | flops 4194304 | bytes 4228096 | tf_op jit(solution)/shard_map/convert_element_type | solution.py:176
  6.2 5.5 %reshape.137 = bf16[1024,1024,1]{1,0,2:T(8,128)(2,1)S(1)} reshape(bf16[16,64,16,64]{3,2,1,0:T(8,128)(2,1)} %get-tuple-element.18) | data formatting | bytes 4194304 | tf_op jit(solution)/shard_map/convert_element_type | solution.py:176
  17.3 5.5 %reshape.138 = bf16[1024,1024,1]{1,0,2:T(8,128)(2,1)S(1)} reshape(bf16[16,64,16,64]{3,2,1,0:T(8,128)(2,1)} %get-tuple-element.17) | data formatting | bytes 4194304 | tf_op jit(solution)/shard_map/convert_element_type | solution.py:176
  22.8 1.9 %fusion.14 = f32[16,16,1024]{2,1,0:T(8,128)} fusion(bf16[1024,1024,1]{1,0,2:T(8,128)(2,1)S(1)} %reshape.138, bf16[16,16,1024]{2,1,0:T(8,128)(2,1)S(1)} %copy-done, f32[]{:T(128)} %bitcast.3), kind=kOutput, calls=%fused_computation.23 | convolution fusion | flops 537919488 | bytes 3670020 | tf_op jit(solution)/shard_map/xyl,lm->xym/dot_general | solution.py:175
  25.1 1.7 %convert_bitcast_fusion = bf16[3,3,6,64,4,64]{5,2,1,0,3,4:T(8,128)(2,1)S(1)} fusion(bf16[64,3,3,3,64,1]{4,3,2,1,0,5:T(4,128)(2,1)S(1)} %reshape.141, s32[6,4]{0,1:T(4,128)S(1)} %iota_subtract_fusion), kind=kOutput, calls=%fused_computation.2 | convolution fusion | flops 6193224 | bytes 1990752 | tf_op jit(solution)/shard_map/abd,ixydo->xyaibo/dot_general | solution.py:27
  26.8 4.5 %copy.15 = bf16[3,3,6,64,4,64]{5,4,3,2,1,0:T(4,128)(2,1)} copy(bf16[3,3,6,64,4,64]{5,2,1,0,3,4:T(8,128)(2,1)S(1)} %convert_bitcast_fusion) | data formatting | bytes 3538944 | tf_op jit(solution)/shard_map/convert_element_type | solution.py:28
  31.2 6.3 %convert_element_type.102.wb_ref = bf16[9,384,256]{2,1,0:T(8,128)(2,1)} reshape(bf16[3,3,6,64,4,64]{5,4,3,2,1,0:T(4,128)(2,1)} %copy.15) | data formatting | bytes 3538944 | tf_op jit(solution)/shard_map/convert_element_type | solution.py:28
  37.9 1.9 %convert_bitcast_fusion.1 = bf16[3,3,6,64,4,64]{5,2,1,0,3,4:T(8,128)(2,1)S(1)} fusion(bf16[64,3,3,3,64,1]{4,3,2,1,0,5:T(4,128)(2,1)S(1)} %reshape.140, s32[6,4]{0,1:T(4,128)S(1)} %iota_subtract_fusion), kind=kOutput, calls=%fused_computation.3 | convolution fusion | flops 6193224 | bytes 1990752 | tf_op jit(solution)/shard_map/abd,ixydo->xyaibo/dot_general | solution.py:27
  39.8 4.5 %copy.14 = bf16[3,3,6,64,4,64]{5,4,3,2,1,0:T(4,128)(2,1)} copy(bf16[3,3,6,64,4,64]{5,2,1,0,3,4:T(8,128)(2,1)S(1)} %convert_bitcast_fusion.1) | data formatting | bytes 3538944 | tf_op jit(solution)/shard_map/convert_element_type | solution.py:28
  44.3 6.3 %convert_element_type.99.wa_ref = bf16[9,384,256]{2,1,0:T(8,128)(2,1)} reshape(bf16[3,3,6,64,4,64]{5,4,3,2,1,0:T(4,128)(2,1)} %copy.14) | data formatting | bytes 3538944 | tf_op jit(solution)/shard_map/convert_element_type | solution.py:28
  50.6 1.4 %pad.24 = f32[16,24,1024]{2,1,0:T(8,128)} pad(f32[16,16,1024]{2,1,0:T(8,128)S(1)} %copy-done.3, f32[]{:T(128)} %constant.63.clone.1), padding=0_0x0_8x0_0 | pad | bytes 2621444 | tf_op jit(solution)/shard_map/jit(_pad)/pad | solution.py:197
  53.5 1.6 %broadcast_select_fusion = (f32[16,16,64]{2,1,0:T(8,128)}, f32[16,16,64]{2,1,0:T(8,128)}) fusion(f32[16,16,64]{2,1,0:T(8,128)} %collective-permute-done.5, pred[]{:T(512)S(6)} %eq.53), kind=kLoop, calls=%fused_computation.58 | loop fusion | flops 32768 | bytes 196609 | tf_op jit(solution)/shard_map/jit(_where)/select_n | solution.py:190
  55.7 1.6 %concatenate.33 = f32[16,16,1280]{2,1,0:T(8,128)S(1)} concatenate(f32[16,16,64]{2,1,0:T(8,128)} %get-tuple-element.14, f32[16,16,1024]{2,1,0:T(8,128)S(1)} %copy-done.2, f32[16,16,64]{2,1,0:T(8,128)} %get-tuple-element.13, f32[16,16,128]{2,1,0:T(8,128)} %broadcast_in_dim.47), dimensions={2} | concatenate | bytes 2621440 | tf_op jit(solution)/shard_map/concatenate | solution.py:186
  61.3 4.9 %collective-permute-start.1 = (bf16[8,2,1152]{2,1,0:T(2,128)(2,1)S(1)}, bf16[8,2,1152]{2,1,0:T(2,128)(2,1)S(1)}, u32[]{:S(2)}, u32[]{:S(2)}) collective-permute-start(bf16[8,2,1152]{2,1,0:T(2,128)(2,1)S(1)} %get-tuple-element.11), channel_id=1, source_target_pairs={{0,2},{1,3},{4,6},{5,7},{8,10},{9,11},{12,14},{13,15},{16,18},{17,... | collective-permute-start | bytes 110600 | tf_op jit(solution)/shard_map/ppermute | solution.py:106
  66.1 1.3 %collective-permute-start.2 = (bf16[8,2,1152]{2,1,0:T(2,128)(2,1)S(1)}, bf16[8,2,1152]{2,1,0:T(2,128)(2,1)S(1)}, u32[]{:S(2)}, u32[]{:S(2)}) collective-permute-start(bf16[8,2,1152]{2,1,0:T(2,128)(2,1)S(1)} %get-tuple-element.12), channel_id=1, source_target_pairs={{2,0},{3,1},{6,4},{7,5},{10,8},{11,9},{14,12},{15,13},{18,16},{19,... | collective-permute-start | bytes 110600 | tf_op jit(solution)/shard_map/ppermute | solution.py:107
  67.5 4.5 %collective-permute-start.6 = (f32[16,1,1280]{2,1,0:T(1,128)S(1)}, f32[16,1,1280]{2,1,0:T(1,128)S(1)}, u32[]{:S(2)}, u32[]{:S(2)}) collective-permute-start(f32[16,1,1280]{2,1,0:T(1,128)S(1)} %get-tuple-element.7), channel_id=1, source_target_pairs={{0,2},{1,3},{4,6},{5,7},{8,10},{9,11},{12,14},{13,15},{16,18},{17,... | collective-permute-start | bytes 245768 | tf_op jit(solution)/shard_map/ppermute | solution.py:106
  72.1 1.3 %collective-permute-start.7 = (f32[16,1,1280]{2,1,0:T(1,128)S(1)}, f32[16,1,1280]{2,1,0:T(1,128)S(1)}, u32[]{:S(2)}, u32[]{:S(2)}) collective-permute-start(f32[16,1,1280]{2,1,0:T(1,128)S(1)} %get-tuple-element.8), channel_id=1, source_target_pairs={{2,0},{3,1},{6,4},{7,5},{10,8},{11,9},{14,12},{15,13},{18,16},{19,... | collective-permute-start | bytes 245768 | tf_op jit(solution)/shard_map/ppermute | solution.py:107
  73.5 3.5 %collective-permute-start.3 = (bf16[2,12,1152]{2,1,0:T(8,128)(2,1)S(1)}, bf16[2,12,1152]{2,1,0:T(8,128)(2,1)S(1)}, u32[]{:S(2)}, u32[]{:S(2)}) collective-permute-start(bf16[2,12,1152]{2,1,0:T(8,128)(2,1)S(1)} %get-tuple-element.9), channel_id=1, source_target_pairs={{0,4},{4,8},{8,12},{1,5},{5,9},{9,13},{2,6},{6,10},{10,14},{3,7},{... | collective-permute-start | bytes 165896 | tf_op jit(solution)/shard_map/ppermute | solution.py:106
  77.0 1.3 %collective-permute-start.4 = (bf16[2,12,1152]{2,1,0:T(8,128)(2,1)S(1)}, bf16[2,12,1152]{2,1,0:T(8,128)(2,1)S(1)}, u32[]{:S(2)}, u32[]{:S(2)}) collective-permute-start(bf16[2,12,1152]{2,1,0:T(8,128)(2,1)S(1)} %get-tuple-element.10), channel_id=1, source_target_pairs={{4,0},{8,4},{12,8},{5,1},{9,5},{13,9},{6,2},{10,6},{14,10},{7,3},{... | collective-permute-start | bytes 165896 | tf_op jit(solution)/shard_map/ppermute | solution.py:107
  79.2 5.1 %collective-permute-start.8 = (f32[1,18,1280]{2,1,0:T(8,128)}, f32[1,18,1280]{2,1,0:T(8,128)}, u32[]{:S(2)}, u32[]{:S(2)}) collective-permute-start(f32[1,18,1280]{2,1,0:T(8,128)} %get-tuple-element.5), channel_id=1, source_target_pairs={{0,4},{4,8},{8,12},{1,5},{5,9},{9,13},{2,6},{6,10},{10,14},{3,7},{... | collective-permute-start | bytes 276488 | tf_op jit(solution)/shard_map/ppermute | solution.py:106
  87.3 4.3 %fusion.15 = f32[1,10,10,10,64]{4,0,3,2,1:T(1,128)S(1)} fusion(bf16[1,12,12,12,64]{4,3,2,1,0:T(8,128)(2,1)S(1)} %fusion.21, bf16[64,3,3,3,64]{4,3,2,1,0:T(4,128)(2,1)S(1)} %reshape.130), kind=kOutput, calls=%fused_computation.26 | convolution fusion | flops 221184000 | bytes 698368 | tf_op jit(solution)/shard_map/conv_general_dilated | solution.py:84
  93.4 2.7 %select_maximum_fusion = f32[18,24,1280]{2,1,0:T(8,128)} fusion(f32[1,18,1280]{2,1,0:T(8,128)} %collective-permute-done.9, f32[1,18,1280]{2,1,0:T(8,128)} %collective-permute-done.8, f32[16,1,1280]{2,1,0:T(1,128)S(1)} %copy-done.12, f32[16,16,1280]{2,1,0:T(8,128)S(1)} %concatenate.33, f32[16,1,1280]{2,1,0:T(1,128)S(1)} %copy-done.10), kind=kLoop, calls=%fused_computation.4 | loop fusion | flops 5529600 | bytes 3870720 | tf_op jit(solution)/shard_map/concatenate | solution.py:108
  96.1 15.6 %shard_map.82 = bf16[384,1024]{1,0:T(8,128)(2,1)} custom-call(bf16[112,640]{1,0:T(8,128)(2,1)} %pad.22.hid_ref, bf16[488,112]{1,0:T(8,128)(2,1)} %fusion.24.spread_ref, f32[432,1280]{1,0:T(8,128)} %bitcast.47, f32[384,1024]{1,0:T(8,128)} %bitcast.48, bf16[9,384,256]{2,1,0:T(8,128)(2,1)} %convert_element_type.99.wa_ref, ...), custom_call_target="tpu_custom_call" | custom-call | tf_op jit(solution)/shard_map/pallas_call | solution.py:71
  111.6 1.9 %slice.93 = bf16[16,16,1024]{2,1,0:T(8,128)(2,1)} slice(bf16[16,24,1024]{2,1,0:T(8,128)(2,1)} %bitcast.49), slice={[0:16], [0:16], [0:1024]} | slice | bytes 1048576 | tf_op jit(solution)/shard_map/slice | solution.py:207
  (100 shorter events, 16.7 us)
Async XLA Ops:
  0.0 12.3 %copy-start = (bf16[16,16,1024]{2,1,0:T(8,128)(2,1)S(1)}, bf16[16,16,1024]{2,1,0:T(8,128)(2,1)}, u32[]{:S(2)}) copy-start(bf16[16,16,1024]{2,1,0:T(8,128)(2,1)} %param.11) | copy-start | bytes 1572868
  12.4 4.6 %copy-start.17 = (bf16[64,1728]{1,0:T(8,128)(2,1)S(1)}, bf16[64,1728]{1,0:T(8,128)(2,1)}, u32[]{:S(2)}) copy-start(bf16[64,1728]{1,0:T(8,128)(2,1)} %param.12) | copy-start | bytes 663556
  15.0 38.5 %collective-permute-start.5 = (f32[16,16,64]{2,1,0:T(8,128)}, f32[16,16,64]{2,1,0:T(8,128)}, u32[]{:S(2)}, u32[]{:S(2)}) collective-permute-start(f32[16,16,64]{2,1,0:T(8,128)} %slice_select_fusion), channel_id=1, source_target_pairs={{0,1},{1,0},{2,3},{3,2},{4,5},{5,4},{6,7},{7,6},{8,9},{9,8},{10,11... | collective-permute-start | bytes 196616 | tf_op jit(solution)/shard_map/ppermute | solution.py:184
  15.6 41.8 %collective-permute-start = (bf16[8,4,1152]{2,1,0:T(4,128)(2,1)S(1)}, bf16[8,4,1152]{2,1,0:T(4,128)(2,1)}, u32[]{:S(2)}, u32[]{:S(2)}) collective-permute-start(bf16[8,4,1152]{2,1,0:T(4,128)(2,1)S(1)} %concatenate.27), channel_id=1, source_target_pairs={{0,1},{1,0},{2,3},{3,2},{4,5},{5,4},{6,7},{7,6},{8,9},{9,8},{10,11... | collective-permute-start | bytes 221192 | tf_op jit(solution)/shard_map/ppermute | solution.py:134
  31.2 6.3 %copy-start.19 = (bf16[64,1728]{1,0:T(8,128)(2,1)S(1)}, bf16[64,1728]{1,0:T(8,128)(2,1)}, u32[]{:S(2)}) copy-start(bf16[64,1728]{1,0:T(8,128)(2,1)} %param.13) | copy-start | bytes 663556
  44.2 6.3 %copy-start.3 = (f32[16,16,1024]{2,1,0:T(8,128)S(1)}, f32[16,16,1024]{2,1,0:T(8,128)}, u32[]{:S(2)}) copy-start(f32[16,16,1024]{2,1,0:T(8,128)} %fusion.14) | copy-start | bytes 3145732
  50.6 5.2 %copy-start.2 = (f32[16,16,1024]{2,1,0:T(8,128)S(1)}, f32[16,16,1024]{2,1,0:T(8,128)}, u32[]{:S(2)}) copy-start(f32[16,16,1024]{2,1,0:T(8,128)} %copy-done.1) | copy-start | bytes 3145732
  61.3 12.1 %collective-permute-start.1 = (bf16[8,2,1152]{2,1,0:T(2,128)(2,1)S(1)}, bf16[8,2,1152]{2,1,0:T(2,128)(2,1)S(1)}, u32[]{:S(2)}, u32[]{:S(2)}) collective-permute-start(bf16[8,2,1152]{2,1,0:T(2,128)(2,1)S(1)} %get-tuple-element.11), channel_id=1, source_target_pairs={{0,2},{1,3},{4,6},{5,7},{8,10},{9,11},{12,14},{13,15},{16,18},{17,... | collective-permute-start | bytes 110600 | tf_op jit(solution)/shard_map/ppermute | solution.py:106
  66.1 7.3 %collective-permute-start.2 = (bf16[8,2,1152]{2,1,0:T(2,128)(2,1)S(1)}, bf16[8,2,1152]{2,1,0:T(2,128)(2,1)S(1)}, u32[]{:S(2)}, u32[]{:S(2)}) collective-permute-start(bf16[8,2,1152]{2,1,0:T(2,128)(2,1)S(1)} %get-tuple-element.12), channel_id=1, source_target_pairs={{2,0},{3,1},{6,4},{7,5},{10,8},{11,9},{14,12},{15,13},{18,16},{19,... | collective-permute-start | bytes 110600 | tf_op jit(solution)/shard_map/ppermute | solution.py:107
  67.5 10.8 %collective-permute-start.6 = (f32[16,1,1280]{2,1,0:T(1,128)S(1)}, f32[16,1,1280]{2,1,0:T(1,128)S(1)}, u32[]{:S(2)}, u32[]{:S(2)}) collective-permute-start(f32[16,1,1280]{2,1,0:T(1,128)S(1)} %get-tuple-element.7), channel_id=1, source_target_pairs={{0,2},{1,3},{4,6},{5,7},{8,10},{9,11},{12,14},{13,15},{16,18},{17,... | collective-permute-start | bytes 245768 | tf_op jit(solution)/shard_map/ppermute | solution.py:106
  72.1 6.3 %collective-permute-start.7 = (f32[16,1,1280]{2,1,0:T(1,128)S(1)}, f32[16,1,1280]{2,1,0:T(1,128)S(1)}, u32[]{:S(2)}, u32[]{:S(2)}) collective-permute-start(f32[16,1,1280]{2,1,0:T(1,128)S(1)} %get-tuple-element.8), channel_id=1, source_target_pairs={{2,0},{3,1},{6,4},{7,5},{10,8},{11,9},{14,12},{15,13},{18,16},{19,... | collective-permute-start | bytes 245768 | tf_op jit(solution)/shard_map/ppermute | solution.py:107
  73.4 13.0 %copy-start.4 = (bf16[8,2,1152]{2,1,0:T(2,128)(2,1)}, bf16[8,2,1152]{2,1,0:T(2,128)(2,1)S(1)}, u32[]{:S(2)}) copy-start(bf16[8,2,1152]{2,1,0:T(2,128)(2,1)S(1)} %collective-permute-done.1) | copy-start | bytes 110596
  73.4 13.0 %copy-start.6 = (bf16[8,2,1152]{2,1,0:T(2,128)(2,1)}, bf16[8,2,1152]{2,1,0:T(2,128)(2,1)S(1)}, u32[]{:S(2)}) copy-start(bf16[8,2,1152]{2,1,0:T(2,128)(2,1)S(1)} %collective-permute-done.2) | copy-start | bytes 110596
  73.5 12.0 %collective-permute-start.3 = (bf16[2,12,1152]{2,1,0:T(8,128)(2,1)S(1)}, bf16[2,12,1152]{2,1,0:T(8,128)(2,1)S(1)}, u32[]{:S(2)}, u32[]{:S(2)}) collective-permute-start(bf16[2,12,1152]{2,1,0:T(8,128)(2,1)S(1)} %get-tuple-element.9), channel_id=1, source_target_pairs={{0,4},{4,8},{8,12},{1,5},{5,9},{9,13},{2,6},{6,10},{10,14},{3,7},{... | collective-permute-start | bytes 165896 | tf_op jit(solution)/shard_map/ppermute | solution.py:106
  77.0 8.6 %collective-permute-start.4 = (bf16[2,12,1152]{2,1,0:T(8,128)(2,1)S(1)}, bf16[2,12,1152]{2,1,0:T(8,128)(2,1)S(1)}, u32[]{:S(2)}, u32[]{:S(2)}) collective-permute-start(bf16[2,12,1152]{2,1,0:T(8,128)(2,1)S(1)} %get-tuple-element.10), channel_id=1, source_target_pairs={{4,0},{8,4},{12,8},{5,1},{9,5},{13,9},{6,2},{10,6},{14,10},{7,3},{... | collective-permute-start | bytes 165896 | tf_op jit(solution)/shard_map/ppermute | solution.py:107
  78.3 7.3 %copy-start.9 = (f32[16,1,1280]{2,1,0:T(1,128)}, f32[16,1,1280]{2,1,0:T(1,128)S(1)}, u32[]{:S(2)}) copy-start(f32[16,1,1280]{2,1,0:T(1,128)S(1)} %collective-permute-done.6) | copy-start | bytes 245764
  78.4 7.2 %copy-start.11 = (f32[16,1,1280]{2,1,0:T(1,128)}, f32[16,1,1280]{2,1,0:T(1,128)S(1)}, u32[]{:S(2)}) copy-start(f32[16,1,1280]{2,1,0:T(1,128)S(1)} %collective-permute-done.7) | copy-start | bytes 245764
  79.2 14.2 %collective-permute-start.8 = (f32[1,18,1280]{2,1,0:T(8,128)}, f32[1,18,1280]{2,1,0:T(8,128)}, u32[]{:S(2)}, u32[]{:S(2)}) collective-permute-start(f32[1,18,1280]{2,1,0:T(8,128)} %get-tuple-element.5), channel_id=1, source_target_pairs={{0,4},{4,8},{8,12},{1,5},{5,9},{9,13},{2,6},{6,10},{10,14},{3,7},{... | collective-permute-start | bytes 276488 | tf_op jit(solution)/shard_map/ppermute | solution.py:106
  84.3 9.1 %collective-permute-start.9 = (f32[1,18,1280]{2,1,0:T(8,128)}, f32[1,18,1280]{2,1,0:T(8,128)}, u32[]{:S(2)}, u32[]{:S(2)}) collective-permute-start(f32[1,18,1280]{2,1,0:T(8,128)} %get-tuple-element.6), channel_id=1, source_target_pairs={{4,0},{8,4},{12,8},{5,1},{9,5},{13,9},{6,2},{10,6},{14,10},{7,3},{... | collective-permute-start | bytes 276488 | tf_op jit(solution)/shard_map/ppermute | solution.py:107
  87.2 4.4 %copy-start.5 = (bf16[8,2,1152]{2,1,0:T(2,128)(2,1)S(1)}, bf16[8,2,1152]{2,1,0:T(2,128)(2,1)}, u32[]{:S(2)}) copy-start(bf16[8,2,1152]{2,1,0:T(2,128)(2,1)} %copy-done.4) | copy-start | bytes 110596
  87.2 4.4 %copy-start.7 = (bf16[8,2,1152]{2,1,0:T(2,128)(2,1)S(1)}, bf16[8,2,1152]{2,1,0:T(2,128)(2,1)}, u32[]{:S(2)}) copy-start(bf16[8,2,1152]{2,1,0:T(2,128)(2,1)} %copy-done.6) | copy-start | bytes 110596
  87.2 4.4 %copy-start.8 = (s32[12,12,10]{2,1,0:T(8,128)S(1)}, s32[12,12,10]{2,1,0:T(8,128)}, u32[]{:S(2)}) copy-start(s32[12,12,10]{2,1,0:T(8,128)} %iota_add_fusion) | copy-start | bytes 17284
  87.2 4.4 %copy-start.14 = (bf16[2,12,1152]{2,1,0:T(8,128)(2,1)S(1)}, bf16[2,12,1152]{2,1,0:T(8,128)(2,1)}, u32[]{:S(2)}) copy-start(bf16[2,12,1152]{2,1,0:T(8,128)(2,1)} %copy-done.13) | copy-start | bytes 165892
  87.2 4.4 %copy-start.16 = (bf16[2,12,1152]{2,1,0:T(8,128)(2,1)S(1)}, bf16[2,12,1152]{2,1,0:T(8,128)(2,1)}, u32[]{:S(2)}) copy-start(bf16[2,12,1152]{2,1,0:T(8,128)(2,1)} %copy-done.15) | copy-start | bytes 165892
  (11 other events, 24.4 us)

commit v2 on v1

--- a/solution.py
+++ b/solution.py
@@ -18,21 +18,64 @@
 LANES_B = 1024
 
 
-def bands(weight):
-    channels = weight.shape[0]
-    cells = weight.astype(jnp.float32).reshape(channels, 3, 3, 3, channels)
-    pick = (
-        jnp.arange(6)[:, None, None] - jnp.arange(4)[None, :, None] == jnp.arange(3)[None, None, :]
-    ).astype(jnp.float32)
-    band = jnp.einsum("abd,ixydo->xyaibo", pick, cells, precision=lax.Precision.HIGHEST)
-    return band.reshape(9, 6 * channels, 4 * channels).astype(jnp.bfloat16)
+def select(shape, rule):
+    rows = lax.broadcasted_iota(jnp.int32, shape, 0)
+    cols = lax.broadcasted_iota(jnp.int32, shape, 1)
+    return rule(rows, cols)
+
+
+def build_bands(w_ref, band_ref):
+    rows_all = select((384, 64), lambda r, c: (r & 63) == c).astype(jnp.bfloat16)
+    halves = [
+        select((128, 256), lambda r, c, h=h: ((r >> 6) == h) & ((r & 63) == (c & 63))).astype(
+            jnp.bfloat16
+        )
+        for h in range(2)
+    ]
+    for t in range(9):
+        acc = jnp.zeros((384, 256), jnp.float32)
+        for dz in range(3):
+            d = 3 * t + dz
+            block = w_ref[:, 128 * (d // 2) : 128 * (d // 2) + 128]
+            spread = jnp.dot(block, halves[d % 2], preferred_element_type=jnp.float32)
+            tall = jnp.dot(rows_all, spread.astype(jnp.bfloat16), preferred_element_type=jnp.float32)
+            keep = select((384, 256), lambda r, c, dz=dz: (r >> 6) - (c >> 6) == dz)
+            acc = acc + jnp.where(keep, tall, 0.0)
+        band_ref[t] = acc.astype(jnp.bfloat16)
+
+
+def gate_kernel(field_ref, mw_ref, live_ref, ga_ref, gb_ref):
+    tiles = []
+    for part in range(2):
+        pick = select((128, 128), lambda r, c, p=part: ((r >> 6) == p) & ((r & 63) == (c & 63)))
+        spread = jnp.dot(mw_ref[...], pick.astype(jnp.bfloat16), preferred_element_type=jnp.float32)
+        rows_all = select((128, 64), lambda r, c: (r & 63) == c).astype(jnp.bfloat16)
+        tall = jnp.dot(rows_all, spread.astype(jnp.bfloat16), preferred_element_type=jnp.float32)
+        keep = select((128, 128), lambda r, c: (r >> 6) == (c >> 6))
+        tiles.append(jnp.where(keep, tall, 0.0).astype(jnp.bfloat16))
+    live = live_ref[...]
+    for k in range(field_ref.shape[1] // 128):
+        lanes = slice(128 * k, 128 * k + 128)
+        x = field_ref[:, lanes]
+        for tile, out in zip(tiles, (ga_ref, gb_ref)):
+            v = jnp.dot(x, tile, preferred_element_type=jnp.float32)
+            out[:, lanes] = live / (1.0 + jnp.exp(-v))
+
+
+def gate_stage(field2d, mod_weight, live_row):
+    shape = jax.ShapeDtypeStruct(field2d.shape, jnp.float32)
+    return pl.pallas_call(gate_kernel, out_shape=(shape, shape))(field2d, mod_weight, live_row)
 
 
 def silu(v):
     return v / (1.0 + jnp.exp(-v))
 
 
-def fine_kernel(hid_ref, spread_ref, ga_ref, gb_ref, wa_ref, wb_ref, out_ref, fin_ref, lvl_ref):
+def fine_kernel(
+    hid_ref, spread_ref, ga_ref, gb_ref, wa_raw, wb_raw, out_ref, fin_ref, lvl_ref, wa_ref, wb_ref
+):
+    build_bands(wa_raw, wa_ref)
+    build_bands(wb_raw, wb_ref)
     wide_c = hid_ref.shape[1]
     i = lax.broadcasted_iota(jnp.int32, (wide_c, LANES_F), 0)
     j = lax.broadcasted_iota(jnp.int32, (wide_c, LANES_F), 1)
@@ -74,6 +117,8 @@
         scratch_shapes=[
             pltpu.VMEM((ROWS_F, LANES_F), jnp.float32),
             pltpu.VMEM((ROWS_L, LANES_A), jnp.float32),
+            pltpu.VMEM((9, 384, 256), jnp.bfloat16),
+            pltpu.VMEM((9, 384, 256), jnp.bfloat16),
         ],
     )(hid, spread, gate_a, gate_b, band_a, band_b)
 
@@ -164,21 +209,10 @@
     cells = hidden.shape[0] * hidden.shape[1]
     hid = jnp.pad(hidden.reshape(cells, -1), ((0, ROWS_C - cells), (0, 0)))
 
-    eye = jnp.eye(edge, dtype=jnp.float32)
-    flat_w = mod_weight.astype(jnp.float32)
-
-    def gate(part):
-        block = (eye[:, None, :, None] * part[None, :, None, :]).reshape(
-            edge * channels, edge * channels
-        )
-        return jax.nn.sigmoid(
-            jnp.einsum(
-                "xyl,lm->xym", field, block.astype(jnp.bfloat16), preferred_element_type=jnp.float32
-            )
-        ) * live.astype(jnp.float32)
-
-    gate_a = gate(flat_w[:, :channels])
-    gate_b = gate(flat_w[:, channels:])
+    live_row = jnp.broadcast_to(live.astype(jnp.float32), (1, 128))
+    gate_a, gate_b = gate_stage(field.reshape(edge * edge, -1), mod_weight, live_row)
+    gate_a = gate_a.reshape(field.shape)
+    gate_b = gate_b.reshape(field.shape)
     width = edge * channels
     face = jnp.where(first, gate_a[:, :, width - channels :], gate_a[:, :, :channels])
     face = lax.ppermute(face, "gz", [(0, 1), (1, 0)])
@@ -203,7 +237,10 @@
     spread = (inside[:, None] & (source[:, None] == jnp.arange(ROWS_C)[None, :])).astype(
         jnp.bfloat16
     )
-    out = fine_stage(hid, spread, gate_a, gate_b, bands(fine_weight_a), bands(fine_weight_b))
+    wide = ((0, 0), (0, 1792 - fine_weight_a.shape[1]))
+    out = fine_stage(
+        hid, spread, gate_a, gate_b, jnp.pad(fine_weight_a, wide), jnp.pad(fine_weight_b, wide)
+    )
     return out.reshape(edge, STRIDE, width)[:, :edge]
 
 

time: 115 us -> 78.5 us (0.68)
  local copies, waits for them, and re-layouts: 44.9 us -> 11.6 us
  Pallas kernels: 15.6 us -> 24.5 us
  matrix products: 10.6 us -> 4.22 us
  other arithmetic: 16 us -> 9.71 us
  starting transfers between devices: 23.7 us -> 25.6 us
    convert_element_type x6 -> x0, local copies, waits for them, and re-layouts: 32.5 us -> none  [the longest x4 21.6 us: bands(): return band.reshape(9, 6 * channels, 4 * channels).astype(jnp.bfloat16)]
    dot_general x4 -> x0, matrix products: 6.37 us -> none  [the longest x2 3.57 us: bands(): jnp.einsum('abd,ixydo->xyaibo', pick, cells, precision=lax.Precision.HIGH...]
    pallas_call x1, Pallas kernels: 15.6 us -> 21.1 us  [fine_stage(): pl.pallas_call(fine_kernel, out_shape=jax.ShapeDtypeStruct((ROWS_B, LANES...]
    convert_element_type x2 -> x0, other arithmetic: 5.31 us -> none  [the longest x1 5.3 us: gate(): block.astype(jnp.bfloat16)]
    pallas_call x0 -> x1, Pallas kernels: none -> 3.42 us  [gate_stage(): pl.pallas_call(gate_kernel, out_shape=(shape, shape))]
    ppermute x4, starting transfers between devices: 18 us -> 19.9 us  [grow(): low = lax.ppermute(tail, axis, shift_pairs(count, True))]
    unnamed x50 -> x10, local copies, waits for them, and re-layouts: 1.68 us -> 0.02 us
    select_n x1, other arithmetic: 1.61 us -> 0.02 us  [body(): jnp.where(first, face, blank)]
  transfers between devices with their start and end apart: 10 -> 10, of which waited for: 1 -> 0; matrix products, arithmetic and copies ran while one was open for 44% -> 21% of each run, Pallas kernels for 0% -> 4%
where the time goes in v2:
time: 78.5 us; the launch traced here: 77.9 us
  starting transfers between devices  25.6 us (33%)
  Pallas kernels  24.5 us (31%)
  local copies, waits for them, and re-layouts  11.6 us (15%)
  other arithmetic  9.71 us (12%)
  matrix products  4.22 us (5%)
  between operations  2.26 us (3%)
    pallas_call x1, Pallas kernels, fine_stage(): pl.pallas_call(fine_kernel, out_shape=jax.ShapeDtypeStruct((ROWS_B, LANES...  21.1 us
    ppermute x4, starting transfers between devices, grow(): low = lax.ppermute(tail, axis, shift_pairs(count, True))  19.9 us
    ppermute x4, starting transfers between devices, grow(): high = lax.ppermute(head, axis, shift_pairs(count, False))  5.16 us
    conv_general_dilated x1, matrix products, convolve(): lax.conv_general_dilated(padded[None], kernel, (1, 1, 1), 'VALID', dimens...  4.22 us
    pallas_call x1, Pallas kernels, gate_stage(): pl.pallas_call(gate_kernel, out_shape=(shape, shape))  3.42 us
    concatenate x2, other arithmetic, grow(): return jnp.concatenate([low, cells, high], axis=dim)  2.89 us
    slice x1, local copies, waits for them, and re-layouts, body(): return out.reshape(edge, STRIDE, width)[:, :edge]  1.88 us
    select_n x1, other arithmetic, body(): jnp.where(first, gate_a[:, :, width - channels:], gate_a[:, :, :channels])  1.81 us
  transfers between devices with their start and end apart: 10, of which 0 were waited for; matrix products, arithmetic and copies ran while one was open for 21% of the time, Pallas kernels for 4%

profile of v2, /device:TPU:0, one launch (start us, length us, event | category | flops | bytes accessed | tf_op | source)
XLA Modules:
  0.0 77.9 jit_solution(6201008730186238124)
XLA Ops:
  0.0 0.8 convert_element_type.42
  1.5 1.0 %concatenate.27 = bf16[8,4,1152]{2,1,0:T(4,128)(2,1)S(1)} concatenate(bf16[8,4,1024]{2,1,0:T(4,128)(2,1)} %param.8, bf16[8,4,16]{2,1,0:T(4,128)(2,1)S(1)} %convert_element_type.42, bf16[8,4,1]{2,1,0:T(4,128)(2,1)S(1)} %broadcast_in_dim.33, bf16[8,4,111]{2,1,0:T(4,128)(2,1)S(1)} %broadcast_in_dim.34), dimensions={2} | concatenate | bytes 147456 | tf_op jit(solution)/shard_map/concatenate | solution.py:178
  3.5 3.4 %shard_map.82 = (f32[256,1024]{1,0:T(8,128)}, f32[256,1024]{1,0:T(8,128)}) custom-call(bf16[256,1024]{1,0:T(8,128)(2,1)} %bitcast.32, bf16[64,128]{1,0:T(8,128)(2,1)} %mw_ref.1, f32[1,128]{1,0:T(1,128)} %broadcast_in_dim.40.live_ref), custom_call_target="tpu_custom_call" | custom-call | tf_op jit(solution)/shard_map/pallas_call | solution.py:67
  6.9 1.8 %slice_select_fusion = f32[16,16,64]{2,1,0:T(8,128)} fusion(f32[16,16,1024]{2,1,0:T(8,128)} %bitcast.29, pred[]{:T(512)S(6)} %eq.18), kind=kLoop, calls=%fused_computation.28 | loop fusion | flops 16384 | bytes 196609 | tf_op jit(solution)/shard_map/jit(_where)/select_n | solution.py:217
  8.8 1.5 %reshape.94 = bf16[64,3,3,3,64]{4,3,2,1,0:T(4,128)(2,1)S(1)} reshape(bf16[64,1728]{1,0:T(8,128)(2,1)} %param.12) | data formatting | bytes 442368 | tf_op jit(solution)/shard_map/reshape | solution.py:128
  11.1 0.7 pad.33.wb_raw
  11.8 0.8 %fusion.14.spread_ref = bf16[488,112]{1,0:T(8,128)(2,1)} fusion(s32[488]{0:T(512)S(1)} %fusion.33, pred[488]{0:T(512)(128)(4,1)S(1)} %compare_and_fusion), kind=kLoop, calls=%fused_computation.24 | loop fusion | flops 163968 | bytes 111752 | tf_op jit(solution)/shard_map/convert_element_type | solution.py:237
  12.7 1.3 %pad.31 = f32[16,24,1024]{2,1,0:T(8,128)} pad(f32[16,16,1024]{2,1,0:T(8,128)S(1)} %bitcast.31, f32[]{:T(128)} %constant.62.clone.1), padding=0_0x0_8x0_0 | pad | bytes 2621444 | tf_op jit(solution)/shard_map/jit(_pad)/pad | solution.py:231
  14.6 0.8 %concatenate.33 = f32[16,16,1280]{2,1,0:T(8,128)S(1)} concatenate(f32[16,16,64]{2,1,0:T(8,128)S(1)} %get-tuple-element.18, f32[16,16,1024]{2,1,0:T(8,128)S(1)} %bitcast.30, f32[16,16,64]{2,1,0:T(8,128)S(1)} %get-tuple-element.17, f32[16,16,128]{2,1,0:T(8,128)S(1)} %broadcast_in_dim.41), dimensions={2} | concatenate | bytes 2621440 | tf_op jit(solution)/shard_map/concatenate | solution.py:220
  15.5 1.2 %slice.74 = bf16[1,1,1]{2,1,0:T(2,128)(2,1)} slice(bf16[8,4,1152]{2,1,0:T(4,128)(2,1)} %collective-permute-done), slice={[0:1], [0:1], [1040:1041]} | slice | bytes 4 | tf_op jit(solution)/shard_map/slice | solution.py:181
  18.0 1.1 %maximum_select_fusion = bf16[8,8,1152]{2,1,0:T(8,128)(2,1)S(1)} fusion(bf16[8,4,1152]{2,1,0:T(4,128)(2,1)} %collective-permute-done, bf16[8,4,1152]{2,1,0:T(4,128)(2,1)S(1)} %concatenate.27, pred[]{:T(512)S(6)} %eq.18), kind=kLoop, calls=%fused_computation.27 | loop fusion | flops 663552 | bytes 294913 | tf_op jit(solution)/shard_map/jit(_where)/select_n | solution.py:180
  19.3 1.3 %collective-permute-start.2 = (bf16[8,2,1152]{2,1,0:T(2,128)(2,1)S(1)}, bf16[8,2,1152]{2,1,0:T(2,128)(2,1)S(1)}, u32[]{:S(2)}, u32[]{:S(2)}) collective-permute-start(bf16[8,2,1152]{2,1,0:T(2,128)(2,1)S(1)} %get-tuple-element.16), channel_id=1, source_target_pairs={{2,0},{3,1},{6,4},{7,5},{10,8},{11,9},{14,12},{15,13},{18,16},{19,... | collective-permute-start | bytes 110600 | tf_op jit(solution)/shard_map/ppermute | solution.py:152
  20.6 4.8 %collective-permute-start.1 = (bf16[8,2,1152]{2,1,0:T(2,128)(2,1)S(1)}, bf16[8,2,1152]{2,1,0:T(2,128)(2,1)S(1)}, u32[]{:S(2)}, u32[]{:S(2)}) collective-permute-start(bf16[8,2,1152]{2,1,0:T(2,128)(2,1)S(1)} %get-tuple-element.15), channel_id=1, source_target_pairs={{0,2},{1,3},{4,6},{5,7},{8,10},{9,11},{12,14},{13,15},{16,18},{17,... | collective-permute-start | bytes 110600 | tf_op jit(solution)/shard_map/ppermute | solution.py:151
  25.6 1.3 %collective-permute-start.7 = (f32[16,1,1280]{2,1,0:T(1,128)S(1)}, f32[16,1,1280]{2,1,0:T(1,128)S(1)}, u32[]{:S(2)}, u32[]{:S(2)}) collective-permute-start(f32[16,1,1280]{2,1,0:T(1,128)S(1)} %get-tuple-element.12), channel_id=1, source_target_pairs={{2,0},{3,1},{6,4},{7,5},{10,8},{11,9},{14,12},{15,13},{18,16},{19,... | collective-permute-start | bytes 245768 | tf_op jit(solution)/shard_map/ppermute | solution.py:152
  26.9 4.6 %collective-permute-start.6 = (f32[16,1,1280]{2,1,0:T(1,128)S(1)}, f32[16,1,1280]{2,1,0:T(1,128)S(1)}, u32[]{:S(2)}, u32[]{:S(2)}) collective-permute-start(f32[16,1,1280]{2,1,0:T(1,128)S(1)} %get-tuple-element.11), channel_id=1, source_target_pairs={{0,2},{1,3},{4,6},{5,7},{8,10},{9,11},{12,14},{13,15},{16,18},{17,... | collective-permute-start | bytes 245768 | tf_op jit(solution)/shard_map/ppermute | solution.py:151
  31.5 1.3 %collective-permute-start.4 = (bf16[2,12,1152]{2,1,0:T(8,128)(2,1)S(1)}, bf16[2,12,1152]{2,1,0:T(8,128)(2,1)S(1)}, u32[]{:S(2)}, u32[]{:S(2)}) collective-permute-start(bf16[2,12,1152]{2,1,0:T(8,128)(2,1)S(1)} %get-tuple-element.14), channel_id=1, source_target_pairs={{4,0},{8,4},{12,8},{5,1},{9,5},{13,9},{6,2},{10,6},{14,10},{7,3},{... | collective-permute-start | bytes 165896 | tf_op jit(solution)/shard_map/ppermute | solution.py:152
  32.8 5.3 %collective-permute-start.3 = (bf16[2,12,1152]{2,1,0:T(8,128)(2,1)S(1)}, bf16[2,12,1152]{2,1,0:T(8,128)(2,1)S(1)}, u32[]{:S(2)}, u32[]{:S(2)}) collective-permute-start(bf16[2,12,1152]{2,1,0:T(8,128)(2,1)S(1)} %get-tuple-element.13), channel_id=1, source_target_pairs={{0,4},{4,8},{8,12},{1,5},{5,9},{9,13},{2,6},{6,10},{10,14},{3,7},{... | collective-permute-start | bytes 165896 | tf_op jit(solution)/shard_map/ppermute | solution.py:151
  38.1 0.7 pad_maximum_fusion.3
  38.9 1.3 %collective-permute-start.9 = (f32[1,18,1280]{2,1,0:T(8,128)}, f32[1,18,1280]{2,1,0:T(8,128)}, u32[]{:S(2)}, u32[]{:S(2)}) collective-permute-start(f32[1,18,1280]{2,1,0:T(8,128)} %get-tuple-element.10), channel_id=1, source_target_pairs={{4,0},{8,4},{12,8},{5,1},{9,5},{13,9},{6,2},{10,6},{14,10},{7,3},{... | collective-permute-start | bytes 276488 | tf_op jit(solution)/shard_map/ppermute | solution.py:152
  40.2 5.2 %collective-permute-start.8 = (f32[1,18,1280]{2,1,0:T(8,128)}, f32[1,18,1280]{2,1,0:T(8,128)}, u32[]{:S(2)}, u32[]{:S(2)}) collective-permute-start(f32[1,18,1280]{2,1,0:T(8,128)} %get-tuple-element.9), channel_id=1, source_target_pairs={{0,4},{4,8},{8,12},{1,5},{5,9},{9,13},{2,6},{6,10},{10,14},{3,7},{... | collective-permute-start | bytes 276488 | tf_op jit(solution)/shard_map/ppermute | solution.py:151
  46.3 4.2 %fusion.5 = f32[1,10,10,10,64]{4,0,3,2,1:T(1,128)S(1)} fusion(bf16[1,12,12,12,64]{4,3,2,1,0:T(8,128)(2,1)S(1)} %fusion.11, bf16[64,3,3,3,64]{4,3,2,1,0:T(4,128)(2,1)S(1)} %reshape.94), kind=kOutput, calls=%fused_computation.10 | convolution fusion | flops 221184000 | bytes 698368 | tf_op jit(solution)/shard_map/conv_general_dilated | solution.py:129
  52.3 2.7 %select_maximum_fusion = f32[18,24,1280]{2,1,0:T(8,128)} fusion(f32[1,18,1280]{2,1,0:T(8,128)} %collective-permute-done.9, f32[1,18,1280]{2,1,0:T(8,128)} %collective-permute-done.8, f32[16,1,1280]{2,1,0:T(1,128)S(1)} %collective-permute-done.7, f32[16,16,1280]{2,1,0:T(8,128)S(1)} %concatenate.33, f32[16,1,1280]{2,1,0:T(1,128)S(1)} %collective-permute-done.6), kind=kLoop, calls=%fused_computation | loop fusion | flops 5529600 | bytes 3870720 | tf_op jit(solution)/shard_map/concatenate | solution.py:153
  55.0 21.1 %shard_map.83 = bf16[384,1024]{1,0:T(8,128)(2,1)} custom-call(bf16[112,640]{1,0:T(8,128)(2,1)} %pad.29.hid_ref, bf16[488,112]{1,0:T(8,128)(2,1)} %fusion.14.spread_ref, f32[432,1280]{1,0:T(8,128)} %bitcast.26, f32[384,1024]{1,0:T(8,128)} %bitcast.27, bf16[64,1792]{1,0:T(8,128)(2,1)} %pad.32.wa_raw, bf16[64,1792]{1,0:T(8,128)(2,1)} %pad.33.wb_raw), custom_call_target="tpu_custom_call" | custom-call | tf_op jit(solution)/shard_map/pallas_call | solution.py:114
  76.0 1.9 %slice.83 = bf16[16,16,1024]{2,1,0:T(8,128)(2,1)} slice(bf16[16,24,1024]{2,1,0:T(8,128)(2,1)} %bitcast.28), slice={[0:16], [0:16], [0:1024]} | slice | bytes 1048576 | tf_op jit(solution)/shard_map/slice | solution.py:244
  (48 shorter events, 5.5 us)
Async XLA Ops:
  0.0 10.4 %copy-start.2 = (bf16[64,1728]{1,0:T(8,128)(2,1)S(1)}, bf16[64,1728]{1,0:T(8,128)(2,1)}, u32[]{:S(2)}) copy-start(bf16[64,1728]{1,0:T(8,128)(2,1)} %param.13) | copy-start | bytes 663556
  0.0 11.1 %copy-start.3 = (bf16[64,1728]{1,0:T(8,128)(2,1)S(1)}, bf16[64,1728]{1,0:T(8,128)(2,1)}, u32[]{:S(2)}) copy-start(bf16[64,1728]{1,0:T(8,128)(2,1)} %param.14) | copy-start | bytes 663556
  2.4 13.0 %collective-permute-start = (bf16[8,4,1152]{2,1,0:T(4,128)(2,1)S(1)}, bf16[8,4,1152]{2,1,0:T(4,128)(2,1)}, u32[]{:S(2)}, u32[]{:S(2)}) collective-permute-start(bf16[8,4,1152]{2,1,0:T(4,128)(2,1)S(1)} %concatenate.27), channel_id=1, source_target_pairs={{0,1},{1,0},{2,3},{3,2},{4,5},{5,4},{6,7},{7,6},{8,9},{9,8},{10,11... | collective-permute-start | bytes 221192 | tf_op jit(solution)/shard_map/ppermute | solution.py:179
  6.9 5.8 %copy-start.1 = (f32[256,1024]{1,0:T(8,128)S(1)}, f32[256,1024]{1,0:T(8,128)}, u32[]{:S(2)}) copy-start(f32[256,1024]{1,0:T(8,128)} %get-tuple-element.8) | copy-start | bytes 3145732
  8.7 5.9 %collective-permute-start.5 = (f32[16,16,64]{2,1,0:T(8,128)}, f32[16,16,64]{2,1,0:T(8,128)S(1)}, u32[]{:S(2)}, u32[]{:S(2)}) collective-permute-start(f32[16,16,64]{2,1,0:T(8,128)} %slice_select_fusion), channel_id=1, source_target_pairs={{0,1},{1,0},{2,3},{3,2},{4,5},{5,4},{6,7},{7,6},{8,9},{9,8},{10,11... | collective-permute-start | bytes 196616 | tf_op jit(solution)/shard_map/ppermute | solution.py:218
  10.3 4.3 %copy-start = (f32[256,1024]{1,0:T(8,128)S(1)}, f32[256,1024]{1,0:T(8,128)}, u32[]{:S(2)}) copy-start(f32[256,1024]{1,0:T(8,128)} %get-tuple-element.7) | copy-start | bytes 3145732
  19.3 12.1 %collective-permute-start.2 = (bf16[8,2,1152]{2,1,0:T(2,128)(2,1)S(1)}, bf16[8,2,1152]{2,1,0:T(2,128)(2,1)S(1)}, u32[]{:S(2)}, u32[]{:S(2)}) collective-permute-start(bf16[8,2,1152]{2,1,0:T(2,128)(2,1)S(1)} %get-tuple-element.16), channel_id=1, source_target_pairs={{2,0},{3,1},{6,4},{7,5},{10,8},{11,9},{14,12},{15,13},{18,16},{19,... | collective-permute-start | bytes 110600 | tf_op jit(solution)/shard_map/ppermute | solution.py:152
  20.6 10.8 %collective-permute-start.1 = (bf16[8,2,1152]{2,1,0:T(2,128)(2,1)S(1)}, bf16[8,2,1152]{2,1,0:T(2,128)(2,1)S(1)}, u32[]{:S(2)}, u32[]{:S(2)}) collective-permute-start(bf16[8,2,1152]{2,1,0:T(2,128)(2,1)S(1)} %get-tuple-element.15), channel_id=1, source_target_pairs={{0,2},{1,3},{4,6},{5,7},{8,10},{9,11},{12,14},{13,15},{16,18},{17,... | collective-permute-start | bytes 110600 | tf_op jit(solution)/shard_map/ppermute | solution.py:151
  25.6 12.5 %collective-permute-start.7 = (f32[16,1,1280]{2,1,0:T(1,128)S(1)}, f32[16,1,1280]{2,1,0:T(1,128)S(1)}, u32[]{:S(2)}, u32[]{:S(2)}) collective-permute-start(f32[16,1,1280]{2,1,0:T(1,128)S(1)} %get-tuple-element.12), channel_id=1, source_target_pairs={{2,0},{3,1},{6,4},{7,5},{10,8},{11,9},{14,12},{15,13},{18,16},{19,... | collective-permute-start | bytes 245768 | tf_op jit(solution)/shard_map/ppermute | solution.py:152
  26.9 11.2 %collective-permute-start.6 = (f32[16,1,1280]{2,1,0:T(1,128)S(1)}, f32[16,1,1280]{2,1,0:T(1,128)S(1)}, u32[]{:S(2)}, u32[]{:S(2)}) collective-permute-start(f32[16,1,1280]{2,1,0:T(1,128)S(1)} %get-tuple-element.11), channel_id=1, source_target_pairs={{0,2},{1,3},{4,6},{5,7},{8,10},{9,11},{12,14},{13,15},{16,18},{17,... | collective-permute-start | bytes 245768 | tf_op jit(solution)/shard_map/ppermute | solution.py:151
  31.5 13.8 %collective-permute-start.4 = (bf16[2,12,1152]{2,1,0:T(8,128)(2,1)S(1)}, bf16[2,12,1152]{2,1,0:T(8,128)(2,1)S(1)}, u32[]{:S(2)}, u32[]{:S(2)}) collective-permute-start(bf16[2,12,1152]{2,1,0:T(8,128)(2,1)S(1)} %get-tuple-element.14), channel_id=1, source_target_pairs={{4,0},{8,4},{12,8},{5,1},{9,5},{13,9},{6,2},{10,6},{14,10},{7,3},{... | collective-permute-start | bytes 165896 | tf_op jit(solution)/shard_map/ppermute | solution.py:152
  32.8 12.5 %collective-permute-start.3 = (bf16[2,12,1152]{2,1,0:T(8,128)(2,1)S(1)}, bf16[2,12,1152]{2,1,0:T(8,128)(2,1)S(1)}, u32[]{:S(2)}, u32[]{:S(2)}) collective-permute-start(bf16[2,12,1152]{2,1,0:T(8,128)(2,1)S(1)} %get-tuple-element.13), channel_id=1, source_target_pairs={{0,4},{4,8},{8,12},{1,5},{5,9},{9,13},{2,6},{6,10},{10,14},{3,7},{... | collective-permute-start | bytes 165896 | tf_op jit(solution)/shard_map/ppermute | solution.py:151
  38.9 13.4 %collective-permute-start.9 = (f32[1,18,1280]{2,1,0:T(8,128)}, f32[1,18,1280]{2,1,0:T(8,128)}, u32[]{:S(2)}, u32[]{:S(2)}) collective-permute-start(f32[1,18,1280]{2,1,0:T(8,128)} %get-tuple-element.10), channel_id=1, source_target_pairs={{4,0},{8,4},{12,8},{5,1},{9,5},{13,9},{6,2},{10,6},{14,10},{7,3},{... | collective-permute-start | bytes 276488 | tf_op jit(solution)/shard_map/ppermute | solution.py:152
  40.2 12.1 %collective-permute-start.8 = (f32[1,18,1280]{2,1,0:T(8,128)}, f32[1,18,1280]{2,1,0:T(8,128)}, u32[]{:S(2)}, u32[]{:S(2)}) collective-permute-start(f32[1,18,1280]{2,1,0:T(8,128)} %get-tuple-element.9), channel_id=1, source_target_pairs={{0,4},{4,8},{8,12},{1,5},{5,9},{9,13},{2,6},{6,10},{10,14},{3,7},{... | collective-permute-start | bytes 276488 | tf_op jit(solution)/shard_map/ppermute | solution.py:151
  46.3 4.2 %copy-start.4 = (pred[12,12,20]{2,1,0:T(8,128)(4,1)S(1)}, pred[12,12,20]{2,1,0:T(8,128)(4,1)}, u32[]{:S(2)}) copy-start(pred[12,12,20]{2,1,0:T(8,128)(4,1)} %get-tuple-element.20) | copy-start | bytes 8644

commit v3 on v2

--- a/solution.py
+++ b/solution.py
@@ -143,6 +143,31 @@
     return [(k + 1, k) for k in range(count - 1)]
 
 
+def grow_both(cells, gate, axis, dim, widths):
+    count = lax.axis_size(axis)
+    lanes = gate.shape[-1]
+
+    def ends(arr, width):
+        size = arr.shape[dim]
+        return lax.slice_in_dim(arr, 0, width, axis=dim), lax.slice_in_dim(arr, size - width, size, axis=dim)
+
+    (cells_head, cells_tail), (gate_head, gate_tail) = ends(cells, widths[0]), ends(gate, widths[1])
+
+    def pack(c, g):
+        return jnp.concatenate([c.astype(jnp.float32).reshape(-1, lanes), g.reshape(-1, lanes)], 0)
+
+    def unpack(m):
+        split = cells_head.size // lanes
+        return m[:split].reshape(cells_head.shape).astype(cells.dtype), m[split:].reshape(gate_head.shape)
+
+    low = unpack(lax.ppermute(pack(cells_tail, gate_tail), axis, shift_pairs(count, True)))
+    high = unpack(lax.ppermute(pack(cells_head, gate_head), axis, shift_pairs(count, False)))
+    return (
+        jnp.concatenate([low[0], cells, high[0]], axis=dim),
+        jnp.concatenate([low[1], gate, high[1]], axis=dim),
+    )
+
+
 def grow(cells, axis, dim, width):
     count = lax.axis_size(axis)
     size = cells.shape[dim]
@@ -162,7 +187,7 @@
     edge = field.shape[0]
     half = edge // 2
     assert lax.axis_size("gz") == 2 and rows_x == half and 2 * rows_y == half
-    lanes = 128
+    lanes = 256
     zside = lax.axis_index("gz")
     first = zside == 0
     live = brick_live.reshape(())
@@ -194,21 +219,6 @@
         axis=2,
     )
 
-    region = grow(grow(packed, "gy", 1, 2), "gx", 0, 2)
-    size = region.shape[0]
-    volume = region[:, :, :flat_z].reshape(size, size, cells_z, channels)
-    volume = jnp.pad(volume, ((0, 0), (0, 0), (2, 2), (0, 0)))
-    volume = lax.dynamic_slice_in_dim(volume, zside * half, half + 4, axis=2)
-    keep = jnp.pad(region[:, :, flat_z : flat_z + cells_z], ((0, 0), (0, 0), (2, 2)))
-    keep = lax.dynamic_slice_in_dim(keep, zside * half + 1, half + 2, axis=2)[1:-1, 1:-1]
-    activity = convolve(volume, coarse_weight)
-    centre = volume[1:-1, 1:-1, 1:-1].astype(jnp.float32)
-    hidden = ((centre + jax.nn.silu(activity)) * keep[..., None].astype(jnp.float32)).astype(
-        jnp.bfloat16
-    )
-    cells = hidden.shape[0] * hidden.shape[1]
-    hid = jnp.pad(hidden.reshape(cells, -1), ((0, ROWS_C - cells), (0, 0)))
-
     live_row = jnp.broadcast_to(live.astype(jnp.float32), (1, 128))
     gate_a, gate_b = gate_stage(field.reshape(edge * edge, -1), mod_weight, live_row)
     gate_a = gate_a.reshape(field.shape)
@@ -226,7 +236,22 @@
         ],
         axis=2,
     )
-    gate_a = grow(grow(gate_a, "gy", 1, 1), "gx", 0, 1)
+    region, gate_a = grow_both(packed, gate_a, "gy", 1, (2, 1))
+    region, gate_a = grow_both(region, gate_a, "gx", 0, (2, 1))
+    size = region.shape[0]
+    volume = region[:, :, :flat_z].reshape(size, size, cells_z, channels)
+    volume = jnp.pad(volume, ((0, 0), (0, 0), (2, 2), (0, 0)))
+    volume = lax.dynamic_slice_in_dim(volume, zside * half, half + 4, axis=2)
+    keep = jnp.pad(region[:, :, flat_z : flat_z + cells_z], ((0, 0), (0, 0), (2, 2)))
+    keep = lax.dynamic_slice_in_dim(keep, zside * half + 1, half + 2, axis=2)[1:-1, 1:-1]
+    activity = convolve(volume, coarse_weight)
+    centre = volume[1:-1, 1:-1, 1:-1].astype(jnp.float32)
+    hidden = ((centre + jax.nn.silu(activity)) * keep[..., None].astype(jnp.float32)).astype(
+        jnp.bfloat16
+    )
+    cells = hidden.shape[0] * hidden.shape[1]
+    hid = jnp.pad(hidden.reshape(cells, -1), ((0, ROWS_C - cells), (0, 0)))
+
     gate_a = jnp.pad(gate_a, ((0, 0), (0, STRIDE - edge - 2), (0, 0))).reshape(-1, gate_a.shape[2])
     gate_b = jnp.pad(gate_b, ((0, 0), (0, STRIDE - edge), (0, 0))).reshape(-1, width)
 

time: 78.5 us -> 73.3 us (0.934)
  starting transfers between devices: 25.6 us -> 13.2 us
  waiting for transfers between devices: 0.03 us -> 7.04 us
  other arithmetic: 9.71 us -> 5.64 us
  local copies, waits for them, and re-layouts: 11.6 us -> 15.4 us
    ppermute x8 -> x4, starting transfers between devices: 25 us -> 12.6 us  [the longest x2 10 us: grow_both(): lax.ppermute(pack(cells_tail, gate_tail), axis, shift_pairs(count, True))]
    ppermute x8 -> x4, waiting for transfers between devices: 0.02 us -> 7.04 us  [the longest x2 3.57 us: grow_both(): lax.ppermute(pack(cells_head, gate_head), axis, shift_pairs(count, False))]
    reshape x0 -> x10, local copies, waits for them, and re-layouts: none -> 2.23 us  [the longest x1 1.92 us: body(): gate_a = gate_a.reshape(field.shape)]
    concatenate x2 -> x6, other arithmetic: 2.89 us -> 1.24 us  [the longest x4 0.76 us: pack(): jnp.concatenate([c.astype(jnp.float32).reshape(-1, lanes), g.reshape(-1,...]
    pad x0 -> x1, local copies, waits for them, and re-layouts: none -> 1.54 us  [body(): jnp.pad(gate_a, ((0, 0), (0, STRIDE - edge - 2), (0, 0)))]
    reshape x1, local copies, waits for them, and re-layouts: 1.54 us -> 0.34 us  [convolve(): weight.reshape(channels, 3, 3, 3, channels).transpose(1, 2, 3, 0, 4)]
    unnamed x10 -> x21, local copies, waits for them, and re-layouts: 0.02 us -> 1.08 us
    select_n x1, other arithmetic: 1.81 us -> 0.76 us  [body(): jnp.where(first, gate_a[:, :, width - channels:], gate_a[:, :, :channels])]
  transfers between devices with their start and end apart: 10 -> 6, of which waited for: 0 -> 4; matrix products, arithmetic and copies ran while one was open for 21% -> 10% of each run, Pallas kernels for 4% -> 0%
where the time goes in v3:
time: 73.3 us; the launch traced here: 72.4 us
  Pallas kernels  24.5 us (33%)
  local copies, waits for them, and re-layouts  15.4 us (21%)
  starting transfers between devices  13.2 us (18%)
  waiting for transfers between devices  7.04 us (10%)
  other arithmetic  5.64 us (8%)
  matrix products  4.22 us (6%)
  between operations  2.5 us (3%)
    pallas_call x1, Pallas kernels, fine_stage(): pl.pallas_call(fine_kernel, out_shape=jax.ShapeDtypeStruct((ROWS_B, LANES...  21.1 us
    ppermute x2, starting transfers between devices, grow_both(): lax.ppermute(pack(cells_tail, gate_tail), axis, shift_pairs(count, True))  10 us
    conv_general_dilated x1, matrix products, convolve(): lax.conv_general_dilated(padded[None], kernel, (1, 1, 1), 'VALID', dimens...  4.22 us
    ppermute x2, waiting for transfers between devices, grow_both(): lax.ppermute(pack(cells_head, gate_head), axis, shift_pairs(count, False))  3.57 us
    ppermute x2, waiting for transfers between devices, grow_both(): lax.ppermute(pack(cells_tail, gate_tail), axis, shift_pairs(count, True))  3.47 us
    pallas_call x1, Pallas kernels, gate_stage(): pl.pallas_call(gate_kernel, out_shape=(shape, shape))  3.41 us
    ppermute x2, starting transfers between devices, grow_both(): lax.ppermute(pack(cells_head, gate_head), axis, shift_pairs(count, False))  2.58 us
    reshape x1, local copies, waits for them, and re-layouts, body(): gate_a = gate_a.reshape(field.shape)  1.92 us
  transfers between devices with their start and end apart: 6, of which 4 were waited for; matrix products, arithmetic and copies ran while one was open for 10% of the time, Pallas kernels for 0%

profile of v3, /device:TPU:0, one launch (start us, length us, event | category | flops | bytes accessed | tf_op | source)
XLA Modules:
  0.0 72.4 jit_solution(5978860503690597196)
XLA Ops:
  1.3 3.4 %shard_map.82 = (f32[256,1024]{1,0:T(8,128)}, f32[256,1024]{1,0:T(8,128)}) custom-call(bf16[256,1024]{1,0:T(8,128)(2,1)} %bitcast.45, bf16[64,128]{1,0:T(8,128)(2,1)} %mw_ref.1, f32[1,128]{1,0:T(1,128)} %broadcast_in_dim.39.live_ref), custom_call_target="tpu_custom_call" | custom-call | tf_op jit(solution)/shard_map/pallas_call | solution.py:67
  4.7 1.9 %copy.23 = f32[16,16,1024]{2,0,1:T(8,128)S(1)} copy(f32[16,16,1024]{2,1,0:T(8,128)} %bitcast.44) | data formatting | bytes 2097152 | tf_op jit(solution)/shard_map/reshape | solution.py:224
  6.6 0.8 %slice_select_fusion = f32[16,16,64]{2,0,1:T(8,128)} fusion(f32[16,16,1024]{2,0,1:T(8,128)S(1)} %copy.23, pred[]{:T(512)S(6)} %eq.18), kind=kLoop, calls=%fused_computation.25 | loop fusion | flops 16384 | bytes 196609 | tf_op jit(solution)/shard_map/jit(_where)/select_n | solution.py:227
  9.2 0.7 pad.32.wa_raw
  9.9 1.6 %pad.33.wb_raw = bf16[64,1792]{1,0:T(8,128)(2,1)} pad(bf16[64,1728]{1,0:T(8,128)(2,1)} %param.14, bf16[]{:T(256)} %constant.53.clone.1), padding=0_0x0_64 | pad | bytes 450562 | tf_op jit(solution)/shard_map/jit(_pad)/pad | solution.py:267
  11.6 1.3 %pad.31 = f32[16,24,1024]{2,1,0:T(8,128)} pad(f32[16,16,1024]{2,1,0:T(8,128)S(1)} %bitcast.43, f32[]{:T(128)} %constant.55.clone.1), padding=0_0x0_8x0_0 | pad | bytes 2621444 | tf_op jit(solution)/shard_map/jit(_pad)/pad | solution.py:256
  12.9 0.8 %concatenate.43 = f32[16,16,1280]{2,0,1:T(8,128)S(1)} concatenate(f32[16,16,64]{2,0,1:T(8,128)S(1)} %get-tuple-element.18, f32[16,16,1024]{2,0,1:T(8,128)S(1)} %copy.23, f32[16,16,64]{2,0,1:T(8,128)S(1)} %get-tuple-element.17, f32[16,16,128]{2,0,1:T(8,128)S(1)} %broadcast_in_dim.40), dimensions={2} | concatenate | bytes 2621440 | tf_op jit(solution)/shard_map/concatenate | solution.py:230
  13.8 1.3 %slice.110 = bf16[1,1,1]{2,1,0:T(2,128)(2,1)} slice(bf16[8,4,1280]{2,1,0:T(4,128)(2,1)} %collective-permute-done), slice={[0:1], [0:1], [1040:1041]} | slice | bytes 4 | tf_op jit(solution)/shard_map/slice | solution.py:206
  16.3 1.1 %maximum_select_fusion = bf16[8,8,1280]{2,1,0:T(8,128)(2,1)S(1)} fusion(bf16[8,4,1280]{2,1,0:T(4,128)(2,1)} %collective-permute-done, bf16[8,4,1280]{2,1,0:T(4,128)(2,1)S(1)} %concatenate.39, pred[]{:T(512)S(6)} %eq.18), kind=kLoop, calls=%fused_computation.20 | loop fusion | flops 737280 | bytes 327681 | tf_op jit(solution)/shard_map/jit(_where)/select_n | solution.py:205
  17.8 1.3 %collective-permute-start.3 = (f32[32,1280]{1,0:T(8,128)S(1)}, f32[32,1280]{1,0:T(8,128)S(1)}, u32[]{:S(2)}, u32[]{:S(2)}) collective-permute-start(f32[32,1280]{1,0:T(8,128)S(1)} %pad_maximum_fusion.5), channel_id=1, source_target_pairs={{2,0},{3,1},{6,4},{7,5},{10,8},{11,9},{14,12},{15,13},{18,16},{19,... | collective-permute-start | bytes 491528 | tf_op jit(solution)/shard_map/ppermute | solution.py:164
  19.2 4.9 %collective-permute-start.2 = (f32[32,1280]{1,0:T(8,128)S(1)}, f32[32,1280]{1,0:T(8,128)S(1)}, u32[]{:S(2)}, u32[]{:S(2)}) collective-permute-start(f32[32,1280]{1,0:T(8,128)S(1)} %pad_maximum_fusion.4), channel_id=1, source_target_pairs={{0,2},{1,3},{4,6},{5,7},{8,10},{9,11},{12,14},{13,15},{16,18},{17,... | collective-permute-start | bytes 491528 | tf_op jit(solution)/shard_map/ppermute | solution.py:163
  24.0 2.3 %collective-permute-done.3 = f32[32,1280]{1,0:T(8,128)S(1)} collective-permute-done((f32[32,1280]{1,0:T(8,128)S(1)}, f32[32,1280]{1,0:T(8,128)S(1)}, u32[]{:S(2)}, u32[]{:S(2)}) %collective-permute-start.3) | collective-permute-done | bytes 163872 | tf_op jit(solution)/shard_map/ppermute | solution.py:164
  26.4 1.3 %collective-permute-done.2 = f32[32,1280]{1,0:T(8,128)S(1)} collective-permute-done((f32[32,1280]{1,0:T(8,128)S(1)}, f32[32,1280]{1,0:T(8,128)S(1)}, u32[]{:S(2)}, u32[]{:S(2)}) %collective-permute-start.2) | collective-permute-done | bytes 163872 | tf_op jit(solution)/shard_map/ppermute | solution.py:163
  28.0 1.3 %collective-permute-start.5 = (f32[42,1280]{1,0:T(8,128)S(1)}, f32[42,1280]{1,0:T(8,128)S(1)}, u32[]{:S(2)}, u32[]{:S(2)}) collective-permute-start(f32[42,1280]{1,0:T(8,128)S(1)} %pad_maximum_fusion.3), channel_id=1, source_target_pairs={{4,0},{8,4},{12,8},{5,1},{9,5},{13,9},{6,2},{10,6},{14,10},{7,3},{... | collective-permute-start | bytes 645128 | tf_op jit(solution)/shard_map/ppermute | solution.py:164
  29.4 0.7 pad_maximum_fusion.2
  30.1 5.2 %collective-permute-start.4 = (f32[42,1280]{1,0:T(8,128)}, f32[42,1280]{1,0:T(8,128)S(1)}, u32[]{:S(2)}, u32[]{:S(2)}) collective-permute-start(f32[42,1280]{1,0:T(8,128)} %pad_maximum_fusion.2), channel_id=1, source_target_pairs={{0,4},{4,8},{8,12},{1,5},{5,9},{9,13},{2,6},{6,10},{10,14},{3,7},{... | collective-permute-start | bytes 645128 | tf_op jit(solution)/shard_map/ppermute | solution.py:163
  35.2 0.9 %fusion.9.spread_ref = bf16[488,112]{1,0:T(8,128)(2,1)} fusion(s32[488]{0:T(512)S(1)} %fusion.29, pred[488]{0:T(512)(128)(4,1)S(1)} %compare_and_fusion), kind=kLoop, calls=%fused_computation.17 | loop fusion | flops 163968 | bytes 111752 | tf_op jit(solution)/shard_map/convert_element_type | solution.py:262
  36.1 1.2 %collective-permute-done.5 = f32[42,1280]{1,0:T(8,128)S(1)} collective-permute-done((f32[42,1280]{1,0:T(8,128)S(1)}, f32[42,1280]{1,0:T(8,128)S(1)}, u32[]{:S(2)}, u32[]{:S(2)}) %collective-permute-start.5) | collective-permute-done | bytes 215072 | tf_op jit(solution)/shard_map/ppermute | solution.py:164
  37.4 2.2 %collective-permute-done.4 = f32[42,1280]{1,0:T(8,128)S(1)} collective-permute-done((f32[42,1280]{1,0:T(8,128)}, f32[42,1280]{1,0:T(8,128)S(1)}, u32[]{:S(2)}, u32[]{:S(2)}) %collective-permute-start.4) | collective-permute-done | bytes 215072 | tf_op jit(solution)/shard_map/ppermute | solution.py:163
  41.0 4.2 %fusion = f32[1,10,10,10,64]{4,0,3,2,1:T(1,128)S(1)} fusion(bf16[1,12,12,12,64]{4,3,2,1,0:T(8,128)(2,1)S(1)} %fusion.6, bf16[64,3,3,3,64]{4,3,2,1,0:T(4,128)(2,1)S(1)} %reshape.166), kind=kOutput, calls=%fused_computation.3 | convolution fusion | flops 221184000 | bytes 698368 | tf_op jit(solution)/shard_map/conv_general_dilated | solution.py:129
  46.2 0.7 pad.29.hid_ref
  48.0 1.5 %pad.30.clone = f32[18,24,1280]{2,1,0:T(8,128)} pad(f32[18,18,1280]{2,1,0:T(8,128)S(1)} %copy.34, f32[]{:T(128)} %constant.55.clone.1), padding=0_0x0_6x0_0 | pad | bytes 3870724 | tf_op jit(solution)/shard_map/jit(_pad)/pad | solution.py:255
  49.5 21.1 %shard_map.83 = bf16[384,1024]{1,0:T(8,128)(2,1)} custom-call(bf16[112,640]{1,0:T(8,128)(2,1)} %pad.29.hid_ref, bf16[488,112]{1,0:T(8,128)(2,1)} %fusion.9.spread_ref, f32[432,1280]{1,0:T(8,128)} %bitcast.40, f32[384,1024]{1,0:T(8,128)} %bitcast.41, bf16[64,1792]{1,0:T(8,128)(2,1)} %pad.32.wa_raw, bf16[64,1792]{1,0:T(8,128)(2,1)} %pad.33.wb_raw), custom_call_target="tpu_custom_call" | custom-call | tf_op jit(solution)/shard_map/pallas_call | solution.py:114
  70.6 1.9 %slice.127 = bf16[16,16,1024]{2,1,0:T(8,128)(2,1)} slice(bf16[16,24,1024]{2,1,0:T(8,128)(2,1)} %bitcast.42), slice={[0:16], [0:16], [0:1024]} | slice | bytes 1048576 | tf_op jit(solution)/shard_map/slice | solution.py:269
  (77 shorter events, 6.4 us)
Async XLA Ops:
  0.0 7.8 %copy-start.8 = (s32[8,4,16]{2,1,0:T(4,128)S(1)}, s32[8,4,16]{2,1,0:T(4,128)}, u32[]{:S(2)}) copy-start(s32[8,4,16]{2,1,0:T(4,128)} %param.9) | copy-start | bytes 6148
  0.0 7.9 %copy-start.7 = (bf16[8,4,1024]{2,1,0:T(4,128)(2,1)S(1)}, bf16[8,4,1024]{2,1,0:T(4,128)(2,1)}, u32[]{:S(2)}) copy-start(bf16[8,4,1024]{2,1,0:T(4,128)(2,1)} %param.8) | copy-start | bytes 196612
  0.0 8.8 %copy-start.3 = (bf16[64,1728]{1,0:T(8,128)(2,1)S(1)}, bf16[64,1728]{1,0:T(8,128)(2,1)}, u32[]{:S(2)}) copy-start(bf16[64,1728]{1,0:T(8,128)(2,1)} %param.12) | copy-start | bytes 663556
  0.0 9.2 %copy-start.4 = (bf16[64,1728]{1,0:T(8,128)(2,1)S(1)}, bf16[64,1728]{1,0:T(8,128)(2,1)}, u32[]{:S(2)}) copy-start(bf16[64,1728]{1,0:T(8,128)(2,1)} %param.13) | copy-start | bytes 663556
  4.7 6.9 %copy-start = (f32[256,1024]{1,0:T(8,128)S(1)}, f32[256,1024]{1,0:T(8,128)}, u32[]{:S(2)}) copy-start(f32[256,1024]{1,0:T(8,128)} %get-tuple-element.8) | copy-start | bytes 3145732
  7.4 5.5 %collective-permute-start.1 = (f32[16,16,64]{2,0,1:T(8,128)}, f32[16,16,64]{2,0,1:T(8,128)S(1)}, u32[]{:S(2)}, u32[]{:S(2)}) collective-permute-start(f32[16,16,64]{2,0,1:T(8,128)} %slice_select_fusion), channel_id=1, source_target_pairs={{0,1},{1,0},{2,3},{3,2},{4,5},{5,4},{6,7},{7,6},{8,9},{9,8},{10,11... | collective-permute-start | bytes 196616 | tf_op jit(solution)/shard_map/ppermute | solution.py:228
  8.0 5.7 %collective-permute-start = (bf16[8,4,1280]{2,1,0:T(4,128)(2,1)S(1)}, bf16[8,4,1280]{2,1,0:T(4,128)(2,1)}, u32[]{:S(2)}, u32[]{:S(2)}) collective-permute-start(bf16[8,4,1280]{2,1,0:T(4,128)(2,1)S(1)} %concatenate.39), channel_id=1, source_target_pairs={{0,1},{1,0},{2,3},{3,2},{4,5},{5,4},{6,7},{7,6},{8,9},{9,8},{10,11... | collective-permute-start | bytes 245768 | tf_op jit(solution)/shard_map/ppermute | solution.py:204
  17.8 8.6 %collective-permute-start.3 = (f32[32,1280]{1,0:T(8,128)S(1)}, f32[32,1280]{1,0:T(8,128)S(1)}, u32[]{:S(2)}, u32[]{:S(2)}) collective-permute-start(f32[32,1280]{1,0:T(8,128)S(1)} %pad_maximum_fusion.5), channel_id=1, source_target_pairs={{2,0},{3,1},{6,4},{7,5},{10,8},{11,9},{14,12},{15,13},{18,16},{19,... | collective-permute-start | bytes 491528 | tf_op jit(solution)/shard_map/ppermute | solution.py:164
  19.2 8.5 %collective-permute-start.2 = (f32[32,1280]{1,0:T(8,128)S(1)}, f32[32,1280]{1,0:T(8,128)S(1)}, u32[]{:S(2)}, u32[]{:S(2)}) collective-permute-start(f32[32,1280]{1,0:T(8,128)S(1)} %pad_maximum_fusion.4), channel_id=1, source_target_pairs={{0,2},{1,3},{4,6},{5,7},{8,10},{9,11},{12,14},{13,15},{16,18},{17,... | collective-permute-start | bytes 491528 | tf_op jit(solution)/shard_map/ppermute | solution.py:163
  28.0 9.3 %collective-permute-start.5 = (f32[42,1280]{1,0:T(8,128)S(1)}, f32[42,1280]{1,0:T(8,128)S(1)}, u32[]{:S(2)}, u32[]{:S(2)}) collective-permute-start(f32[42,1280]{1,0:T(8,128)S(1)} %pad_maximum_fusion.3), channel_id=1, source_target_pairs={{4,0},{8,4},{12,8},{5,1},{9,5},{13,9},{6,2},{10,6},{14,10},{7,3},{... | collective-permute-start | bytes 645128 | tf_op jit(solution)/shard_map/ppermute | solution.py:164
  30.1 9.5 %collective-permute-start.4 = (f32[42,1280]{1,0:T(8,128)}, f32[42,1280]{1,0:T(8,128)S(1)}, u32[]{:S(2)}, u32[]{:S(2)}) collective-permute-start(f32[42,1280]{1,0:T(8,128)} %pad_maximum_fusion.2), channel_id=1, source_target_pairs={{0,4},{4,8},{8,12},{1,5},{5,9},{9,13},{2,6},{6,10},{10,14},{3,7},{... | collective-permute-start | bytes 645128 | tf_op jit(solution)/shard_map/ppermute | solution.py:163
  37.3 2.5 %copy-start.1 = (f32[42,1280]{1,0:T(8,128)}, f32[42,1280]{1,0:T(8,128)S(1)}, u32[]{:S(2)}) copy-start(f32[42,1280]{1,0:T(8,128)S(1)} %collective-permute-done.5) | copy-start | bytes 645124
  39.6 0.7 copy-start.2
  41.0 4.3 %copy-start.5 = (pred[12,12,20]{2,1,0:T(8,128)(4,1)S(1)}, pred[12,12,20]{2,1,0:T(8,128)(4,1)}, u32[]{:S(2)}) copy-start(pred[12,12,20]{2,1,0:T(8,128)(4,1)} %get-tuple-element.19) | copy-start | bytes 8644
  41.0 4.3 %copy-start.6 = (pred[12,12,20]{2,1,0:T(8,128)(4,1)S(1)}, pred[12,12,20]{2,1,0:T(8,128)(4,1)}, u32[]{:S(2)}) copy-start(pred[12,12,20]{2,1,0:T(8,128)(4,1)} %get-tuple-element.20) | copy-start | bytes 8644
  45.3 1.7 %slice-start = ((f32[42,1280]{1,0:T(8,128)}), f32[18,1280]{1,0:T(8,128)S(1)}, s32[]{:S(2)}) async-start(f32[42,1280]{1,0:T(8,128)} %copy-done.1), calls=%async_computation | async-start | bytes 245760 | tf_op jit(solution)/shard_map/slice | solution.py:161
  45.3 1.7 %slice-start.1 = ((f32[42,1280]{1,0:T(8,128)}), f32[18,1280]{1,0:T(8,128)S(1)}, s32[]{:S(2)}) async-start(f32[42,1280]{1,0:T(8,128)} %copy-done.2), calls=%async_computation.1 | async-start | bytes 245760 | tf_op jit(solution)/shard_map/slice | solution.py:161

commit v4 on v3

--- a/solution.py
+++ b/solution.py
@@ -71,11 +71,22 @@
     return v / (1.0 + jnp.exp(-v))
 
 
-def fine_kernel(
-    hid_ref, spread_ref, ga_ref, gb_ref, wa_raw, wb_raw, out_ref, fin_ref, lvl_ref, wa_ref, wb_ref
-):
+def band_kernel(wa_raw, wb_raw, wa_ref, wb_ref):
     build_bands(wa_raw, wa_ref)
     build_bands(wb_raw, wb_ref)
+
+
+def band_stage(weight_a, weight_b):
+    shape = jax.ShapeDtypeStruct((9, 384, 256), jnp.bfloat16)
+    flops = 2 * 27 * 2 * (64 * 128 * 256 + 384 * 64 * 256)
+    return pl.pallas_call(
+        band_kernel,
+        out_shape=(shape, shape),
+        cost_estimate=pl.CostEstimate(flops=flops, transcendentals=0, bytes_accessed=4 * 9 * 384 * 256),
+    )(weight_a, weight_b)
+
+
+def fine_kernel(hid_ref, spread_ref, ga_ref, gb_ref, wa_ref, wb_ref, out_ref, fin_ref, lvl_ref):
     wide_c = hid_ref.shape[1]
     i = lax.broadcasted_iota(jnp.int32, (wide_c, LANES_F), 0)
     j = lax.broadcasted_iota(jnp.int32, (wide_c, LANES_F), 1)
@@ -107,18 +118,20 @@
     for k in range(LANES_B // 256):
         centre, acc = conv(lvl_ref, wb_ref, ROWS_B, k)
         lanes = slice(256 * k, 256 * k + 256)
-        out_ref[:, lanes] = (centre + silu(acc) * gb_ref[:, lanes]).astype(out_ref.dtype)
+        edge = out_ref.shape[0] // 16
+        for x in range(edge):
+            mine = slice(x * STRIDE, x * STRIDE + 16)
+            value = centre[mine] + silu(acc[mine]) * gb_ref[16 * x : 16 * x + 16, lanes]
+            out_ref[16 * x : 16 * x + 16, lanes] = value.astype(out_ref.dtype)
 
 
 def fine_stage(hid, spread, gate_a, gate_b, band_a, band_b):
     return pl.pallas_call(
         fine_kernel,
-        out_shape=jax.ShapeDtypeStruct((ROWS_B, LANES_B), jnp.bfloat16),
+        out_shape=jax.ShapeDtypeStruct(gate_b.shape, jnp.bfloat16),
         scratch_shapes=[
             pltpu.VMEM((ROWS_F, LANES_F), jnp.float32),
             pltpu.VMEM((ROWS_L, LANES_A), jnp.float32),
-            pltpu.VMEM((9, 384, 256), jnp.bfloat16),
-            pltpu.VMEM((9, 384, 256), jnp.bfloat16),
         ],
     )(hid, spread, gate_a, gate_b, band_a, band_b)
 
@@ -222,7 +235,6 @@
     live_row = jnp.broadcast_to(live.astype(jnp.float32), (1, 128))
     gate_a, gate_b = gate_stage(field.reshape(edge * edge, -1), mod_weight, live_row)
     gate_a = gate_a.reshape(field.shape)
-    gate_b = gate_b.reshape(field.shape)
     width = edge * channels
     face = jnp.where(first, gate_a[:, :, width - channels :], gate_a[:, :, :channels])
     face = lax.ppermute(face, "gz", [(0, 1), (1, 0)])
@@ -253,7 +265,6 @@
     hid = jnp.pad(hidden.reshape(cells, -1), ((0, ROWS_C - cells), (0, 0)))
 
     gate_a = jnp.pad(gate_a, ((0, 0), (0, STRIDE - edge - 2), (0, 0))).reshape(-1, gate_a.shape[2])
-    gate_b = jnp.pad(gate_b, ((0, 0), (0, STRIDE - edge), (0, 0))).reshape(-1, width)
 
     rows = jnp.arange(ROWS_F)
     fx, fy = rows // STRIDE, rows % STRIDE
@@ -263,10 +274,9 @@
         jnp.bfloat16
     )
     wide = ((0, 0), (0, 1792 - fine_weight_a.shape[1]))
-    out = fine_stage(
-        hid, spread, gate_a, gate_b, jnp.pad(fine_weight_a, wide), jnp.pad(fine_weight_b, wide)
-    )
-    return out.reshape(edge, STRIDE, width)[:, :edge]
+    band_a, band_b = band_stage(jnp.pad(fine_weight_a, wide), jnp.pad(fine_weight_b, wide))
+    out = fine_stage(hid, spread, gate_a, gate_b, band_a, band_b)
+    return out.reshape(field.shape)
 
 
 def solution(mesh):

time: 73.3 us -> 69.1 us (0.943)
  local copies, waits for them, and re-layouts: 15.4 us -> 11.5 us
  waiting for transfers between devices: 7.04 us -> 3.64 us
  Pallas kernels: 24.5 us -> 27.7 us
    pallas_call x1 -> x2, Pallas kernels: 21.1 us -> 24.2 us  [the longest x1 15.3 us: fine_stage(): pl.pallas_call(fine_kernel, out_shape=jax.ShapeDtypeStruct(gate_b.shape,...]
    ppermute x2, waiting for transfers between devices: 3.47 us -> 1.08 us  [grow_both(): lax.ppermute(pack(cells_tail, gate_tail), axis, shift_pairs(count, True))]
    slice x1 -> x0, local copies, waits for them, and re-layouts: 1.88 us -> none  [body(): return out.reshape(edge, STRIDE, width)[:, :edge]]
    pad x1 -> x0, local copies, waits for them, and re-layouts: 1.32 us -> none  [body(): jnp.pad(gate_b, ((0, 0), (0, STRIDE - edge), (0, 0))).reshape(-1, width)]
    ppermute x2, waiting for transfers between devices: 3.57 us -> 2.55 us  [grow_both(): lax.ppermute(pack(cells_head, gate_head), axis, shift_pairs(count, False))]
    select_n x1, other arithmetic: 1.12 us -> 0.15 us  [body(): jnp.where(first, jnp.concatenate([mine, theirs], 1), jnp.concatenate([the...]
    pad x1, local copies, waits for them, and re-layouts: 1.64 us -> 0.69 us  [body(): jnp.pad(fine_weight_b, wide)]
    concatenate x1, other arithmetic: 0.3 us -> 1.19 us  [grow_both(): jnp.concatenate([low[1], gate, high[1]], axis=dim)]
  transfers between devices with their start and end apart: 6 -> 6, of which waited for: 4 -> 2; matrix products, arithmetic and copies ran while one was open for 10% -> 11% of each run, Pallas kernels for 0% -> 18%
where the time goes in v4:
time: 69.1 us; the launch traced here: 68.7 us
  Pallas kernels  27.7 us (40%)
  starting transfers between devices  13.5 us (20%)
  local copies, waits for them, and re-layouts  11.5 us (17%)
  other arithmetic  5.56 us (8%)
  matrix products  4.22 us (6%)
  waiting for transfers between devices  3.64 us (5%)
  between operations  2.58 us (4%)
    pallas_call x1, Pallas kernels, fine_stage(): pl.pallas_call(fine_kernel, out_shape=jax.ShapeDtypeStruct(gate_b.shape,...  15.3 us
    ppermute x2, starting transfers between devices, grow_both(): lax.ppermute(pack(cells_tail, gate_tail), axis, shift_pairs(count, True))  10.3 us
    pallas_call x1, Pallas kernels, band_stage(): pl.pallas_call(band_kernel, out_shape=(shape, shape), cost_estimate=pl.Co...  8.94 us
    conv_general_dilated x1, matrix products, convolve(): lax.conv_general_dilated(padded[None], kernel, (1, 1, 1), 'VALID', dimens...  4.22 us
    pallas_call x1, Pallas kernels, gate_stage(): pl.pallas_call(gate_kernel, out_shape=(shape, shape))  3.44 us
    ppermute x2, starting transfers between devices, grow_both(): lax.ppermute(pack(cells_head, gate_head), axis, shift_pairs(count, False))  2.58 us
    ppermute x2, waiting for transfers between devices, grow_both(): lax.ppermute(pack(cells_head, gate_head), axis, shift_pairs(count, False))  2.55 us
    reshape x1, local copies, waits for them, and re-layouts, body(): gate_a = gate_a.reshape(field.shape)  1.84 us
  transfers between devices with their start and end apart: 6, of which 2 were waited for; matrix products, arithmetic and copies ran while one was open for 11% of the time, Pallas kernels for 18%

profile of v4, /device:TPU:0, one launch (start us, length us, event | category | flops | bytes accessed | tf_op | source)
XLA Modules:
  0.0 68.7 jit_solution(17393141012542915304)
XLA Ops:
  0.7 0.7 %convert_element_type.60 = bf16[8,4,16]{2,1,0:T(4,128)(2,1)S(1)} convert(s32[8,4,16]{2,1,0:T(4,128)} %param.9) | non-fusion elementwise | flops 512 | bytes 3072 | tf_op jit(solution)/shard_map/convert_element_type | solution.py:210
  1.5 1.0 %concatenate.39 = bf16[8,4,1280]{2,1,0:T(4,128)(2,1)S(1)} concatenate(bf16[8,4,1024]{2,1,0:T(4,128)(2,1)} %param.8, bf16[8,4,16]{2,1,0:T(4,128)(2,1)S(1)} %convert_element_type.60, bf16[8,4,1]{2,1,0:T(4,128)(2,1)S(1)} %broadcast_in_dim.33, bf16[8,4,239]{2,1,0:T(4,128)(2,1)S(1)} %broadcast_in_dim.34), dimensions={2} | concatenate | bytes 163840 | tf_op jit(solution)/shard_map/concatenate | solution.py:216
  3.5 3.4 %shard_map.82 = (f32[256,1024]{1,0:T(8,128)}, f32[256,1024]{1,0:T(8,128)}) custom-call(bf16[256,1024]{1,0:T(8,128)(2,1)} %bitcast.40, bf16[64,128]{1,0:T(8,128)(2,1)} %mw_ref.1, f32[1,128]{1,0:T(1,128)} %broadcast_in_dim.39.live_ref), custom_call_target="tpu_custom_call" | custom-call | tf_op jit(solution)/shard_map/pallas_call | solution.py:67
  6.9 1.8 %copy.23 = f32[16,16,1024]{2,0,1:T(8,128)S(1)} copy(f32[16,16,1024]{2,1,0:T(8,128)} %bitcast.39) | data formatting | bytes 2097152 | tf_op jit(solution)/shard_map/reshape | solution.py:237
  9.0 0.6 iota_compare_fusion.1
  9.7 0.7 %pad.27.wa_raw = bf16[64,1792]{1,0:T(8,128)(2,1)} pad(bf16[64,1728]{1,0:T(8,128)(2,1)S(1)} %copy-done.1, bf16[]{:T(256)} %constant.53.clone.1), padding=0_0x0_64 | pad | bytes 450562 | tf_op jit(solution)/shard_map/jit(_pad)/pad | solution.py:277
  10.4 0.7 %pad.28.wb_raw = bf16[64,1792]{1,0:T(8,128)(2,1)} pad(bf16[64,1728]{1,0:T(8,128)(2,1)S(1)} %copy-done.2, bf16[]{:T(256)} %constant.53.clone.1), padding=0_0x0_64 | pad | bytes 450562 | tf_op jit(solution)/shard_map/jit(_pad)/pad | solution.py:277
  11.5 0.8 %concatenate.43 = f32[16,16,1280]{2,0,1:T(8,128)S(1)} concatenate(f32[16,16,64]{2,0,1:T(8,128)S(1)} %get-tuple-element.22, f32[16,16,1024]{2,0,1:T(8,128)S(1)} %copy.23, f32[16,16,64]{2,0,1:T(8,128)S(1)} %get-tuple-element.21, f32[16,16,128]{2,0,1:T(8,128)S(1)} %broadcast_in_dim.40), dimensions={2} | concatenate | bytes 2621440 | tf_op jit(solution)/shard_map/concatenate | solution.py:242
  12.3 0.7 slice.106
  14.9 1.3 %collective-permute-start.3 = (f32[32,1280]{1,0:T(8,128)S(1)}, f32[32,1280]{1,0:T(8,128)S(1)}, u32[]{:S(2)}, u32[]{:S(2)}) collective-permute-start(f32[32,1280]{1,0:T(8,128)S(1)} %pad_maximum_fusion.5), channel_id=1, source_target_pairs={{2,0},{3,1},{6,4},{7,5},{10,8},{11,9},{14,12},{15,13},{18,16},{19,... | collective-permute-start | bytes 491528 | tf_op jit(solution)/shard_map/ppermute | solution.py:177
  16.2 4.9 %collective-permute-start.2 = (f32[32,1280]{1,0:T(8,128)S(1)}, f32[32,1280]{1,0:T(8,128)S(1)}, u32[]{:S(2)}, u32[]{:S(2)}) collective-permute-start(f32[32,1280]{1,0:T(8,128)S(1)} %pad_maximum_fusion.4), channel_id=1, source_target_pairs={{0,2},{1,3},{4,6},{5,7},{8,10},{9,11},{12,14},{13,15},{16,18},{17,... | collective-permute-start | bytes 491528 | tf_op jit(solution)/shard_map/ppermute | solution.py:176
  21.1 8.9 %shard_map.83 = (bf16[9,384,256]{2,1,0:T(8,128)(2,1)}, bf16[9,384,256]{2,1,0:T(8,128)(2,1)}) custom-call(bf16[64,1792]{1,0:T(8,128)(2,1)} %pad.27.wa_raw, bf16[64,1792]{1,0:T(8,128)(2,1)} %pad.28.wb_raw), custom_call_target="tpu_custom_call" | custom-call | flops 905969664 | bytes 3538944 | tf_op jit(solution)/shard_map/pallas_call | solution.py:82
  30.0 0.6 iota_add_fusion
  31.1 1.3 %collective-permute-start.5 = (f32[42,1280]{1,0:T(8,128)S(1)}, f32[42,1280]{1,0:T(8,128)S(1)}, u32[]{:S(2)}, u32[]{:S(2)}) collective-permute-start(f32[42,1280]{1,0:T(8,128)S(1)} %pad_maximum_fusion.3), channel_id=1, source_target_pairs={{4,0},{8,4},{12,8},{5,1},{9,5},{13,9},{6,2},{10,6},{14,10},{7,3},{... | collective-permute-start | bytes 645128 | tf_op jit(solution)/shard_map/ppermute | solution.py:177
  32.5 5.5 %collective-permute-start.4 = (f32[42,1280]{1,0:T(8,128)S(1)}, f32[42,1280]{1,0:T(8,128)S(1)}, u32[]{:S(2)}, u32[]{:S(2)}) collective-permute-start(f32[42,1280]{1,0:T(8,128)S(1)} %pad_maximum_fusion.2), channel_id=1, source_target_pairs={{0,4},{4,8},{8,12},{1,5},{5,9},{9,13},{2,6},{6,10},{10,14},{3,7},{... | collective-permute-start | bytes 645128 | tf_op jit(solution)/shard_map/ppermute | solution.py:176
  37.9 0.9 %fusion.9.spread_ref = bf16[488,112]{1,0:T(8,128)(2,1)} fusion(s32[488]{0:T(512)S(1)} %fusion.29, pred[488]{0:T(512)(128)(4,1)S(1)} %compare_and_fusion), kind=kLoop, calls=%fused_computation.17 | loop fusion | flops 163968 | bytes 111752 | tf_op jit(solution)/shard_map/convert_element_type | solution.py:273
  38.8 2.5 %collective-permute-done.5 = f32[42,1280]{1,0:T(8,128)S(1)} collective-permute-done((f32[42,1280]{1,0:T(8,128)S(1)}, f32[42,1280]{1,0:T(8,128)S(1)}, u32[]{:S(2)}, u32[]{:S(2)}) %collective-permute-start.5) | collective-permute-done | bytes 215072 | tf_op jit(solution)/shard_map/ppermute | solution.py:177
  41.5 1.1 %collective-permute-done.4 = f32[42,1280]{1,0:T(8,128)S(1)} collective-permute-done((f32[42,1280]{1,0:T(8,128)S(1)}, f32[42,1280]{1,0:T(8,128)S(1)}, u32[]{:S(2)}, u32[]{:S(2)}) %collective-permute-start.4) | collective-permute-done | bytes 215072 | tf_op jit(solution)/shard_map/ppermute | solution.py:176
  42.6 0.7 %reshape.162 = f32[1,18,1280]{2,0,1:T(1,128)} reshape(f32[18,1280]{1,0:T(8,128)S(1)} %slice.121) | data formatting | bytes 184320 | tf_op jit(solution)/shard_map/reshape | solution.py:174
  43.9 1.2 %pad_maximum_fusion = f32[18,18,1280]{2,0,1:T(8,128)S(1)} fusion(f32[1,18,1280]{2,0,1:T(1,128)S(1)} %reshape.163, f32[16,1,1280]{2,0,1:T(8,128)S(1)} %slice_bitcast_fusion, f32[16,16,1280]{2,0,1:T(8,128)S(1)} %concatenate.43, f32[16,1,1280]{2,0,1:T(8,128)S(1)} %slice_bitcast_fusion.1, f32[1,18,1280]{2,0,1:T(1,128)} %reshape.162), kind=kLoop, calls=%fused_computation | loop fusion | flops 1658880 | bytes 3317760 | tf_op jit(solution)/shard_map/concatenate | solution.py:180
  45.7 1.5 %pad.26.clone = f32[18,24,1280]{2,1,0:T(8,128)} pad(f32[18,18,1280]{2,1,0:T(8,128)S(1)} %copy.34, f32[]{:T(128)} %constant.55.clone.1), padding=0_0x0_6x0_0 | pad | bytes 3870724 | tf_op jit(solution)/shard_map/jit(_pad)/pad | solution.py:267
  47.5 4.2 %fusion = f32[1,10,10,10,64]{4,0,3,2,1:T(1,128)S(1)} fusion(bf16[1,12,12,12,64]{4,3,2,1,0:T(8,128)(2,1)S(1)} %fusion.6, bf16[64,3,3,3,64]{4,3,2,1,0:T(4,128)(2,1)S(1)} %reshape.160), kind=kOutput, calls=%fused_computation.3 | convolution fusion | flops 221184000 | bytes 698368 | tf_op jit(solution)/shard_map/conv_general_dilated | solution.py:142
  52.7 0.7 pad.25.hid_ref
  53.4 15.3 %shard_map.84 = bf16[256,1024]{1,0:T(8,128)(2,1)} custom-call(bf16[112,640]{1,0:T(8,128)(2,1)} %pad.25.hid_ref, bf16[488,112]{1,0:T(8,128)(2,1)} %fusion.9.spread_ref, f32[432,1280]{1,0:T(8,128)} %bitcast.38, f32[256,1024]{1,0:T(8,128)} %get-tuple-element.10.gb_ref, bf16[9,384,256]{2,1,0:T(8,128)(2,1)} %get-tuple-element.11.wa_ref, ...), custom_call_target="tpu_custom_call" | custom-call | tf_op jit(solution)/shard_map/pallas_call | solution.py:129
  (68 shorter events, 5.1 us)
Async XLA Ops:
  0.0 9.7 %copy-start.1 = (bf16[64,1728]{1,0:T(8,128)(2,1)S(1)}, bf16[64,1728]{1,0:T(8,128)(2,1)}, u32[]{:S(2)}) copy-start(bf16[64,1728]{1,0:T(8,128)(2,1)} %param.13) | copy-start | bytes 663556
  0.0 10.4 %copy-start.2 = (bf16[64,1728]{1,0:T(8,128)(2,1)S(1)}, bf16[64,1728]{1,0:T(8,128)(2,1)}, u32[]{:S(2)}) copy-start(bf16[64,1728]{1,0:T(8,128)(2,1)} %param.14) | copy-start | bytes 663556
  0.0 11.1 %copy-start.3 = (bf16[64,1728]{1,0:T(8,128)(2,1)S(1)}, bf16[64,1728]{1,0:T(8,128)(2,1)}, u32[]{:S(2)}) copy-start(bf16[64,1728]{1,0:T(8,128)(2,1)} %param.12) | copy-start | bytes 663556
  2.4 9.9 %collective-permute-start = (bf16[8,4,1280]{2,1,0:T(4,128)(2,1)S(1)}, bf16[8,4,1280]{2,1,0:T(4,128)(2,1)S(1)}, u32[]{:S(2)}, u32[]{:S(2)}) collective-permute-start(bf16[8,4,1280]{2,1,0:T(4,128)(2,1)S(1)} %concatenate.39), channel_id=1, source_target_pairs={{0,1},{1,0},{2,3},{3,2},{4,5},{5,4},{6,7},{7,6},{8,9},{9,8},{10,11... | collective-permute-start | bytes 245768 | tf_op jit(solution)/shard_map/ppermute | solution.py:217
  8.9 2.5 %collective-permute-start.1 = (f32[16,16,64]{2,0,1:T(8,128)S(1)}, f32[16,16,64]{2,0,1:T(8,128)S(1)}, u32[]{:S(2)}, u32[]{:S(2)}) collective-permute-start(f32[16,16,64]{2,0,1:T(8,128)S(1)} %slice_select_fusion), channel_id=1, source_target_pairs={{0,1},{1,0},{2,3},{3,2},{4,5},{5,4},{6,7},{7,6},{8,9},{9,8},{10,11... | collective-permute-start | bytes 196616 | tf_op jit(solution)/shard_map/ppermute | solution.py:240
  14.9 15.8 %collective-permute-start.3 = (f32[32,1280]{1,0:T(8,128)S(1)}, f32[32,1280]{1,0:T(8,128)S(1)}, u32[]{:S(2)}, u32[]{:S(2)}) collective-permute-start(f32[32,1280]{1,0:T(8,128)S(1)} %pad_maximum_fusion.5), channel_id=1, source_target_pairs={{2,0},{3,1},{6,4},{7,5},{10,8},{11,9},{14,12},{15,13},{18,16},{19,... | collective-permute-start | bytes 491528 | tf_op jit(solution)/shard_map/ppermute | solution.py:177
  16.2 14.5 %collective-permute-start.2 = (f32[32,1280]{1,0:T(8,128)S(1)}, f32[32,1280]{1,0:T(8,128)S(1)}, u32[]{:S(2)}, u32[]{:S(2)}) collective-permute-start(f32[32,1280]{1,0:T(8,128)S(1)} %pad_maximum_fusion.4), channel_id=1, source_target_pairs={{0,2},{1,3},{4,6},{5,7},{8,10},{9,11},{12,14},{13,15},{16,18},{17,... | collective-permute-start | bytes 491528 | tf_op jit(solution)/shard_map/ppermute | solution.py:176
  31.1 10.2 %collective-permute-start.5 = (f32[42,1280]{1,0:T(8,128)S(1)}, f32[42,1280]{1,0:T(8,128)S(1)}, u32[]{:S(2)}, u32[]{:S(2)}) collective-permute-start(f32[42,1280]{1,0:T(8,128)S(1)} %pad_maximum_fusion.3), channel_id=1, source_target_pairs={{4,0},{8,4},{12,8},{5,1},{9,5},{13,9},{6,2},{10,6},{14,10},{7,3},{... | collective-permute-start | bytes 645128 | tf_op jit(solution)/shard_map/ppermute | solution.py:177
  32.5 10.1 %collective-permute-start.4 = (f32[42,1280]{1,0:T(8,128)S(1)}, f32[42,1280]{1,0:T(8,128)S(1)}, u32[]{:S(2)}, u32[]{:S(2)}) collective-permute-start(f32[42,1280]{1,0:T(8,128)S(1)} %pad_maximum_fusion.2), channel_id=1, source_target_pairs={{0,4},{4,8},{8,12},{1,5},{5,9},{9,13},{2,6},{6,10},{10,14},{3,7},{... | collective-permute-start | bytes 645128 | tf_op jit(solution)/shard_map/ppermute | solution.py:176
  47.5 4.3 %copy-start = (s32[12,12,10]{2,1,0:T(8,128)S(1)}, s32[12,12,10]{2,1,0:T(8,128)}, u32[]{:S(2)}) copy-start(s32[12,12,10]{2,1,0:T(8,128)} %iota_add_fusion) | copy-start | bytes 17284
  47.5 4.3 %copy-start.4 = (pred[12,12,20]{2,1,0:T(8,128)(4,1)S(1)}, pred[12,12,20]{2,1,0:T(8,128)(4,1)}, u32[]{:S(2)}) copy-start(pred[12,12,20]{2,1,0:T(8,128)(4,1)} %get-tuple-element.23) | copy-start | bytes 8644
  47.5 4.3 %copy-start.5 = (pred[12,12,20]{2,1,0:T(8,128)(4,1)S(1)}, pred[12,12,20]{2,1,0:T(8,128)(4,1)}, u32[]{:S(2)}) copy-start(pred[12,12,20]{2,1,0:T(8,128)(4,1)} %get-tuple-element.24) | copy-start | bytes 8644

commit v5 on v4

--- a/solution.py
+++ b/solution.py
@@ -25,23 +25,24 @@
 
 
 def build_bands(w_ref, band_ref):
-    rows_all = select((384, 64), lambda r, c: (r & 63) == c).astype(jnp.bfloat16)
     halves = [
         select((128, 256), lambda r, c, h=h: ((r >> 6) == h) & ((r & 63) == (c & 63))).astype(
             jnp.bfloat16
         )
         for h in range(2)
     ]
+    column = select((64, 256), lambda r, c: c >> 6)
     for t in range(9):
-        acc = jnp.zeros((384, 256), jnp.float32)
+        spreads = []
         for dz in range(3):
             d = 3 * t + dz
             block = w_ref[:, 128 * (d // 2) : 128 * (d // 2) + 128]
-            spread = jnp.dot(block, halves[d % 2], preferred_element_type=jnp.float32)
-            tall = jnp.dot(rows_all, spread.astype(jnp.bfloat16), preferred_element_type=jnp.float32)
-            keep = select((384, 256), lambda r, c, dz=dz: (r >> 6) - (c >> 6) == dz)
-            acc = acc + jnp.where(keep, tall, 0.0)
-        band_ref[t] = acc.astype(jnp.bfloat16)
+            spreads.append(jnp.dot(block, halves[d % 2], preferred_element_type=jnp.float32))
+        for zi in range(6):
+            part = jnp.zeros((64, 256), jnp.float32)
+            for dz in range(3):
+                part = jnp.where(column == zi - dz, spreads[dz], part)
+            band_ref[t, 64 * zi : 64 * zi + 64, :] = part.astype(jnp.bfloat16)
 
 
 def gate_kernel(field_ref, mw_ref, live_ref, ga_ref, gb_ref):

time: 69.1 us -> 64.1 us (0.928)
  Pallas kernels: 27.7 us -> 22.7 us
    pallas_call x1, Pallas kernels: 8.94 us -> 3.94 us  [band_stage(): pl.pallas_call(band_kernel, out_shape=(shape, shape), cost_estimate=pl.Co...]
  transfers between devices with their start and end apart: 6 -> 6, of which waited for: 2 -> 2; matrix products, arithmetic and copies ran while one was open for 11% -> 12% of each run, Pallas kernels for 18% -> 12%
where the time goes in v5:
time: 64.1 us; the launch traced here: 63.7 us
  Pallas kernels  22.7 us (35%)
  starting transfers between devices  13.5 us (21%)
  local copies, waits for them, and re-layouts  11.5 us (18%)
  other arithmetic  5.56 us (9%)
  matrix products  4.22 us (7%)
  waiting for transfers between devices  3.65 us (6%)
  between operations  2.58 us (4%)
    pallas_call x1, Pallas kernels, fine_stage(): pl.pallas_call(fine_kernel, out_shape=jax.ShapeDtypeStruct(gate_b.shape,...  15.3 us
    ppermute x2, starting transfers between devices, grow_both(): lax.ppermute(pack(cells_tail, gate_tail), axis, shift_pairs(count, True))  10.3 us
    conv_general_dilated x1, matrix products, convolve(): lax.conv_general_dilated(padded[None], kernel, (1, 1, 1), 'VALID', dimens...  4.22 us
    pallas_call x1, Pallas kernels, band_stage(): pl.pallas_call(band_kernel, out_shape=(shape, shape), cost_estimate=pl.Co...  3.94 us
    pallas_call x1, Pallas kernels, gate_stage(): pl.pallas_call(gate_kernel, out_shape=(shape, shape))  3.44 us
    ppermute x2, starting transfers between devices, grow_both(): lax.ppermute(pack(cells_head, gate_head), axis, shift_pairs(count, False))  2.58 us
    ppermute x2, waiting for transfers between devices, grow_both(): lax.ppermute(pack(cells_head, gate_head), axis, shift_pairs(count, False))  2.56 us
    reshape x1, local copies, waits for them, and re-layouts, body(): gate_a = gate_a.reshape(field.shape)  1.84 us
  transfers between devices with their start and end apart: 6, of which 2 were waited for; matrix products, arithmetic and copies ran while one was open for 12% of the time, Pallas kernels for 12%

profile of v5, /device:TPU:0, one launch (start us, length us, event | category | flops | bytes accessed | tf_op | source)
XLA Modules:
  0.0 63.7 jit_solution(13519351182677063479)
XLA Ops:
  0.7 0.7 %convert_element_type.60 = bf16[8,4,16]{2,1,0:T(4,128)(2,1)S(1)} convert(s32[8,4,16]{2,1,0:T(4,128)} %param.9) | non-fusion elementwise | flops 512 | bytes 3072 | tf_op jit(solution)/shard_map/convert_element_type | solution.py:211
  1.5 1.0 %concatenate.39 = bf16[8,4,1280]{2,1,0:T(4,128)(2,1)S(1)} concatenate(bf16[8,4,1024]{2,1,0:T(4,128)(2,1)} %param.8, bf16[8,4,16]{2,1,0:T(4,128)(2,1)S(1)} %convert_element_type.60, bf16[8,4,1]{2,1,0:T(4,128)(2,1)S(1)} %broadcast_in_dim.33, bf16[8,4,239]{2,1,0:T(4,128)(2,1)S(1)} %broadcast_in_dim.34), dimensions={2} | concatenate | bytes 163840 | tf_op jit(solution)/shard_map/concatenate | solution.py:217
  3.5 3.4 %shard_map.82 = (f32[256,1024]{1,0:T(8,128)}, f32[256,1024]{1,0:T(8,128)}) custom-call(bf16[256,1024]{1,0:T(8,128)(2,1)} %bitcast.40, bf16[64,128]{1,0:T(8,128)(2,1)} %mw_ref.1, f32[1,128]{1,0:T(1,128)} %broadcast_in_dim.39.live_ref), custom_call_target="tpu_custom_call" | custom-call | tf_op jit(solution)/shard_map/pallas_call | solution.py:68
  6.9 1.8 %copy.23 = f32[16,16,1024]{2,0,1:T(8,128)S(1)} copy(f32[16,16,1024]{2,1,0:T(8,128)} %bitcast.39) | data formatting | bytes 2097152 | tf_op jit(solution)/shard_map/reshape | solution.py:238
  9.0 0.6 iota_compare_fusion.1
  9.7 0.7 %pad.27.wa_raw = bf16[64,1792]{1,0:T(8,128)(2,1)} pad(bf16[64,1728]{1,0:T(8,128)(2,1)S(1)} %copy-done.1, bf16[]{:T(256)} %constant.53.clone.1), padding=0_0x0_64 | pad | bytes 450562 | tf_op jit(solution)/shard_map/jit(_pad)/pad | solution.py:278
  10.4 0.7 %pad.28.wb_raw = bf16[64,1792]{1,0:T(8,128)(2,1)} pad(bf16[64,1728]{1,0:T(8,128)(2,1)S(1)} %copy-done.2, bf16[]{:T(256)} %constant.53.clone.1), padding=0_0x0_64 | pad | bytes 450562 | tf_op jit(solution)/shard_map/jit(_pad)/pad | solution.py:278
  11.5 0.8 %concatenate.43 = f32[16,16,1280]{2,0,1:T(8,128)S(1)} concatenate(f32[16,16,64]{2,0,1:T(8,128)S(1)} %get-tuple-element.22, f32[16,16,1024]{2,0,1:T(8,128)S(1)} %copy.23, f32[16,16,64]{2,0,1:T(8,128)S(1)} %get-tuple-element.21, f32[16,16,128]{2,0,1:T(8,128)S(1)} %broadcast_in_dim.40), dimensions={2} | concatenate | bytes 2621440 | tf_op jit(solution)/shard_map/concatenate | solution.py:243
  12.3 0.7 %slice.106 = bf16[1,1,1]{2,1,0:T(2,128)(2,1)} slice(bf16[8,4,1280]{2,1,0:T(4,128)(2,1)S(1)} %collective-permute-done), slice={[0:1], [0:1], [1040:1041]} | slice | bytes 4 | tf_op jit(solution)/shard_map/slice | solution.py:220
  14.9 1.3 %collective-permute-start.3 = (f32[32,1280]{1,0:T(8,128)S(1)}, f32[32,1280]{1,0:T(8,128)S(1)}, u32[]{:S(2)}, u32[]{:S(2)}) collective-permute-start(f32[32,1280]{1,0:T(8,128)S(1)} %pad_maximum_fusion.5), channel_id=1, source_target_pairs={{2,0},{3,1},{6,4},{7,5},{10,8},{11,9},{14,12},{15,13},{18,16},{19,... | collective-permute-start | bytes 491528 | tf_op jit(solution)/shard_map/ppermute | solution.py:178
  16.2 4.9 %collective-permute-start.2 = (f32[32,1280]{1,0:T(8,128)S(1)}, f32[32,1280]{1,0:T(8,128)S(1)}, u32[]{:S(2)}, u32[]{:S(2)}) collective-permute-start(f32[32,1280]{1,0:T(8,128)S(1)} %pad_maximum_fusion.4), channel_id=1, source_target_pairs={{0,2},{1,3},{4,6},{5,7},{8,10},{9,11},{12,14},{13,15},{16,18},{17,... | collective-permute-start | bytes 491528 | tf_op jit(solution)/shard_map/ppermute | solution.py:177
  21.1 3.9 %shard_map.83 = (bf16[9,384,256]{2,1,0:T(8,128)(2,1)}, bf16[9,384,256]{2,1,0:T(8,128)(2,1)}) custom-call(bf16[64,1792]{1,0:T(8,128)(2,1)} %pad.27.wa_raw, bf16[64,1792]{1,0:T(8,128)(2,1)} %pad.28.wb_raw), custom_call_target="tpu_custom_call" | custom-call | flops 905969664 | bytes 3538944 | tf_op jit(solution)/shard_map/pallas_call | solution.py:83
  25.0 0.6 %iota_add_fusion = s32[12,12,10]{2,1,0:T(8,128)} fusion(s32[]{:T(128)S(6)} %select_n.96), kind=kLoop, calls=%fused_computation.30 | loop fusion | flops 1440 | bytes 5764 | tf_op jit(solution)/shard_map/dynamic_slice | solution.py:259
  26.1 1.3 %collective-permute-start.5 = (f32[42,1280]{1,0:T(8,128)S(1)}, f32[42,1280]{1,0:T(8,128)S(1)}, u32[]{:S(2)}, u32[]{:S(2)}) collective-permute-start(f32[42,1280]{1,0:T(8,128)S(1)} %pad_maximum_fusion.3), channel_id=1, source_target_pairs={{4,0},{8,4},{12,8},{5,1},{9,5},{13,9},{6,2},{10,6},{14,10},{7,3},{... | collective-permute-start | bytes 645128 | tf_op jit(solution)/shard_map/ppermute | solution.py:178
  27.5 5.4 %collective-permute-start.4 = (f32[42,1280]{1,0:T(8,128)S(1)}, f32[42,1280]{1,0:T(8,128)S(1)}, u32[]{:S(2)}, u32[]{:S(2)}) collective-permute-start(f32[42,1280]{1,0:T(8,128)S(1)} %pad_maximum_fusion.2), channel_id=1, source_target_pairs={{0,4},{4,8},{8,12},{1,5},{5,9},{9,13},{2,6},{6,10},{10,14},{3,7},{... | collective-permute-start | bytes 645128 | tf_op jit(solution)/shard_map/ppermute | solution.py:177
  32.9 0.9 %fusion.9.spread_ref = bf16[488,112]{1,0:T(8,128)(2,1)} fusion(s32[488]{0:T(512)S(1)} %fusion.29, pred[488]{0:T(512)(128)(4,1)S(1)} %compare_and_fusion), kind=kLoop, calls=%fused_computation.17 | loop fusion | flops 163968 | bytes 111752 | tf_op jit(solution)/shard_map/convert_element_type | solution.py:274
  33.8 2.6 %collective-permute-done.5 = f32[42,1280]{1,0:T(8,128)S(1)} collective-permute-done((f32[42,1280]{1,0:T(8,128)S(1)}, f32[42,1280]{1,0:T(8,128)S(1)}, u32[]{:S(2)}, u32[]{:S(2)}) %collective-permute-start.5) | collective-permute-done | bytes 215072 | tf_op jit(solution)/shard_map/ppermute | solution.py:178
  36.5 1.1 %collective-permute-done.4 = f32[42,1280]{1,0:T(8,128)S(1)} collective-permute-done((f32[42,1280]{1,0:T(8,128)S(1)}, f32[42,1280]{1,0:T(8,128)S(1)}, u32[]{:S(2)}, u32[]{:S(2)}) %collective-permute-start.4) | collective-permute-done | bytes 215072 | tf_op jit(solution)/shard_map/ppermute | solution.py:177
  37.6 0.7 %reshape.162 = f32[1,18,1280]{2,0,1:T(1,128)} reshape(f32[18,1280]{1,0:T(8,128)S(1)} %slice.121) | data formatting | bytes 184320 | tf_op jit(solution)/shard_map/reshape | solution.py:175
  38.9 1.2 %pad_maximum_fusion = f32[18,18,1280]{2,0,1:T(8,128)S(1)} fusion(f32[1,18,1280]{2,0,1:T(1,128)S(1)} %reshape.163, f32[16,1,1280]{2,0,1:T(8,128)S(1)} %slice_bitcast_fusion, f32[16,16,1280]{2,0,1:T(8,128)S(1)} %concatenate.43, f32[16,1,1280]{2,0,1:T(8,128)S(1)} %slice_bitcast_fusion.1, f32[1,18,1280]{2,0,1:T(1,128)} %reshape.162), kind=kLoop, calls=%fused_computation | loop fusion | flops 1658880 | bytes 3317760 | tf_op jit(solution)/shard_map/concatenate | solution.py:181
  40.7 1.5 %pad.26.clone = f32[18,24,1280]{2,1,0:T(8,128)} pad(f32[18,18,1280]{2,1,0:T(8,128)S(1)} %copy.34, f32[]{:T(128)} %constant.55.clone.1), padding=0_0x0_6x0_0 | pad | bytes 3870724 | tf_op jit(solution)/shard_map/jit(_pad)/pad | solution.py:268
  42.5 4.2 %fusion = f32[1,10,10,10,64]{4,0,3,2,1:T(1,128)S(1)} fusion(bf16[1,12,12,12,64]{4,3,2,1,0:T(8,128)(2,1)S(1)} %fusion.6, bf16[64,3,3,3,64]{4,3,2,1,0:T(4,128)(2,1)S(1)} %reshape.160), kind=kOutput, calls=%fused_computation.3 | convolution fusion | flops 221184000 | bytes 698368 | tf_op jit(solution)/shard_map/conv_general_dilated | solution.py:143
  47.7 0.7 %pad.25.hid_ref = bf16[112,640]{1,0:T(8,128)(2,1)} pad(bf16[100,640]{1,0:T(8,128)(2,1)S(1)} %reshape.161, bf16[]{:T(256)} %constant.53.clone.1), padding=0_12x0_0 | pad | bytes 271362 | tf_op jit(solution)/shard_map/jit(_pad)/pad | solution.py:266
  48.4 15.3 %shard_map.84 = bf16[256,1024]{1,0:T(8,128)(2,1)} custom-call(bf16[112,640]{1,0:T(8,128)(2,1)} %pad.25.hid_ref, bf16[488,112]{1,0:T(8,128)(2,1)} %fusion.9.spread_ref, f32[432,1280]{1,0:T(8,128)} %bitcast.38, f32[256,1024]{1,0:T(8,128)} %get-tuple-element.10.gb_ref, bf16[9,384,256]{2,1,0:T(8,128)(2,1)} %get-tuple-element.11.wa_ref, ...), custom_call_target="tpu_custom_call" | custom-call | tf_op jit(solution)/shard_map/pallas_call | solution.py:130
  (68 shorter events, 5.1 us)
Async XLA Ops:
  0.0 9.7 %copy-start.1 = (bf16[64,1728]{1,0:T(8,128)(2,1)S(1)}, bf16[64,1728]{1,0:T(8,128)(2,1)}, u32[]{:S(2)}) copy-start(bf16[64,1728]{1,0:T(8,128)(2,1)} %param.13) | copy-start | bytes 663556
  0.0 10.4 %copy-start.2 = (bf16[64,1728]{1,0:T(8,128)(2,1)S(1)}, bf16[64,1728]{1,0:T(8,128)(2,1)}, u32[]{:S(2)}) copy-start(bf16[64,1728]{1,0:T(8,128)(2,1)} %param.14) | copy-start | bytes 663556
  0.0 11.1 %copy-start.3 = (bf16[64,1728]{1,0:T(8,128)(2,1)S(1)}, bf16[64,1728]{1,0:T(8,128)(2,1)}, u32[]{:S(2)}) copy-start(bf16[64,1728]{1,0:T(8,128)(2,1)} %param.12) | copy-start | bytes 663556
  2.4 9.9 %collective-permute-start = (bf16[8,4,1280]{2,1,0:T(4,128)(2,1)S(1)}, bf16[8,4,1280]{2,1,0:T(4,128)(2,1)S(1)}, u32[]{:S(2)}, u32[]{:S(2)}) collective-permute-start(bf16[8,4,1280]{2,1,0:T(4,128)(2,1)S(1)} %concatenate.39), channel_id=1, source_target_pairs={{0,1},{1,0},{2,3},{3,2},{4,5},{5,4},{6,7},{7,6},{8,9},{9,8},{10,11... | collective-permute-start | bytes 245768 | tf_op jit(solution)/shard_map/ppermute | solution.py:218
  8.9 2.5 %collective-permute-start.1 = (f32[16,16,64]{2,0,1:T(8,128)S(1)}, f32[16,16,64]{2,0,1:T(8,128)S(1)}, u32[]{:S(2)}, u32[]{:S(2)}) collective-permute-start(f32[16,16,64]{2,0,1:T(8,128)S(1)} %slice_select_fusion), channel_id=1, source_target_pairs={{0,1},{1,0},{2,3},{3,2},{4,5},{5,4},{6,7},{7,6},{8,9},{9,8},{10,11... | collective-permute-start | bytes 196616 | tf_op jit(solution)/shard_map/ppermute | solution.py:241
  14.9 10.8 %collective-permute-start.3 = (f32[32,1280]{1,0:T(8,128)S(1)}, f32[32,1280]{1,0:T(8,128)S(1)}, u32[]{:S(2)}, u32[]{:S(2)}) collective-permute-start(f32[32,1280]{1,0:T(8,128)S(1)} %pad_maximum_fusion.5), channel_id=1, source_target_pairs={{2,0},{3,1},{6,4},{7,5},{10,8},{11,9},{14,12},{15,13},{18,16},{19,... | collective-permute-start | bytes 491528 | tf_op jit(solution)/shard_map/ppermute | solution.py:178
  16.2 9.5 %collective-permute-start.2 = (f32[32,1280]{1,0:T(8,128)S(1)}, f32[32,1280]{1,0:T(8,128)S(1)}, u32[]{:S(2)}, u32[]{:S(2)}) collective-permute-start(f32[32,1280]{1,0:T(8,128)S(1)} %pad_maximum_fusion.4), channel_id=1, source_target_pairs={{0,2},{1,3},{4,6},{5,7},{8,10},{9,11},{12,14},{13,15},{16,18},{17,... | collective-permute-start | bytes 491528 | tf_op jit(solution)/shard_map/ppermute | solution.py:177
  26.1 10.2 %collective-permute-start.5 = (f32[42,1280]{1,0:T(8,128)S(1)}, f32[42,1280]{1,0:T(8,128)S(1)}, u32[]{:S(2)}, u32[]{:S(2)}) collective-permute-start(f32[42,1280]{1,0:T(8,128)S(1)} %pad_maximum_fusion.3), channel_id=1, source_target_pairs={{4,0},{8,4},{12,8},{5,1},{9,5},{13,9},{6,2},{10,6},{14,10},{7,3},{... | collective-permute-start | bytes 645128 | tf_op jit(solution)/shard_map/ppermute | solution.py:178
  27.5 10.1 %collective-permute-start.4 = (f32[42,1280]{1,0:T(8,128)S(1)}, f32[42,1280]{1,0:T(8,128)S(1)}, u32[]{:S(2)}, u32[]{:S(2)}) collective-permute-start(f32[42,1280]{1,0:T(8,128)S(1)} %pad_maximum_fusion.2), channel_id=1, source_target_pairs={{0,4},{4,8},{8,12},{1,5},{5,9},{9,13},{2,6},{6,10},{10,14},{3,7},{... | collective-permute-start | bytes 645128 | tf_op jit(solution)/shard_map/ppermute | solution.py:177
  42.5 4.3 %copy-start = (s32[12,12,10]{2,1,0:T(8,128)S(1)}, s32[12,12,10]{2,1,0:T(8,128)}, u32[]{:S(2)}) copy-start(s32[12,12,10]{2,1,0:T(8,128)} %iota_add_fusion) | copy-start | bytes 17284
  42.5 4.3 %copy-start.4 = (pred[12,12,20]{2,1,0:T(8,128)(4,1)S(1)}, pred[12,12,20]{2,1,0:T(8,128)(4,1)}, u32[]{:S(2)}) copy-start(pred[12,12,20]{2,1,0:T(8,128)(4,1)} %get-tuple-element.23) | copy-start | bytes 8644
  42.5 4.3 %copy-start.5 = (pred[12,12,20]{2,1,0:T(8,128)(4,1)S(1)}, pred[12,12,20]{2,1,0:T(8,128)(4,1)}, u32[]{:S(2)}) copy-start(pred[12,12,20]{2,1,0:T(8,128)(4,1)} %get-tuple-element.24) | copy-start | bytes 8644

commit v6 on v5

--- a/solution.py
+++ b/solution.py
@@ -168,11 +168,11 @@
     (cells_head, cells_tail), (gate_head, gate_tail) = ends(cells, widths[0]), ends(gate, widths[1])
 
     def pack(c, g):
-        return jnp.concatenate([c.astype(jnp.float32).reshape(-1, lanes), g.reshape(-1, lanes)], 0)
+        return jnp.concatenate([c.reshape(-1, lanes), g.astype(c.dtype).reshape(-1, lanes)], 0)
 
     def unpack(m):
         split = cells_head.size // lanes
-        return m[:split].reshape(cells_head.shape).astype(cells.dtype), m[split:].reshape(gate_head.shape)
+        return m[:split].reshape(cells_head.shape), m[split:].reshape(gate_head.shape).astype(gate.dtype)
 
     low = unpack(lax.ppermute(pack(cells_tail, gate_tail), axis, shift_pairs(count, True)))
     high = unpack(lax.ppermute(pack(cells_head, gate_head), axis, shift_pairs(count, False)))
@@ -238,7 +238,7 @@
     gate_a = gate_a.reshape(field.shape)
     width = edge * channels
     face = jnp.where(first, gate_a[:, :, width - channels :], gate_a[:, :, :channels])
-    face = lax.ppermute(face, "gz", [(0, 1), (1, 0)])
+    face = lax.ppermute(face.astype(jnp.bfloat16), "gz", [(0, 1), (1, 0)]).astype(jnp.float32)
     blank = jnp.zeros_like(face)
     gate_a = jnp.concatenate(
         [

time: 64.1 us -> 65.3 us (1.019); the launches traced: 63.7 us -> 64.1 us
    ppermute x2, waiting for transfers between devices: 1.08 us -> 2.73 us  [grow_both(): lax.ppermute(pack(cells_tail, gate_tail), axis, shift_pairs(count, True))]
    ppermute x2, waiting for transfers between devices: 2.56 us -> 1.38 us  [grow_both(): lax.ppermute(pack(cells_head, gate_head), axis, shift_pairs(count, False))]
    reshape x9 -> x10, local copies, waits for them, and re-layouts: 0.94 us -> 0.18 us  [the longest x4 0.08 us: unpack(): m[:split].reshape(cells_head.shape)]
    convert_element_type x4 -> x2, local copies, waits for them, and re-layouts: 0.08 us -> 0.77 us  [unpack(): m[split:].reshape(gate_head.shape).astype(gate.dtype)]
    concatenate x1 -> x2, other arithmetic: 1.19 us -> 1.31 us  [grow_both(): jnp.concatenate([low[1], gate, high[1]], axis=dim)]
  transfers between devices with their start and end apart: 6 -> 6, of which waited for: 2 -> 4; matrix products, arithmetic and copies ran while one was open for 12% -> 12% of each run, Pallas kernels for 12% -> 11%
where the time goes in v6:
time: 65.3 us; the launch traced here: 64.1 us
  Pallas kernels  22.6 us (35%)
  starting transfers between devices  13.5 us (21%)
  local copies, waits for them, and re-layouts  11.6 us (18%)
  other arithmetic  5.55 us (8%)
  matrix products  4.22 us (6%)
  waiting for transfers between devices  4.11 us (6%)
  between operations  2.45 us (4%)
    pallas_call x1, Pallas kernels, fine_stage(): pl.pallas_call(fine_kernel, out_shape=jax.ShapeDtypeStruct(gate_b.shape,...  15.3 us
    ppermute x2, starting transfers between devices, grow_both(): lax.ppermute(pack(cells_tail, gate_tail), axis, shift_pairs(count, True))  10.3 us
    conv_general_dilated x1, matrix products, convolve(): lax.conv_general_dilated(padded[None], kernel, (1, 1, 1), 'VALID', dimens...  4.22 us
    pallas_call x1, Pallas kernels, band_stage(): pl.pallas_call(band_kernel, out_shape=(shape, shape), cost_estimate=pl.Co...  3.94 us
    pallas_call x1, Pallas kernels, gate_stage(): pl.pallas_call(gate_kernel, out_shape=(shape, shape))  3.43 us
    ppermute x2, waiting for transfers between devices, grow_both(): lax.ppermute(pack(cells_tail, gate_tail), axis, shift_pairs(count, True))  2.73 us
    ppermute x2, starting transfers between devices, grow_both(): lax.ppermute(pack(cells_head, gate_head), axis, shift_pairs(count, False))  2.58 us
    reshape x1, local copies, waits for them, and re-layouts, body(): gate_a = gate_a.reshape(field.shape)  1.84 us
  transfers between devices with their start and end apart: 6, of which 4 were waited for; matrix products, arithmetic and copies ran while one was open for 12% of the time, Pallas kernels for 11%

profile of v6, /device:TPU:0, one launch (start us, length us, event | category | flops | bytes accessed | tf_op | source)
XLA Modules:
  0.0 64.1 jit_solution(2774090877831516146)
XLA Ops:
  0.7 0.7 %convert_element_type.74 = bf16[8,4,16]{2,1,0:T(4,128)(2,1)S(1)} convert(s32[8,4,16]{2,1,0:T(4,128)} %param.9) | non-fusion elementwise | flops 512 | bytes 3072 | tf_op jit(solution)/shard_map/convert_element_type | solution.py:211
  1.5 1.0 %concatenate.39 = bf16[8,4,1280]{2,1,0:T(4,128)(2,1)S(1)} concatenate(bf16[8,4,1024]{2,1,0:T(4,128)(2,1)} %param.8, bf16[8,4,16]{2,1,0:T(4,128)(2,1)S(1)} %convert_element_type.74, bf16[8,4,1]{2,1,0:T(4,128)(2,1)S(1)} %broadcast_in_dim.33, bf16[8,4,239]{2,1,0:T(4,128)(2,1)S(1)} %broadcast_in_dim.34), dimensions={2} | concatenate | bytes 163840 | tf_op jit(solution)/shard_map/concatenate | solution.py:217
  3.5 3.4 %shard_map.82 = (f32[256,1024]{1,0:T(8,128)}, f32[256,1024]{1,0:T(8,128)}) custom-call(bf16[256,1024]{1,0:T(8,128)(2,1)} %bitcast.44, bf16[64,128]{1,0:T(8,128)(2,1)} %mw_ref.1, f32[1,128]{1,0:T(1,128)} %broadcast_in_dim.39.live_ref), custom_call_target="tpu_custom_call" | custom-call | tf_op jit(solution)/shard_map/pallas_call | solution.py:68
  7.0 1.8 %copy.22 = f32[16,16,1024]{2,0,1:T(8,128)S(1)} copy(f32[16,16,1024]{2,1,0:T(8,128)} %bitcast.43) | data formatting | bytes 2097152 | tf_op jit(solution)/shard_map/reshape | solution.py:238
  9.7 0.6 %iota_add_fusion = s32[12,12,10]{2,1,0:T(8,128)} fusion(s32[]{:T(128)S(6)} %select_n.96), kind=kLoop, calls=%fused_computation.29 | loop fusion | flops 1440 | bytes 5764 | tf_op jit(solution)/shard_map/dynamic_slice | solution.py:259
  10.3 0.7 %pad.27.wa_raw = bf16[64,1792]{1,0:T(8,128)(2,1)} pad(bf16[64,1728]{1,0:T(8,128)(2,1)S(1)} %copy-done.1, bf16[]{:T(256)} %constant.53.clone.1), padding=0_0x0_64 | pad | bytes 450562 | tf_op jit(solution)/shard_map/jit(_pad)/pad | solution.py:278
  11.1 0.7 %pad.28.wb_raw = bf16[64,1792]{1,0:T(8,128)(2,1)} pad(bf16[64,1728]{1,0:T(8,128)(2,1)S(1)} %copy-done.2, bf16[]{:T(256)} %constant.53.clone.1), padding=0_0x0_64 | pad | bytes 450562 | tf_op jit(solution)/shard_map/jit(_pad)/pad | solution.py:278
  11.8 0.8 %fusion.9.spread_ref = bf16[488,112]{1,0:T(8,128)(2,1)} fusion(s32[488]{0:T(512)S(1)} %fusion.31, pred[488]{0:T(512)(128)(4,1)S(1)} %compare_and_fusion), kind=kLoop, calls=%fused_computation.19 | loop fusion | flops 163968 | bytes 111752 | tf_op jit(solution)/shard_map/convert_element_type | solution.py:274
  12.6 3.9 %shard_map.83 = (bf16[9,384,256]{2,1,0:T(8,128)(2,1)}, bf16[9,384,256]{2,1,0:T(8,128)(2,1)}) custom-call(bf16[64,1792]{1,0:T(8,128)(2,1)} %pad.27.wa_raw, bf16[64,1792]{1,0:T(8,128)(2,1)} %pad.28.wb_raw), custom_call_target="tpu_custom_call" | custom-call | flops 905969664 | bytes 3538944 | tf_op jit(solution)/shard_map/pallas_call | solution.py:83
  16.9 0.8 %concatenate.43 = f32[16,16,1280]{2,0,1:T(8,128)S(1)} concatenate(f32[16,16,64]{2,0,1:T(8,128)S(1)} %get-tuple-element.26, f32[16,16,1024]{2,0,1:T(8,128)S(1)} %copy.22, f32[16,16,64]{2,0,1:T(8,128)S(1)} %get-tuple-element.25, f32[16,16,128]{2,0,1:T(8,128)S(1)} %broadcast_in_dim.40), dimensions={2} | concatenate | bytes 2621440 | tf_op jit(solution)/shard_map/concatenate | solution.py:243
  20.2 1.3 %collective-permute-start.3 = (bf16[32,1280]{1,0:T(8,128)(2,1)S(1)}, bf16[32,1280]{1,0:T(8,128)(2,1)S(1)}, u32[]{:S(2)}, u32[]{:S(2)}) collective-permute-start(bf16[32,1280]{1,0:T(8,128)(2,1)S(1)} %pad_maximum_fusion.9), channel_id=1, source_target_pairs={{2,0},{3,1},{6,4},{7,5},{10,8},{11,9},{14,12},{15,13},{18,16},{19,... | collective-permute-start | bytes 245768 | tf_op jit(solution)/shard_map/ppermute | solution.py:178
  21.5 4.8 %collective-permute-start.2 = (bf16[32,1280]{1,0:T(8,128)(2,1)S(1)}, bf16[32,1280]{1,0:T(8,128)(2,1)S(1)}, u32[]{:S(2)}, u32[]{:S(2)}) collective-permute-start(bf16[32,1280]{1,0:T(8,128)(2,1)S(1)} %pad_maximum_fusion.8), channel_id=1, source_target_pairs={{0,2},{1,3},{4,6},{5,7},{8,10},{9,11},{12,14},{13,15},{16,18},{17,... | collective-permute-start | bytes 245768 | tf_op jit(solution)/shard_map/ppermute | solution.py:177
  26.4 0.7 %collective-permute-done.3 = bf16[32,1280]{1,0:T(8,128)(2,1)S(1)} collective-permute-done((bf16[32,1280]{1,0:T(8,128)(2,1)S(1)}, bf16[32,1280]{1,0:T(8,128)(2,1)S(1)}, u32[]{:S(2)}, u32[]{:S(2)}) %collective-permute-start.3) | collective-permute-done | bytes 81952 | tf_op jit(solution)/shard_map/ppermute | solution.py:178
  27.1 1.3 %collective-permute-done.2 = bf16[32,1280]{1,0:T(8,128)(2,1)S(1)} collective-permute-done((bf16[32,1280]{1,0:T(8,128)(2,1)S(1)}, bf16[32,1280]{1,0:T(8,128)(2,1)S(1)}, u32[]{:S(2)}, u32[]{:S(2)}) %collective-permute-start.2) | collective-permute-done | bytes 81952 | tf_op jit(solution)/shard_map/ppermute | solution.py:177
  29.0 1.3 %collective-permute-start.5 = (bf16[42,1280]{1,0:T(8,128)(2,1)S(1)}, bf16[42,1280]{1,0:T(8,128)(2,1)S(1)}, u32[]{:S(2)}, u32[]{:S(2)}) collective-permute-start(bf16[42,1280]{1,0:T(8,128)(2,1)S(1)} %pad_maximum_fusion.4), channel_id=1, source_target_pairs={{4,0},{8,4},{12,8},{5,1},{9,5},{13,9},{6,2},{10,6},{14,10},{7,3},{... | collective-permute-start | bytes 322568 | tf_op jit(solution)/shard_map/ppermute | solution.py:178
  30.3 5.4 %collective-permute-start.4 = (bf16[42,1280]{1,0:T(8,128)(2,1)S(1)}, bf16[42,1280]{1,0:T(8,128)(2,1)S(1)}, u32[]{:S(2)}, u32[]{:S(2)}) collective-permute-start(bf16[42,1280]{1,0:T(8,128)(2,1)S(1)} %pad_maximum_fusion.3), channel_id=1, source_target_pairs={{0,4},{4,8},{8,12},{1,5},{5,9},{9,13},{2,6},{6,10},{10,14},{3,7},{... | collective-permute-start | bytes 322568 | tf_op jit(solution)/shard_map/ppermute | solution.py:177
  35.7 0.7 %collective-permute-done.5 = bf16[42,1280]{1,0:T(8,128)(2,1)S(1)} collective-permute-done((bf16[42,1280]{1,0:T(8,128)(2,1)S(1)}, bf16[42,1280]{1,0:T(8,128)(2,1)S(1)}, u32[]{:S(2)}, u32[]{:S(2)}) %collective-permute-start.5) | collective-permute-done | bytes 107552 | tf_op jit(solution)/shard_map/ppermute | solution.py:178
  36.6 1.4 %collective-permute-done.4 = bf16[42,1280]{1,0:T(8,128)(2,1)S(1)} collective-permute-done((bf16[42,1280]{1,0:T(8,128)(2,1)S(1)}, bf16[42,1280]{1,0:T(8,128)(2,1)S(1)}, u32[]{:S(2)}, u32[]{:S(2)}) %collective-permute-start.4) | collective-permute-done | bytes 107552 | tf_op jit(solution)/shard_map/ppermute | solution.py:177
  38.0 0.7 %reshape.156 = f32[1,18,1280]{2,0,1:T(1,128)} reshape(f32[18,1280]{1,0:T(8,128)S(1)} %slice_convert_fusion.1) | data formatting | bytes 184320 | tf_op jit(solution)/shard_map/convert_element_type | solution.py:175
  39.3 1.2 %pad_maximum_fusion = f32[18,18,1280]{2,0,1:T(8,128)S(1)} fusion(f32[1,18,1280]{2,0,1:T(1,128)S(1)} %reshape.157, f32[16,1,1280]{2,0,1:T(8,128)S(1)} %get-tuple-element.24, f32[16,16,1280]{2,0,1:T(8,128)S(1)} %concatenate.43, f32[16,1,1280]{2,0,1:T(8,128)S(1)} %get-tuple-element.22, f32[1,18,1280]{2,0,1:T(1,128)} %reshape.156), kind=kLoop, calls=%fused_computation | loop fusion | flops 1658880 | bytes 3317760 | tf_op jit(solution)/shard_map/concatenate | solution.py:181
  41.1 1.5 %pad.26.clone = f32[18,24,1280]{2,1,0:T(8,128)} pad(f32[18,18,1280]{2,1,0:T(8,128)S(1)} %copy.30, f32[]{:T(128)} %constant.55.clone.1), padding=0_0x0_6x0_0 | pad | bytes 3870724 | tf_op jit(solution)/shard_map/jit(_pad)/pad | solution.py:268
  43.0 4.2 %fusion = f32[1,10,10,10,64]{4,0,3,2,1:T(1,128)S(1)} fusion(bf16[1,12,12,12,64]{4,3,2,1,0:T(8,128)(2,1)S(1)} %fusion.6, bf16[64,3,3,3,64]{4,3,2,1,0:T(4,128)(2,1)S(1)} %reshape.150), kind=kOutput, calls=%fused_computation.5 | convolution fusion | flops 221184000 | bytes 698368 | tf_op jit(solution)/shard_map/conv_general_dilated | solution.py:143
  48.2 0.7 %pad.25.hid_ref = bf16[112,640]{1,0:T(8,128)(2,1)} pad(bf16[100,640]{1,0:T(8,128)(2,1)S(1)} %reshape.151, bf16[]{:T(256)} %constant.53.clone.1), padding=0_12x0_0 | pad | bytes 271362 | tf_op jit(solution)/shard_map/jit(_pad)/pad | solution.py:266
  48.8 15.3 %shard_map.84 = bf16[256,1024]{1,0:T(8,128)(2,1)} custom-call(bf16[112,640]{1,0:T(8,128)(2,1)} %pad.25.hid_ref, bf16[488,112]{1,0:T(8,128)(2,1)} %fusion.9.spread_ref, f32[432,1280]{1,0:T(8,128)} %bitcast.42, f32[256,1024]{1,0:T(8,128)} %get-tuple-element.10.gb_ref, bf16[9,384,256]{2,1,0:T(8,128)(2,1)} %get-tuple-element.11.wa_ref, ...), custom_call_target="tpu_custom_call" | custom-call | tf_op jit(solution)/shard_map/pallas_call | solution.py:130
  (67 shorter events, 6.5 us)
Async XLA Ops:
  0.0 10.3 %copy-start.1 = (bf16[64,1728]{1,0:T(8,128)(2,1)S(1)}, bf16[64,1728]{1,0:T(8,128)(2,1)}, u32[]{:S(2)}) copy-start(bf16[64,1728]{1,0:T(8,128)(2,1)} %param.13) | copy-start | bytes 663556
  0.0 11.1 %copy-start.2 = (bf16[64,1728]{1,0:T(8,128)(2,1)S(1)}, bf16[64,1728]{1,0:T(8,128)(2,1)}, u32[]{:S(2)}) copy-start(bf16[64,1728]{1,0:T(8,128)(2,1)} %param.14) | copy-start | bytes 663556
  2.4 15.4 %collective-permute-start = (bf16[8,4,1280]{2,1,0:T(4,128)(2,1)S(1)}, bf16[8,4,1280]{2,1,0:T(4,128)(2,1)S(1)}, u32[]{:S(2)}, u32[]{:S(2)}) collective-permute-start(bf16[8,4,1280]{2,1,0:T(4,128)(2,1)S(1)} %concatenate.39), channel_id=1, source_target_pairs={{0,1},{1,0},{2,3},{3,2},{4,5},{5,4},{6,7},{7,6},{8,9},{9,8},{10,11... | collective-permute-start | bytes 245768 | tf_op jit(solution)/shard_map/ppermute | solution.py:218
  8.9 8.0 %collective-permute-start.1 = (bf16[16,16,64]{2,0,1:T(8,128)(2,1)S(1)}, bf16[16,16,64]{2,0,1:T(8,128)(2,1)S(1)}, u32[]{:S(2)}, u32[]{:S(2)}) collective-permute-start(bf16[16,16,64]{2,0,1:T(8,128)(2,1)S(1)} %fusion.10), channel_id=1, source_target_pairs={{0,1},{1,0},{2,3},{3,2},{4,5},{5,4},{6,7},{7,6},{8,9},{9,8},{10,11... | collective-permute-start | bytes 98312 | tf_op jit(solution)/shard_map/ppermute | solution.py:241
  10.3 6.2 %copy-start.3 = (bf16[64,1728]{1,0:T(8,128)(2,1)S(1)}, bf16[64,1728]{1,0:T(8,128)(2,1)}, u32[]{:S(2)}) copy-start(bf16[64,1728]{1,0:T(8,128)(2,1)} %param.12) | copy-start | bytes 663556
  20.2 6.8 %collective-permute-start.3 = (bf16[32,1280]{1,0:T(8,128)(2,1)S(1)}, bf16[32,1280]{1,0:T(8,128)(2,1)S(1)}, u32[]{:S(2)}, u32[]{:S(2)}) collective-permute-start(bf16[32,1280]{1,0:T(8,128)(2,1)S(1)} %pad_maximum_fusion.9), channel_id=1, source_target_pairs={{2,0},{3,1},{6,4},{7,5},{10,8},{11,9},{14,12},{15,13},{18,16},{19,... | collective-permute-start | bytes 245768 | tf_op jit(solution)/shard_map/ppermute | solution.py:178
  21.5 6.9 %collective-permute-start.2 = (bf16[32,1280]{1,0:T(8,128)(2,1)S(1)}, bf16[32,1280]{1,0:T(8,128)(2,1)S(1)}, u32[]{:S(2)}, u32[]{:S(2)}) collective-permute-start(bf16[32,1280]{1,0:T(8,128)(2,1)S(1)} %pad_maximum_fusion.8), channel_id=1, source_target_pairs={{0,2},{1,3},{4,6},{5,7},{8,10},{9,11},{12,14},{13,15},{16,18},{17,... | collective-permute-start | bytes 245768 | tf_op jit(solution)/shard_map/ppermute | solution.py:177
  29.0 7.5 %collective-permute-start.5 = (bf16[42,1280]{1,0:T(8,128)(2,1)S(1)}, bf16[42,1280]{1,0:T(8,128)(2,1)S(1)}, u32[]{:S(2)}, u32[]{:S(2)}) collective-permute-start(bf16[42,1280]{1,0:T(8,128)(2,1)S(1)} %pad_maximum_fusion.4), channel_id=1, source_target_pairs={{4,0},{8,4},{12,8},{5,1},{9,5},{13,9},{6,2},{10,6},{14,10},{7,3},{... | collective-permute-start | bytes 322568 | tf_op jit(solution)/shard_map/ppermute | solution.py:178
  30.3 7.7 %collective-permute-start.4 = (bf16[42,1280]{1,0:T(8,128)(2,1)S(1)}, bf16[42,1280]{1,0:T(8,128)(2,1)S(1)}, u32[]{:S(2)}, u32[]{:S(2)}) collective-permute-start(bf16[42,1280]{1,0:T(8,128)(2,1)S(1)} %pad_maximum_fusion.3), channel_id=1, source_target_pairs={{0,4},{4,8},{8,12},{1,5},{5,9},{9,13},{2,6},{6,10},{10,14},{3,7},{... | collective-permute-start | bytes 322568 | tf_op jit(solution)/shard_map/ppermute | solution.py:177
  43.0 4.3 %copy-start = (s32[12,12,10]{2,1,0:T(8,128)S(1)}, s32[12,12,10]{2,1,0:T(8,128)}, u32[]{:S(2)}) copy-start(s32[12,12,10]{2,1,0:T(8,128)} %iota_add_fusion) | copy-start | bytes 17284
  43.0 4.3 %copy-start.4 = (pred[12,12,20]{2,1,0:T(8,128)(4,1)S(1)}, pred[12,12,20]{2,1,0:T(8,128)(4,1)}, u32[]{:S(2)}) copy-start(pred[12,12,20]{2,1,0:T(8,128)(4,1)} %get-tuple-element.27) | copy-start | bytes 8644
  43.0 4.3 %copy-start.5 = (pred[12,12,20]{2,1,0:T(8,128)(4,1)S(1)}, pred[12,12,20]{2,1,0:T(8,128)(4,1)}, u32[]{:S(2)}) copy-start(pred[12,12,20]{2,1,0:T(8,128)(4,1)} %get-tuple-element.28) | copy-start | bytes 8644

commit v7 on v5

--- a/solution.py
+++ b/solution.py
@@ -250,6 +250,7 @@
         axis=2,
     )
     region, gate_a = grow_both(packed, gate_a, "gy", 1, (2, 1))
+    gate_a = jnp.pad(gate_a, ((0, 0), (0, STRIDE - edge - 2), (0, 0)))
     region, gate_a = grow_both(region, gate_a, "gx", 0, (2, 1))
     size = region.shape[0]
     volume = region[:, :, :flat_z].reshape(size, size, cells_z, channels)
@@ -265,7 +266,7 @@
     cells = hidden.shape[0] * hidden.shape[1]
     hid = jnp.pad(hidden.reshape(cells, -1), ((0, ROWS_C - cells), (0, 0)))
 
-    gate_a = jnp.pad(gate_a, ((0, 0), (0, STRIDE - edge - 2), (0, 0))).reshape(-1, gate_a.shape[2])
+    gate_a = gate_a.reshape(-1, gate_a.shape[2])
 
     rows = jnp.arange(ROWS_F)
     fx, fy = rows // STRIDE, rows % STRIDE

time: 64.1 us -> 68.8 us (1.073); the launches traced: 63.7 us -> 67.7 us
  local copies, waits for them, and re-layouts: 11.5 us -> 16 us
  waiting for transfers between devices: 3.65 us -> 2.49 us
  matrix products: 4.22 us -> 5.32 us
    concatenate x0 -> x1, local copies, waits for them, and re-layouts: none -> 2.04 us  [grow_both(): jnp.concatenate([low[1], gate, high[1]], axis=dim)]
    ppermute x2, waiting for transfers between devices: 2.56 us -> 0.66 us  [grow_both(): lax.ppermute(pack(cells_head, gate_head), axis, shift_pairs(count, False))]
    pad x1 -> x0, local copies, waits for them, and re-layouts: 1.51 us -> none  [body(): jnp.pad(gate_a, ((0, 0), (0, STRIDE - edge - 2), (0, 0)))]
    reshape x4, local copies, waits for them, and re-layouts: 0.15 us -> 1.43 us  [pack(): c.astype(jnp.float32).reshape(-1, lanes)]
    conv_general_dilated x1, matrix products: 4.22 us -> 5.32 us  [convolve(): lax.conv_general_dilated(padded[None], kernel, (1, 1, 1), 'VALID', dimens...]
    slice x2, local copies, waits for them, and re-layouts: 0.02 us -> 0.92 us  [unpack(): m[split:].reshape(gate_head.shape)]
    slice x4, local copies, waits for them, and re-layouts: 0.03 us -> 0.93 us  [unpack(): m[:split].reshape(cells_head.shape).astype(cells.dtype)]
    reshape x1, local copies, waits for them, and re-layouts: 0.34 us -> 1.17 us  [convolve(): weight.reshape(channels, 3, 3, 3, channels).transpose(1, 2, 3, 0, 4)]
  transfers between devices with their start and end apart: 6 -> 6, of which waited for: 2 -> 3; matrix products, arithmetic and copies ran while one was open for 12% -> 15% of each run, Pallas kernels for 12% -> 11%
where the time goes in v7:
time: 68.8 us; the launch traced here: 67.7 us
  Pallas kernels  22.7 us (33%)
  local copies, waits for them, and re-layouts  16 us (23%)
  starting transfers between devices  13.1 us (19%)
  other arithmetic  5.7 us (8%)
  matrix products  5.32 us (8%)
  waiting for transfers between devices  2.49 us (4%)
  between operations  2.39 us (3%)
    pallas_call x1, Pallas kernels, fine_stage(): pl.pallas_call(fine_kernel, out_shape=jax.ShapeDtypeStruct(gate_b.shape,...  15.3 us
    ppermute x2, starting transfers between devices, grow_both(): lax.ppermute(pack(cells_tail, gate_tail), axis, shift_pairs(count, True))  9.74 us
    conv_general_dilated x1, matrix products, convolve(): lax.conv_general_dilated(padded[None], kernel, (1, 1, 1), 'VALID', dimens...  5.32 us
    pallas_call x1, Pallas kernels, band_stage(): pl.pallas_call(band_kernel, out_shape=(shape, shape), cost_estimate=pl.Co...  3.94 us
    pallas_call x1, Pallas kernels, gate_stage(): pl.pallas_call(gate_kernel, out_shape=(shape, shape))  3.44 us
    ppermute x2, starting transfers between devices, grow_both(): lax.ppermute(pack(cells_head, gate_head), axis, shift_pairs(count, False))  2.72 us
    concatenate x1, local copies, waits for them, and re-layouts, grow_both(): jnp.concatenate([low[1], gate, high[1]], axis=dim)  2.04 us
    reshape x1, local copies, waits for them, and re-layouts, body(): gate_a = gate_a.reshape(field.shape)  1.84 us
  transfers between devices with their start and end apart: 6, of which 3 were waited for; matrix products, arithmetic and copies ran while one was open for 15% of the time, Pallas kernels for 11%

profile of v7, /device:TPU:0, one launch (start us, length us, event | category | flops | bytes accessed | tf_op | source)
XLA Modules:
  0.0 67.7 jit_solution(12974486108863662648)
XLA Ops:
  0.7 0.7 %convert_element_type.60 = bf16[8,4,16]{2,1,0:T(4,128)(2,1)S(1)} convert(s32[8,4,16]{2,1,0:T(4,128)} %param.9) | non-fusion elementwise | flops 512 | bytes 3072 | tf_op jit(solution)/shard_map/convert_element_type | solution.py:211
  1.4 1.0 %concatenate.39 = bf16[8,4,1280]{2,1,0:T(4,128)(2,1)S(1)} concatenate(bf16[8,4,1024]{2,1,0:T(4,128)(2,1)} %param.8, bf16[8,4,16]{2,1,0:T(4,128)(2,1)S(1)} %convert_element_type.60, bf16[8,4,1]{2,1,0:T(4,128)(2,1)S(1)} %broadcast_in_dim.33, bf16[8,4,239]{2,1,0:T(4,128)(2,1)S(1)} %broadcast_in_dim.34), dimensions={2} | concatenate | bytes 163840 | tf_op jit(solution)/shard_map/concatenate | solution.py:217
  3.5 3.4 %shard_map.82 = (f32[256,1024]{1,0:T(8,128)}, f32[256,1024]{1,0:T(8,128)}) custom-call(bf16[256,1024]{1,0:T(8,128)(2,1)} %bitcast.40, bf16[64,128]{1,0:T(8,128)(2,1)} %mw_ref.1, f32[1,128]{1,0:T(1,128)} %broadcast_in_dim.39.live_ref), custom_call_target="tpu_custom_call" | custom-call | tf_op jit(solution)/shard_map/pallas_call | solution.py:68
  6.9 1.8 %copy.23 = f32[16,16,1024]{2,0,1:T(8,128)S(1)} copy(f32[16,16,1024]{2,1,0:T(8,128)} %bitcast.39) | data formatting | bytes 2097152 | tf_op jit(solution)/shard_map/reshape | solution.py:238
  10.3 0.7 %concatenate.43 = f32[16,16,1280]{2,0,1:T(8,128)S(1)} concatenate(f32[16,16,64]{2,0,1:T(8,128)S(1)} %get-tuple-element.22, f32[16,16,1024]{2,0,1:T(8,128)S(1)} %copy.23, f32[16,16,64]{2,0,1:T(8,128)S(1)} %get-tuple-element.21, f32[16,16,128]{2,0,1:T(8,128)S(1)} %broadcast_in_dim.40), dimensions={2} | concatenate | bytes 2621440 | tf_op jit(solution)/shard_map/concatenate | solution.py:243
  13.5 1.3 %collective-permute-start.3 = (f32[32,1280]{1,0:T(8,128)S(1)}, f32[32,1280]{1,0:T(8,128)S(1)}, u32[]{:S(2)}, u32[]{:S(2)}) collective-permute-start(f32[32,1280]{1,0:T(8,128)S(1)} %pad_maximum_fusion.5), channel_id=1, source_target_pairs={{2,0},{3,1},{6,4},{7,5},{10,8},{11,9},{14,12},{15,13},{18,16},{19,... | collective-permute-start | bytes 491528 | tf_op jit(solution)/shard_map/ppermute | solution.py:178
  14.8 4.6 %collective-permute-start.2 = (f32[32,1280]{1,0:T(8,128)S(1)}, f32[32,1280]{1,0:T(8,128)S(1)}, u32[]{:S(2)}, u32[]{:S(2)}) collective-permute-start(f32[32,1280]{1,0:T(8,128)S(1)} %pad_maximum_fusion.4), channel_id=1, source_target_pairs={{0,2},{1,3},{4,6},{5,7},{8,10},{9,11},{12,14},{13,15},{16,18},{17,... | collective-permute-start | bytes 491528 | tf_op jit(solution)/shard_map/ppermute | solution.py:177
  19.4 0.7 %pad.27.wa_raw = bf16[64,1792]{1,0:T(8,128)(2,1)} pad(bf16[64,1728]{1,0:T(8,128)(2,1)S(1)} %copy-done.3, bf16[]{:T(256)} %constant.53.clone.1), padding=0_0x0_64 | pad | bytes 450562 | tf_op jit(solution)/shard_map/jit(_pad)/pad | solution.py:279
  20.1 0.7 %pad.28.wb_raw = bf16[64,1792]{1,0:T(8,128)(2,1)} pad(bf16[64,1728]{1,0:T(8,128)(2,1)S(1)} %copy-done.4, bf16[]{:T(256)} %constant.53.clone.1), padding=0_0x0_64 | pad | bytes 450562 | tf_op jit(solution)/shard_map/jit(_pad)/pad | solution.py:279
  22.2 1.2 %collective-permute-done.2 = f32[32,1280]{1,0:T(8,128)S(1)} collective-permute-done((f32[32,1280]{1,0:T(8,128)S(1)}, f32[32,1280]{1,0:T(8,128)S(1)}, u32[]{:S(2)}, u32[]{:S(2)}) %collective-permute-start.2) | collective-permute-done | bytes 163872 | tf_op jit(solution)/shard_map/ppermute | solution.py:177
  23.5 0.7 reshape.171
  25.7 1.4 %collective-permute-start.5 = (f32[48,1280]{1,0:T(8,128)S(1)}, f32[48,1280]{1,0:T(8,128)}, u32[]{:S(2)}, u32[]{:S(2)}) collective-permute-start(f32[48,1280]{1,0:T(8,128)S(1)} %pad_maximum_fusion.3), channel_id=1, source_target_pairs={{4,0},{8,4},{12,8},{5,1},{9,5},{13,9},{6,2},{10,6},{14,10},{7,3},{... | collective-permute-start | bytes 737288 | tf_op jit(solution)/shard_map/ppermute | solution.py:178
  27.2 5.2 %collective-permute-start.4 = (f32[48,1280]{1,0:T(8,128)S(1)}, f32[48,1280]{1,0:T(8,128)S(1)}, u32[]{:S(2)}, u32[]{:S(2)}) collective-permute-start(f32[48,1280]{1,0:T(8,128)S(1)} %pad_maximum_fusion.2), channel_id=1, source_target_pairs={{0,4},{4,8},{8,12},{1,5},{5,9},{9,13},{2,6},{6,10},{10,14},{3,7},{... | collective-permute-start | bytes 737288 | tf_op jit(solution)/shard_map/ppermute | solution.py:177
  32.4 3.9 %shard_map.83 = (bf16[9,384,256]{2,1,0:T(8,128)(2,1)}, bf16[9,384,256]{2,1,0:T(8,128)(2,1)}) custom-call(bf16[64,1792]{1,0:T(8,128)(2,1)} %pad.27.wa_raw, bf16[64,1792]{1,0:T(8,128)(2,1)} %pad.28.wb_raw), custom_call_target="tpu_custom_call" | custom-call | flops 905969664 | bytes 3538944 | tf_op jit(solution)/shard_map/pallas_call | solution.py:83
  36.3 1.2 %reshape.160 = bf16[64,3,3,3,64]{4,3,2,1,0:T(4,128)(2,1)} reshape(bf16[64,1728]{1,0:T(8,128)(2,1)S(1)} %copy-done.5) | data formatting | bytes 442368 | tf_op jit(solution)/shard_map/reshape | solution.py:142
  37.5 0.9 %fusion.9.spread_ref = bf16[488,112]{1,0:T(8,128)(2,1)} fusion(s32[488]{0:T(512)S(1)} %fusion.29, pred[488]{0:T(512)(128)(4,1)S(1)} %compare_and_fusion), kind=kLoop, calls=%fused_computation.20 | loop fusion | flops 163968 | bytes 111752 | tf_op jit(solution)/shard_map/convert_element_type | solution.py:275
  38.4 0.9 %slice.124 = f32[24,1280]{1,0:T(8,128)S(1)} slice(f32[48,1280]{1,0:T(8,128)} %collective-permute-done.5), slice={[24:48], [0:1280]} | slice | bytes 245760 | tf_op jit(solution)/shard_map/slice | solution.py:175
  39.4 0.9 %slice.141 = bf16[24,1280]{1,0:T(8,128)(2,1)S(1)} slice(f32[48,1280]{1,0:T(8,128)} %collective-permute-done.5), slice={[0:24], [0:1280]} | slice | bytes 122880 | tf_op jit(solution)/shard_map/slice | solution.py:175
  40.3 0.7 %reshape.162 = f32[1,24,1280]{2,0,1:T(1,128)} reshape(f32[24,1280]{1,0:T(8,128)S(1)} %slice.123) | data formatting | bytes 245760 | tf_op jit(solution)/shard_map/reshape | solution.py:175
  42.0 5.3 %fusion = f32[1,10,10,10,64]{4,0,3,2,1:T(1,128)S(1)} fusion(bf16[1,12,12,12,64]{4,3,2,1,0:T(8,128)(2,1)S(1)} %fusion.6, bf16[64,3,3,3,64]{4,3,2,1,0:T(4,128)(2,1)} %reshape.160), kind=kOutput, calls=%fused_computation.6 | convolution fusion | flops 221184000 | bytes 698368 | tf_op jit(solution)/shard_map/conv_general_dilated | solution.py:143
  48.3 0.7 %pad.26.hid_ref = bf16[112,640]{1,0:T(8,128)(2,1)} pad(bf16[100,640]{1,0:T(8,128)(2,1)S(1)} %reshape.161, bf16[]{:T(256)} %constant.53.clone.1), padding=0_12x0_0 | pad | bytes 271362 | tf_op jit(solution)/shard_map/jit(_pad)/pad | solution.py:267
  49.0 1.3 %pad_maximum_fusion = f32[18,24,1280]{2,0,1:T(8,128)S(1)} fusion(f32[1,24,1280]{2,0,1:T(1,128)S(1)} %reshape.163, f32[16,24,1280]{2,0,1:T(8,128)S(1)} %select_maximum_fusion, f32[1,24,1280]{2,0,1:T(1,128)} %reshape.162), kind=kLoop, calls=%fused_computation | loop fusion | flops 1105920 | bytes 4423680 | tf_op jit(solution)/shard_map/concatenate | solution.py:181
  50.3 2.0 %copy.30 = f32[18,24,1280]{2,1,0:T(8,128)} copy(f32[18,24,1280]{2,0,1:T(8,128)S(1)} %pad_maximum_fusion) | data formatting | bytes 4423680 | tf_op jit(solution)/shard_map/concatenate | solution.py:181
  52.4 15.3 %shard_map.84 = bf16[256,1024]{1,0:T(8,128)(2,1)} custom-call(bf16[112,640]{1,0:T(8,128)(2,1)} %pad.26.hid_ref, bf16[488,112]{1,0:T(8,128)(2,1)} %fusion.9.spread_ref, f32[432,1280]{1,0:T(8,128)} %bitcast.38, f32[256,1024]{1,0:T(8,128)} %get-tuple-element.10.gb_ref, bf16[9,384,256]{2,1,0:T(8,128)(2,1)} %get-tuple-element.11.wa_ref, ...), custom_call_target="tpu_custom_call" | custom-call | tf_op jit(solution)/shard_map/pallas_call | solution.py:130
  (70 shorter events, 8.7 us)
Async XLA Ops:
  2.4 8.7 %collective-permute-start = (bf16[8,4,1280]{2,1,0:T(4,128)(2,1)S(1)}, bf16[8,4,1280]{2,1,0:T(4,128)(2,1)S(1)}, u32[]{:S(2)}, u32[]{:S(2)}) collective-permute-start(bf16[8,4,1280]{2,1,0:T(4,128)(2,1)S(1)} %concatenate.39), channel_id=1, source_target_pairs={{0,1},{1,0},{2,3},{3,2},{4,5},{5,4},{6,7},{7,6},{8,9},{9,8},{10,11... | collective-permute-start | bytes 245768 | tf_op jit(solution)/shard_map/ppermute | solution.py:218
  8.9 1.4 %collective-permute-start.1 = (f32[16,16,64]{2,0,1:T(8,128)S(1)}, f32[16,16,64]{2,0,1:T(8,128)S(1)}, u32[]{:S(2)}, u32[]{:S(2)}) collective-permute-start(f32[16,16,64]{2,0,1:T(8,128)S(1)} %slice_select_fusion), channel_id=1, source_target_pairs={{0,1},{1,0},{2,3},{3,2},{4,5},{5,4},{6,7},{7,6},{8,9},{9,8},{10,11... | collective-permute-start | bytes 196616 | tf_op jit(solution)/shard_map/ppermute | solution.py:241
  11.0 8.4 %copy-start.3 = (bf16[64,1728]{1,0:T(8,128)(2,1)S(1)}, bf16[64,1728]{1,0:T(8,128)(2,1)}, u32[]{:S(2)}) copy-start(bf16[64,1728]{1,0:T(8,128)(2,1)} %param.13) | copy-start | bytes 663556
  11.0 9.1 %copy-start.4 = (bf16[64,1728]{1,0:T(8,128)(2,1)S(1)}, bf16[64,1728]{1,0:T(8,128)(2,1)}, u32[]{:S(2)}) copy-start(bf16[64,1728]{1,0:T(8,128)(2,1)} %param.14) | copy-start | bytes 663556
  13.5 8.6 %collective-permute-start.3 = (f32[32,1280]{1,0:T(8,128)S(1)}, f32[32,1280]{1,0:T(8,128)S(1)}, u32[]{:S(2)}, u32[]{:S(2)}) collective-permute-start(f32[32,1280]{1,0:T(8,128)S(1)} %pad_maximum_fusion.5), channel_id=1, source_target_pairs={{2,0},{3,1},{6,4},{7,5},{10,8},{11,9},{14,12},{15,13},{18,16},{19,... | collective-permute-start | bytes 491528 | tf_op jit(solution)/shard_map/ppermute | solution.py:178
  14.8 8.5 %collective-permute-start.2 = (f32[32,1280]{1,0:T(8,128)S(1)}, f32[32,1280]{1,0:T(8,128)S(1)}, u32[]{:S(2)}, u32[]{:S(2)}) collective-permute-start(f32[32,1280]{1,0:T(8,128)S(1)} %pad_maximum_fusion.4), channel_id=1, source_target_pairs={{0,2},{1,3},{4,6},{5,7},{8,10},{9,11},{12,14},{13,15},{16,18},{17,... | collective-permute-start | bytes 491528 | tf_op jit(solution)/shard_map/ppermute | solution.py:177
  24.8 0.9 %copy-start.1 = (f32[24,1280]{1,0:T(8,128)S(1)}, f32[24,1280]{1,0:T(8,128)}, u32[]{:S(2)}) copy-start(f32[24,1280]{1,0:T(8,128)} %reshape.173) | copy-start | bytes 368644
  24.8 2.4 %copy-start = (f32[24,1280]{1,0:T(8,128)S(1)}, f32[24,1280]{1,0:T(8,128)}, u32[]{:S(2)}) copy-start(f32[24,1280]{1,0:T(8,128)} %reshape.171) | copy-start | bytes 368644
  25.7 10.6 %copy-start.5 = (bf16[64,1728]{1,0:T(8,128)(2,1)S(1)}, bf16[64,1728]{1,0:T(8,128)(2,1)}, u32[]{:S(2)}) copy-start(bf16[64,1728]{1,0:T(8,128)(2,1)} %param.12) | copy-start | bytes 663556
  25.7 12.6 %collective-permute-start.5 = (f32[48,1280]{1,0:T(8,128)S(1)}, f32[48,1280]{1,0:T(8,128)}, u32[]{:S(2)}, u32[]{:S(2)}) collective-permute-start(f32[48,1280]{1,0:T(8,128)S(1)} %pad_maximum_fusion.3), channel_id=1, source_target_pairs={{4,0},{8,4},{12,8},{5,1},{9,5},{13,9},{6,2},{10,6},{14,10},{7,3},{... | collective-permute-start | bytes 737288 | tf_op jit(solution)/shard_map/ppermute | solution.py:178
  27.2 13.1 %collective-permute-start.4 = (f32[48,1280]{1,0:T(8,128)S(1)}, f32[48,1280]{1,0:T(8,128)S(1)}, u32[]{:S(2)}, u32[]{:S(2)}) collective-permute-start(f32[48,1280]{1,0:T(8,128)S(1)} %pad_maximum_fusion.2), channel_id=1, source_target_pairs={{0,4},{4,8},{8,12},{1,5},{5,9},{9,13},{2,6},{6,10},{10,14},{3,7},{... | collective-permute-start | bytes 737288 | tf_op jit(solution)/shard_map/ppermute | solution.py:177
  42.0 5.4 %copy-start.2 = (s32[12,12,10]{2,1,0:T(8,128)S(1)}, s32[12,12,10]{2,1,0:T(8,128)}, u32[]{:S(2)}) copy-start(s32[12,12,10]{2,1,0:T(8,128)} %iota_add_fusion) | copy-start | bytes 17284
  42.0 5.4 %copy-start.6 = (pred[12,12,20]{2,1,0:T(8,128)(4,1)S(1)}, pred[12,12,20]{2,1,0:T(8,128)(4,1)}, u32[]{:S(2)}) copy-start(pred[12,12,20]{2,1,0:T(8,128)(4,1)} %get-tuple-element.24) | copy-start | bytes 8644

commit v8 on v5

--- a/solution.py
+++ b/solution.py
@@ -36,8 +36,10 @@
         spreads = []
         for dz in range(3):
             d = 3 * t + dz
-            block = w_ref[:, 128 * (d // 2) : 128 * (d // 2) + 128]
-            spreads.append(jnp.dot(block, halves[d % 2], preferred_element_type=jnp.float32))
+            low = 128 * (d // 2)
+            high = min(low + 128, w_ref.shape[1])
+            pick = halves[d % 2][: high - low]
+            spreads.append(jnp.dot(w_ref[:, low:high], pick, preferred_element_type=jnp.float32))
         for zi in range(6):
             part = jnp.zeros((64, 256), jnp.float32)
             for dz in range(3):
@@ -274,8 +276,7 @@
     spread = (inside[:, None] & (source[:, None] == jnp.arange(ROWS_C)[None, :])).astype(
         jnp.bfloat16
     )
-    wide = ((0, 0), (0, 1792 - fine_weight_a.shape[1]))
-    band_a, band_b = band_stage(jnp.pad(fine_weight_a, wide), jnp.pad(fine_weight_b, wide))
+    band_a, band_b = band_stage(fine_weight_a, fine_weight_b)
     out = fine_stage(hid, spread, gate_a, gate_b, band_a, band_b)
     return out.reshape(field.shape)
 

time: 64.1 us -> 62.8 us (0.980)
  local copies, waits for them, and re-layouts: 11.5 us -> 10 us
    pad x2 -> x0, local copies, waits for them, and re-layouts: 1.4 us -> none  [the longest x1 0.71 us: body(): jnp.pad(fine_weight_a, wide)]
  transfers between devices with their start and end apart: 6 -> 6, of which waited for: 2 -> 3; matrix products, arithmetic and copies ran while one was open for 12% -> 10% of each run, Pallas kernels for 12% -> 12%
where the time goes in v8:
time: 62.8 us; the launch traced here: 62.4 us
  Pallas kernels  22.6 us (36%)
  starting transfers between devices  13.3 us (21%)
  local copies, waits for them, and re-layouts  10 us (16%)
  other arithmetic  5.55 us (9%)
  waiting for transfers between devices  4.23 us (7%)
  matrix products  4.22 us (7%)
  between operations  2.45 us (4%)
    pallas_call x1, Pallas kernels, fine_stage(): pl.pallas_call(fine_kernel, out_shape=jax.ShapeDtypeStruct(gate_b.shape,...  15.3 us
    ppermute x2, starting transfers between devices, grow_both(): lax.ppermute(pack(cells_tail, gate_tail), axis, shift_pairs(count, True))  10 us
    conv_general_dilated x1, matrix products, convolve(): lax.conv_general_dilated(padded[None], kernel, (1, 1, 1), 'VALID', dimens...  4.22 us
    pallas_call x1, Pallas kernels, band_stage(): pl.pallas_call(band_kernel, out_shape=(shape, shape), cost_estimate=pl.Co...  3.93 us
    pallas_call x1, Pallas kernels, gate_stage(): pl.pallas_call(gate_kernel, out_shape=(shape, shape))  3.42 us
    ppermute x2, waiting for transfers between devices, grow_both(): lax.ppermute(pack(cells_head, gate_head), axis, shift_pairs(count, False))  2.87 us
    ppermute x2, starting transfers between devices, grow_both(): lax.ppermute(pack(cells_head, gate_head), axis, shift_pairs(count, False))  2.58 us
    reshape x1, local copies, waits for them, and re-layouts, body(): gate_a = gate_a.reshape(field.shape)  1.84 us
  transfers between devices with their start and end apart: 6, of which 3 were waited for; matrix products, arithmetic and copies ran while one was open for 10% of the time, Pallas kernels for 12%

profile of v8, /device:TPU:0, one launch (start us, length us, event | category | flops | bytes accessed | tf_op | source)
XLA Modules:
  0.0 62.4 jit_solution(697911381700897774)
XLA Ops:
  0.7 0.7 %convert_element_type.57 = bf16[8,4,16]{2,1,0:T(4,128)(2,1)S(1)} convert(s32[8,4,16]{2,1,0:T(4,128)} %param.9) | non-fusion elementwise | flops 512 | bytes 3072 | tf_op jit(solution)/shard_map/convert_element_type | solution.py:213
  1.4 1.0 %concatenate.39 = bf16[8,4,1280]{2,1,0:T(4,128)(2,1)S(1)} concatenate(bf16[8,4,1024]{2,1,0:T(4,128)(2,1)} %param.8, bf16[8,4,16]{2,1,0:T(4,128)(2,1)S(1)} %convert_element_type.57, bf16[8,4,1]{2,1,0:T(4,128)(2,1)S(1)} %broadcast_in_dim.33, bf16[8,4,239]{2,1,0:T(4,128)(2,1)S(1)} %broadcast_in_dim.34), dimensions={2} | concatenate | bytes 163840 | tf_op jit(solution)/shard_map/concatenate | solution.py:219
  2.9 0.6 broadcast_in_dim.39.live_ref
  3.5 3.4 %shard_map.82 = (f32[256,1024]{1,0:T(8,128)}, f32[256,1024]{1,0:T(8,128)}) custom-call(bf16[256,1024]{1,0:T(8,128)(2,1)} %bitcast.40, bf16[64,128]{1,0:T(8,128)(2,1)} %mw_ref.1, f32[1,128]{1,0:T(1,128)} %broadcast_in_dim.39.live_ref), custom_call_target="tpu_custom_call" | custom-call | tf_op jit(solution)/shard_map/pallas_call | solution.py:70
  6.9 1.8 %copy.23 = f32[16,16,1024]{2,0,1:T(8,128)S(1)} copy(f32[16,16,1024]{2,1,0:T(8,128)} %bitcast.39) | data formatting | bytes 2097152 | tf_op jit(solution)/shard_map/reshape | solution.py:240
  9.0 0.6 %iota_compare_fusion.1 = (pred[12,12,20]{2,1,0:T(8,128)(4,1)}, pred[12,12,20]{2,1,0:T(8,128)(4,1)}) fusion(), kind=kLoop, calls=%fused_computation.23 | loop fusion | flops 5760 | bytes 5760 | tf_op jit(solution)/shard_map/jit(_pad)/pad | solution.py:260
  10.3 0.8 %concatenate.43 = f32[16,16,1280]{2,0,1:T(8,128)S(1)} concatenate(f32[16,16,64]{2,0,1:T(8,128)S(1)} %get-tuple-element.22, f32[16,16,1024]{2,0,1:T(8,128)S(1)} %copy.23, f32[16,16,64]{2,0,1:T(8,128)S(1)} %get-tuple-element.21, f32[16,16,128]{2,0,1:T(8,128)S(1)} %broadcast_in_dim.40), dimensions={2} | concatenate | bytes 2621440 | tf_op jit(solution)/shard_map/concatenate | solution.py:245
  11.2 0.6 slice.106
  13.6 1.3 %collective-permute-start.3 = (f32[32,1280]{1,0:T(8,128)S(1)}, f32[32,1280]{1,0:T(8,128)S(1)}, u32[]{:S(2)}, u32[]{:S(2)}) collective-permute-start(f32[32,1280]{1,0:T(8,128)S(1)} %pad_maximum_fusion.5), channel_id=1, source_target_pairs={{2,0},{3,1},{6,4},{7,5},{10,8},{11,9},{14,12},{15,13},{18,16},{19,... | collective-permute-start | bytes 491528 | tf_op jit(solution)/shard_map/ppermute | solution.py:180
  14.9 4.6 %collective-permute-start.2 = (f32[32,1280]{1,0:T(8,128)S(1)}, f32[32,1280]{1,0:T(8,128)S(1)}, u32[]{:S(2)}, u32[]{:S(2)}) collective-permute-start(f32[32,1280]{1,0:T(8,128)S(1)} %pad_maximum_fusion.4), channel_id=1, source_target_pairs={{0,2},{1,3},{4,6},{5,7},{8,10},{9,11},{12,14},{13,15},{16,18},{17,... | collective-permute-start | bytes 491528 | tf_op jit(solution)/shard_map/ppermute | solution.py:179
  19.5 3.9 %shard_map.83 = (bf16[9,384,256]{2,1,0:T(8,128)(2,1)}, bf16[9,384,256]{2,1,0:T(8,128)(2,1)}) custom-call(bf16[64,1728]{1,0:T(8,128)(2,1)} %wa_raw.1, bf16[64,1728]{1,0:T(8,128)(2,1)} %wb_raw.1), custom_call_target="tpu_custom_call" | custom-call | flops 905969664 | bytes 3538944 | tf_op jit(solution)/shard_map/pallas_call | solution.py:85
  23.4 0.6 %iota_add_fusion = s32[12,12,10]{2,1,0:T(8,128)} fusion(s32[]{:T(128)S(6)} %select_n.96), kind=kLoop, calls=%fused_computation.30 | loop fusion | flops 1440 | bytes 5764 | tf_op jit(solution)/shard_map/dynamic_slice | solution.py:261
  24.5 1.3 %collective-permute-start.5 = (f32[42,1280]{1,0:T(8,128)S(1)}, f32[42,1280]{1,0:T(8,128)S(1)}, u32[]{:S(2)}, u32[]{:S(2)}) collective-permute-start(f32[42,1280]{1,0:T(8,128)S(1)} %pad_maximum_fusion.3), channel_id=1, source_target_pairs={{4,0},{8,4},{12,8},{5,1},{9,5},{13,9},{6,2},{10,6},{14,10},{7,3},{... | collective-permute-start | bytes 645128 | tf_op jit(solution)/shard_map/ppermute | solution.py:180
  25.9 5.4 %collective-permute-start.4 = (f32[42,1280]{1,0:T(8,128)S(1)}, f32[42,1280]{1,0:T(8,128)S(1)}, u32[]{:S(2)}, u32[]{:S(2)}) collective-permute-start(f32[42,1280]{1,0:T(8,128)S(1)} %pad_maximum_fusion.2), channel_id=1, source_target_pairs={{0,4},{4,8},{8,12},{1,5},{5,9},{9,13},{2,6},{6,10},{10,14},{3,7},{... | collective-permute-start | bytes 645128 | tf_op jit(solution)/shard_map/ppermute | solution.py:179
  31.3 0.9 %fusion.9.spread_ref = bf16[488,112]{1,0:T(8,128)(2,1)} fusion(s32[488]{0:T(512)S(1)} %fusion.29, pred[488]{0:T(512)(128)(4,1)S(1)} %compare_and_fusion), kind=kLoop, calls=%fused_computation.17 | loop fusion | flops 163968 | bytes 111752 | tf_op jit(solution)/shard_map/convert_element_type | solution.py:276
  32.2 2.9 %collective-permute-done.5 = f32[42,1280]{1,0:T(8,128)S(1)} collective-permute-done((f32[42,1280]{1,0:T(8,128)S(1)}, f32[42,1280]{1,0:T(8,128)S(1)}, u32[]{:S(2)}, u32[]{:S(2)}) %collective-permute-start.5) | collective-permute-done | bytes 215072 | tf_op jit(solution)/shard_map/ppermute | solution.py:180
  35.2 1.1 %collective-permute-done.4 = f32[42,1280]{1,0:T(8,128)S(1)} collective-permute-done((f32[42,1280]{1,0:T(8,128)S(1)}, f32[42,1280]{1,0:T(8,128)S(1)}, u32[]{:S(2)}, u32[]{:S(2)}) %collective-permute-start.4) | collective-permute-done | bytes 215072 | tf_op jit(solution)/shard_map/ppermute | solution.py:179
  36.3 0.7 %reshape.162 = f32[1,18,1280]{2,0,1:T(1,128)} reshape(f32[18,1280]{1,0:T(8,128)S(1)} %slice.121) | data formatting | bytes 184320 | tf_op jit(solution)/shard_map/reshape | solution.py:177
  37.6 1.2 %pad_maximum_fusion = f32[18,18,1280]{2,0,1:T(8,128)S(1)} fusion(f32[1,18,1280]{2,0,1:T(1,128)S(1)} %reshape.163, f32[16,1,1280]{2,0,1:T(8,128)S(1)} %slice_bitcast_fusion, f32[16,16,1280]{2,0,1:T(8,128)S(1)} %concatenate.43, f32[16,1,1280]{2,0,1:T(8,128)S(1)} %slice_bitcast_fusion.1, f32[1,18,1280]{2,0,1:T(1,128)} %reshape.162), kind=kLoop, calls=%fused_computation | loop fusion | flops 1658880 | bytes 3317760 | tf_op jit(solution)/shard_map/concatenate | solution.py:183
  38.8 0.6 copy.34
  39.4 1.5 %pad.19.clone = f32[18,24,1280]{2,1,0:T(8,128)} pad(f32[18,18,1280]{2,1,0:T(8,128)S(1)} %copy.34, f32[]{:T(128)} %constant.55.clone.1), padding=0_0x0_6x0_0 | pad | bytes 3870724 | tf_op jit(solution)/shard_map/jit(_pad)/pad | solution.py:270
  41.2 4.2 %fusion = f32[1,10,10,10,64]{4,0,3,2,1:T(1,128)S(1)} fusion(bf16[1,12,12,12,64]{4,3,2,1,0:T(8,128)(2,1)S(1)} %fusion.6, bf16[64,3,3,3,64]{4,3,2,1,0:T(4,128)(2,1)S(1)} %reshape.160), kind=kOutput, calls=%fused_computation.3 | convolution fusion | flops 221184000 | bytes 698368 | tf_op jit(solution)/shard_map/conv_general_dilated | solution.py:145
  46.4 0.7 %pad.18.hid_ref = bf16[112,640]{1,0:T(8,128)(2,1)} pad(bf16[100,640]{1,0:T(8,128)(2,1)S(1)} %reshape.161, bf16[]{:T(256)} %constant.53.clone.1), padding=0_12x0_0 | pad | bytes 271362 | tf_op jit(solution)/shard_map/jit(_pad)/pad | solution.py:268
  47.1 15.3 %shard_map.84 = bf16[256,1024]{1,0:T(8,128)(2,1)} custom-call(bf16[112,640]{1,0:T(8,128)(2,1)} %pad.18.hid_ref, bf16[488,112]{1,0:T(8,128)(2,1)} %fusion.9.spread_ref, f32[432,1280]{1,0:T(8,128)} %bitcast.38, f32[256,1024]{1,0:T(8,128)} %get-tuple-element.10.gb_ref, bf16[9,384,256]{2,1,0:T(8,128)(2,1)} %get-tuple-element.11.wa_ref, ...), custom_call_target="tpu_custom_call" | custom-call | tf_op jit(solution)/shard_map/pallas_call | solution.py:132
  (62 shorter events, 4.3 us)
Async XLA Ops:
  0.0 9.7 %copy-start.1 = (bf16[64,1728]{1,0:T(8,128)(2,1)S(1)}, bf16[64,1728]{1,0:T(8,128)(2,1)}, u32[]{:S(2)}) copy-start(bf16[64,1728]{1,0:T(8,128)(2,1)} %param.12) | copy-start | bytes 663556
  2.4 8.7 %collective-permute-start = (bf16[8,4,1280]{2,1,0:T(4,128)(2,1)S(1)}, bf16[8,4,1280]{2,1,0:T(4,128)(2,1)S(1)}, u32[]{:S(2)}, u32[]{:S(2)}) collective-permute-start(bf16[8,4,1280]{2,1,0:T(4,128)(2,1)S(1)} %concatenate.39), channel_id=1, source_target_pairs={{0,1},{1,0},{2,3},{3,2},{4,5},{5,4},{6,7},{7,6},{8,9},{9,8},{10,11... | collective-permute-start | bytes 245768 | tf_op jit(solution)/shard_map/ppermute | solution.py:220
  8.9 1.4 %collective-permute-start.1 = (f32[16,16,64]{2,0,1:T(8,128)S(1)}, f32[16,16,64]{2,0,1:T(8,128)S(1)}, u32[]{:S(2)}, u32[]{:S(2)}) collective-permute-start(f32[16,16,64]{2,0,1:T(8,128)S(1)} %slice_select_fusion), channel_id=1, source_target_pairs={{0,1},{1,0},{2,3},{3,2},{4,5},{5,4},{6,7},{7,6},{8,9},{9,8},{10,11... | collective-permute-start | bytes 196616 | tf_op jit(solution)/shard_map/ppermute | solution.py:243
  13.6 10.5 %collective-permute-start.3 = (f32[32,1280]{1,0:T(8,128)S(1)}, f32[32,1280]{1,0:T(8,128)S(1)}, u32[]{:S(2)}, u32[]{:S(2)}) collective-permute-start(f32[32,1280]{1,0:T(8,128)S(1)} %pad_maximum_fusion.5), channel_id=1, source_target_pairs={{2,0},{3,1},{6,4},{7,5},{10,8},{11,9},{14,12},{15,13},{18,16},{19,... | collective-permute-start | bytes 491528 | tf_op jit(solution)/shard_map/ppermute | solution.py:180
  14.9 9.2 %collective-permute-start.2 = (f32[32,1280]{1,0:T(8,128)S(1)}, f32[32,1280]{1,0:T(8,128)S(1)}, u32[]{:S(2)}, u32[]{:S(2)}) collective-permute-start(f32[32,1280]{1,0:T(8,128)S(1)} %pad_maximum_fusion.4), channel_id=1, source_target_pairs={{0,2},{1,3},{4,6},{5,7},{8,10},{9,11},{12,14},{13,15},{16,18},{17,... | collective-permute-start | bytes 491528 | tf_op jit(solution)/shard_map/ppermute | solution.py:179
  24.5 10.5 %collective-permute-start.5 = (f32[42,1280]{1,0:T(8,128)S(1)}, f32[42,1280]{1,0:T(8,128)S(1)}, u32[]{:S(2)}, u32[]{:S(2)}) collective-permute-start(f32[42,1280]{1,0:T(8,128)S(1)} %pad_maximum_fusion.3), channel_id=1, source_target_pairs={{4,0},{8,4},{12,8},{5,1},{9,5},{13,9},{6,2},{10,6},{14,10},{7,3},{... | collective-permute-start | bytes 645128 | tf_op jit(solution)/shard_map/ppermute | solution.py:180
  25.9 10.4 %collective-permute-start.4 = (f32[42,1280]{1,0:T(8,128)S(1)}, f32[42,1280]{1,0:T(8,128)S(1)}, u32[]{:S(2)}, u32[]{:S(2)}) collective-permute-start(f32[42,1280]{1,0:T(8,128)S(1)} %pad_maximum_fusion.2), channel_id=1, source_target_pairs={{0,4},{4,8},{8,12},{1,5},{5,9},{9,13},{2,6},{6,10},{10,14},{3,7},{... | collective-permute-start | bytes 645128 | tf_op jit(solution)/shard_map/ppermute | solution.py:179
  41.2 4.3 %copy-start = (s32[12,12,10]{2,1,0:T(8,128)S(1)}, s32[12,12,10]{2,1,0:T(8,128)}, u32[]{:S(2)}) copy-start(s32[12,12,10]{2,1,0:T(8,128)} %iota_add_fusion) | copy-start | bytes 17284
  41.2 4.3 %copy-start.2 = (pred[12,12,20]{2,1,0:T(8,128)(4,1)S(1)}, pred[12,12,20]{2,1,0:T(8,128)(4,1)}, u32[]{:S(2)}) copy-start(pred[12,12,20]{2,1,0:T(8,128)(4,1)} %get-tuple-element.23) | copy-start | bytes 8644
  41.2 4.3 %copy-start.3 = (pred[12,12,20]{2,1,0:T(8,128)(4,1)S(1)}, pred[12,12,20]{2,1,0:T(8,128)(4,1)}, u32[]{:S(2)}) copy-start(pred[12,12,20]{2,1,0:T(8,128)(4,1)} %get-tuple-element.24) | copy-start | bytes 8644

commit v9 on v8

--- a/solution.py
+++ b/solution.py
@@ -89,7 +89,19 @@
     )(weight_a, weight_b)
 
 
-def fine_kernel(hid_ref, spread_ref, ga_ref, gb_ref, wa_ref, wb_ref, out_ref, fin_ref, lvl_ref):
+def fine_kernel(
+    hid_ref, spread_ref, core_ref, yl_ref, yh_ref, xl_ref, xh_ref, gb_ref, wa_ref, wb_ref,
+    out_ref, fin_ref, lvl_ref, ga_ref,
+):
+    edge = core_ref.shape[0] // 16
+    ga_ref[...] = jnp.zeros(ga_ref.shape, jnp.float32)
+    for x in range(edge):
+        base = (x + 1) * STRIDE
+        ga_ref[base + 1 : base + 1 + edge, :] = core_ref[edge * x : edge * x + edge, :]
+        ga_ref[base : base + 1, :] = yl_ref[x : x + 1, :]
+        ga_ref[base + edge + 1 : base + edge + 2, :] = yh_ref[x : x + 1, :]
+    ga_ref[: edge + 2, :] = xl_ref[...]
+    ga_ref[(edge + 1) * STRIDE : (edge + 1) * STRIDE + edge + 2, :] = xh_ref[...]
     wide_c = hid_ref.shape[1]
     i = lax.broadcasted_iota(jnp.int32, (wide_c, LANES_F), 0)
     j = lax.broadcasted_iota(jnp.int32, (wide_c, LANES_F), 1)
@@ -121,22 +133,22 @@
     for k in range(LANES_B // 256):
         centre, acc = conv(lvl_ref, wb_ref, ROWS_B, k)
         lanes = slice(256 * k, 256 * k + 256)
-        edge = out_ref.shape[0] // 16
         for x in range(edge):
             mine = slice(x * STRIDE, x * STRIDE + 16)
             value = centre[mine] + silu(acc[mine]) * gb_ref[16 * x : 16 * x + 16, lanes]
             out_ref[16 * x : 16 * x + 16, lanes] = value.astype(out_ref.dtype)
 
 
-def fine_stage(hid, spread, gate_a, gate_b, band_a, band_b):
+def fine_stage(hid, spread, gate_parts, gate_b, band_a, band_b):
     return pl.pallas_call(
         fine_kernel,
         out_shape=jax.ShapeDtypeStruct(gate_b.shape, jnp.bfloat16),
         scratch_shapes=[
             pltpu.VMEM((ROWS_F, LANES_F), jnp.float32),
             pltpu.VMEM((ROWS_L, LANES_A), jnp.float32),
+            pltpu.VMEM((ROWS_A, LANES_A), jnp.float32),
         ],
-    )(hid, spread, gate_a, gate_b, band_a, band_b)
+    )(hid, spread, *gate_parts, gate_b, band_a, band_b)
 
 
 def convolve(padded, weight):
@@ -159,15 +171,12 @@
     return [(k + 1, k) for k in range(count - 1)]
 
 
-def grow_both(cells, gate, axis, dim, widths):
+def grow_both(cells, gate_head, gate_tail, axis, dim, width):
     count = lax.axis_size(axis)
-    lanes = gate.shape[-1]
-
-    def ends(arr, width):
-        size = arr.shape[dim]
-        return lax.slice_in_dim(arr, 0, width, axis=dim), lax.slice_in_dim(arr, size - width, size, axis=dim)
-
-    (cells_head, cells_tail), (gate_head, gate_tail) = ends(cells, widths[0]), ends(gate, widths[1])
+    lanes = gate_head.shape[-1]
+    size = cells.shape[dim]
+    cells_head = lax.slice_in_dim(cells, 0, width, axis=dim)
+    cells_tail = lax.slice_in_dim(cells, size - width, size, axis=dim)
 
     def pack(c, g):
         return jnp.concatenate([c.astype(jnp.float32).reshape(-1, lanes), g.reshape(-1, lanes)], 0)
@@ -178,10 +187,7 @@
 
     low = unpack(lax.ppermute(pack(cells_tail, gate_tail), axis, shift_pairs(count, True)))
     high = unpack(lax.ppermute(pack(cells_head, gate_head), axis, shift_pairs(count, False)))
-    return (
-        jnp.concatenate([low[0], cells, high[0]], axis=dim),
-        jnp.concatenate([low[1], gate, high[1]], axis=dim),
-    )
+    return jnp.concatenate([low[0], cells, high[0]], axis=dim), low[1], high[1]
 
 
 def grow(cells, axis, dim, width):
@@ -251,8 +257,12 @@
         ],
         axis=2,
     )
-    region, gate_a = grow_both(packed, gate_a, "gy", 1, (2, 1))
-    region, gate_a = grow_both(region, gate_a, "gx", 0, (2, 1))
+    region, side_low, side_high = grow_both(packed, gate_a[:, 0], gate_a[:, -1], "gy", 1, 2)
+    planes = [
+        jnp.concatenate([side_low[x : x + 1], gate_a[x], side_high[x : x + 1]], 0) for x in (0, edge - 1)
+    ]
+    region, end_low, end_high = grow_both(region, planes[0], planes[1], "gx", 0, 2)
+    gate_parts = (gate_a.reshape(edge * edge, -1), side_low, side_high, end_low, end_high)
     size = region.shape[0]
     volume = region[:, :, :flat_z].reshape(size, size, cells_z, channels)
     volume = jnp.pad(volume, ((0, 0), (0, 0), (2, 2), (0, 0)))
@@ -267,7 +277,6 @@
     cells = hidden.shape[0] * hidden.shape[1]
     hid = jnp.pad(hidden.reshape(cells, -1), ((0, ROWS_C - cells), (0, 0)))
 
-    gate_a = jnp.pad(gate_a, ((0, 0), (0, STRIDE - edge - 2), (0, 0))).reshape(-1, gate_a.shape[2])
 
     rows = jnp.arange(ROWS_F)
     fx, fy = rows // STRIDE, rows % STRIDE
@@ -277,7 +286,7 @@
         jnp.bfloat16
     )
     band_a, band_b = band_stage(fine_weight_a, fine_weight_b)
-    out = fine_stage(hid, spread, gate_a, gate_b, band_a, band_b)
+    out = fine_stage(hid, spread, gate_parts, gate_b, band_a, band_b)
     return out.reshape(field.shape)
 
 

time: 62.8 us -> 70.2 us (1.12); the launches traced: 62.4 us -> 69 us
  local copies, waits for them, and re-layouts: 10 us -> 17.5 us
  waiting for transfers between devices: 4.23 us -> 3.42 us
    slice x2 -> x4, local copies, waits for them, and re-layouts: 0.02 us -> 4.37 us  [unpack(): m[split:].reshape(gate_head.shape)]
    slice x0 -> x3, local copies, waits for them, and re-layouts: none -> 1.81 us  [the longest x1 0.89 us: body(): side_high[x:x + 1]]
    pad x1 -> x0, local copies, waits for them, and re-layouts: 1.52 us -> none  [body(): jnp.pad(gate_a, ((0, 0), (0, STRIDE - edge - 2), (0, 0)))]
    concatenate x1 -> x2, local copies, waits for them, and re-layouts: 0.79 us -> 2.24 us  [body(): jnp.concatenate([jnp.where(first, blank, face), gate_a, jnp.where(first,...]
    concatenate x1 -> x0, other arithmetic: 1.19 us -> none  [grow_both(): jnp.concatenate([low[1], gate, high[1]], axis=dim)]
    select_n x1, other arithmetic: 0.15 us -> 1.12 us  [body(): jnp.where(first, jnp.concatenate([mine, theirs], 1), jnp.concatenate([the...]
    slice x4, local copies, waits for them, and re-layouts: 0.03 us -> 0.93 us  [unpack(): m[:split].reshape(cells_head.shape).astype(cells.dtype)]
    reshape x5 -> x0, local copies, waits for them, and re-layouts: 0.79 us -> none  [the longest x4 0.77 us: unpack(): m[split:].reshape(gate_head.shape)]
  transfers between devices with their start and end apart: 6 -> 6, of which waited for: 3 -> 2; matrix products, arithmetic and copies ran while one was open for 10% -> 16% of each run, Pallas kernels for 12% -> 11%
where the time goes in v9:
time: 70.2 us; the launch traced here: 69 us
  Pallas kernels  22.7 us (32%)
  local copies, waits for them, and re-layouts  17.5 us (25%)
  starting transfers between devices  13.1 us (19%)
  other arithmetic  5.66 us (8%)
  matrix products  4.21 us (6%)
  waiting for transfers between devices  3.42 us (5%)
  between operations  2.44 us (3%)
    pallas_call x1, Pallas kernels, fine_stage(): pl.pallas_call(fine_kernel, out_shape=jax.ShapeDtypeStruct(gate_b.shape,...  15.4 us
    ppermute x2, starting transfers between devices, grow_both(): lax.ppermute(pack(cells_tail, gate_tail), axis, shift_pairs(count, True))  9.85 us
    slice x4, local copies, waits for them, and re-layouts, unpack(): m[split:].reshape(gate_head.shape)  4.37 us
    conv_general_dilated x1, matrix products, convolve(): lax.conv_general_dilated(padded[None], kernel, (1, 1, 1), 'VALID', dimens...  4.21 us
    pallas_call x1, Pallas kernels, band_stage(): pl.pallas_call(band_kernel, out_shape=(shape, shape), cost_estimate=pl.Co...  3.89 us
    pallas_call x1, Pallas kernels, gate_stage(): pl.pallas_call(gate_kernel, out_shape=(shape, shape))  3.4 us
    ppermute x2, starting transfers between devices, grow_both(): lax.ppermute(pack(cells_head, gate_head), axis, shift_pairs(count, False))  2.58 us
    concatenate x2, local copies, waits for them, and re-layouts, body(): jnp.concatenate([jnp.where(first, blank, face), gate_a, jnp.where(first,...  2.24 us
  transfers between devices with their start and end apart: 6, of which 2 were waited for; matrix products, arithmetic and copies ran while one was open for 16% of the time, Pallas kernels for 11%

profile of v9, /device:TPU:0, one launch (start us, length us, event | category | flops | bytes accessed | tf_op | source)
XLA Modules:
  0.0 69.0 jit_solution(508888871654149345)
XLA Ops:
  0.7 0.7 %convert_element_type.55 = bf16[8,4,16]{2,1,0:T(4,128)(2,1)S(1)} convert(s32[8,4,16]{2,1,0:T(4,128)} %param.9) | non-fusion elementwise | flops 512 | bytes 3072 | tf_op jit(solution)/shard_map/convert_element_type | solution.py:219
  1.4 1.0 %concatenate.40 = bf16[8,4,1280]{2,1,0:T(4,128)(2,1)S(1)} concatenate(bf16[8,4,1024]{2,1,0:T(4,128)(2,1)} %param.8, bf16[8,4,16]{2,1,0:T(4,128)(2,1)S(1)} %convert_element_type.55, bf16[8,4,1]{2,1,0:T(4,128)(2,1)S(1)} %broadcast_in_dim.35, bf16[8,4,239]{2,1,0:T(4,128)(2,1)S(1)} %broadcast_in_dim.36), dimensions={2} | concatenate | bytes 163840 | tf_op jit(solution)/shard_map/concatenate | solution.py:225
  3.4 3.4 %shard_map.82 = (f32[256,1024]{1,0:T(8,128)}, f32[256,1024]{1,0:T(8,128)}) custom-call(bf16[256,1024]{1,0:T(8,128)(2,1)} %bitcast.36, bf16[64,128]{1,0:T(8,128)(2,1)} %mw_ref.1, f32[1,128]{1,0:T(1,128)} %broadcast_in_dim.41.live_ref), custom_call_target="tpu_custom_call" | custom-call | tf_op jit(solution)/shard_map/pallas_call | solution.py:70
  6.8 1.9 %copy.10 = f32[16,16,1024]{2,0,1:T(8,128)S(1)} copy(f32[16,16,1024]{2,1,0:T(8,128)} %bitcast.35) | data formatting | bytes 2097152 | tf_op jit(solution)/shard_map/reshape | solution.py:246
  11.1 3.9 %shard_map.83 = (bf16[9,384,256]{2,1,0:T(8,128)(2,1)}, bf16[9,384,256]{2,1,0:T(8,128)(2,1)}) custom-call(bf16[64,1728]{1,0:T(8,128)(2,1)} %wa_raw.1, bf16[64,1728]{1,0:T(8,128)(2,1)} %wb_raw.1), custom_call_target="tpu_custom_call" | custom-call | flops 905969664 | bytes 3538944 | tf_op jit(solution)/shard_map/pallas_call | solution.py:85
  15.0 0.8 %concatenate.44 = f32[16,16,1280]{2,0,1:T(8,128)S(1)} concatenate(f32[16,16,64]{2,0,1:T(8,128)S(1)} %get-tuple-element.26, f32[16,16,1024]{2,0,1:T(8,128)S(1)} %copy.10, f32[16,16,64]{2,0,1:T(8,128)S(1)} %get-tuple-element.25, f32[16,16,128]{2,0,1:T(8,128)S(1)} %broadcast_in_dim.42), dimensions={2} | concatenate | bytes 2621440 | tf_op jit(solution)/shard_map/concatenate | solution.py:251
  15.9 1.2 %slice.126 = bf16[1,1,1]{2,1,0:T(2,128)(2,1)} slice(bf16[8,4,1280]{2,1,0:T(4,128)(2,1)} %collective-permute-done), slice={[0:1], [0:1], [1040:1041]} | slice | bytes 4 | tf_op jit(solution)/shard_map/slice | solution.py:228
  18.4 1.1 %maximum_select_fusion = bf16[8,8,1280]{2,1,0:T(8,128)(2,1)S(1)} fusion(bf16[8,4,1280]{2,1,0:T(4,128)(2,1)} %collective-permute-done, bf16[8,4,1280]{2,1,0:T(4,128)(2,1)S(1)} %concatenate.40, pred[]{:T(512)S(6)} %eq.18), kind=kLoop, calls=%fused_computation.19 | loop fusion | flops 737280 | bytes 327681 | tf_op jit(solution)/shard_map/jit(_where)/select_n | solution.py:227
  19.9 1.3 %collective-permute-start.3 = (f32[32,1280]{1,0:T(8,128)S(1)}, f32[32,1280]{1,0:T(8,128)S(1)}, u32[]{:S(2)}, u32[]{:S(2)}) collective-permute-start(f32[32,1280]{1,0:T(8,128)S(1)} %pad_maximum_fusion.4), channel_id=1, source_target_pairs={{2,0},{3,1},{6,4},{7,5},{10,8},{11,9},{14,12},{15,13},{18,16},{19,... | collective-permute-start | bytes 491528 | tf_op jit(solution)/shard_map/ppermute | solution.py:189
  21.2 4.9 %collective-permute-start.2 = (f32[32,1280]{1,0:T(8,128)S(1)}, f32[32,1280]{1,0:T(8,128)S(1)}, u32[]{:S(2)}, u32[]{:S(2)}) collective-permute-start(f32[32,1280]{1,0:T(8,128)S(1)} %pad_maximum_fusion.3), channel_id=1, source_target_pairs={{0,2},{1,3},{4,6},{5,7},{8,10},{9,11},{12,14},{13,15},{16,18},{17,... | collective-permute-start | bytes 491528 | tf_op jit(solution)/shard_map/ppermute | solution.py:188
  26.2 2.2 %collective-permute-done.3 = f32[32,1280]{1,0:T(8,128)S(1)} collective-permute-done((f32[32,1280]{1,0:T(8,128)S(1)}, f32[32,1280]{1,0:T(8,128)S(1)}, u32[]{:S(2)}, u32[]{:S(2)}) %collective-permute-start.3) | collective-permute-done | bytes 163872 | tf_op jit(solution)/shard_map/ppermute | solution.py:189
  28.5 1.2 %collective-permute-done.2 = f32[32,1280]{1,0:T(8,128)S(1)} collective-permute-done((f32[32,1280]{1,0:T(8,128)S(1)}, f32[32,1280]{1,0:T(8,128)S(1)}, u32[]{:S(2)}, u32[]{:S(2)}) %collective-permute-start.2) | collective-permute-done | bytes 163872 | tf_op jit(solution)/shard_map/ppermute | solution.py:188
  30.5 0.9 %fusion.38 = (f32[1,1280]{1,0:T(1,128)S(1)}, f32[1,1280]{1,0:T(1,128)S(1)}) fusion(f32[32,1280]{1,0:T(8,128)} %copy-done.4), kind=kLoop, calls=%fused_computation.94 | loop fusion | bytes 20480 | tf_op jit(solution)/shard_map/slice | solution.py:262
  31.4 0.8 %fusion.37 = (f32[1,1280]{1,0:T(1,128)S(1)}, f32[1,1280]{1,0:T(1,128)S(1)}) fusion(f32[32,1280]{1,0:T(8,128)} %copy-done.6), kind=kLoop, calls=%fused_computation.93 | loop fusion | bytes 20480 | tf_op jit(solution)/shard_map/slice | solution.py:262
  32.2 1.3 %collective-permute-start.5 = (f32[42,1280]{1,0:T(8,128)S(1)}, f32[42,1280]{1,0:T(8,128)}, u32[]{:S(2)}, u32[]{:S(2)}) collective-permute-start(f32[42,1280]{1,0:T(8,128)S(1)} %pad_maximum_fusion.2), channel_id=1, source_target_pairs={{4,0},{8,4},{12,8},{5,1},{9,5},{13,9},{6,2},{10,6},{14,10},{7,3},{... | collective-permute-start | bytes 645128 | tf_op jit(solution)/shard_map/ppermute | solution.py:189
  33.5 5.0 %collective-permute-start.4 = (f32[42,1280]{1,0:T(8,128)S(1)}, f32[42,1280]{1,0:T(8,128)S(1)}, u32[]{:S(2)}, u32[]{:S(2)}) collective-permute-start(f32[42,1280]{1,0:T(8,128)S(1)} %pad_maximum_fusion.1), channel_id=1, source_target_pairs={{0,4},{4,8},{8,12},{1,5},{5,9},{9,13},{2,6},{6,10},{10,14},{3,7},{... | collective-permute-start | bytes 645128 | tf_op jit(solution)/shard_map/ppermute | solution.py:188
  38.6 0.8 %fusion.9.spread_ref = bf16[488,112]{1,0:T(8,128)(2,1)} fusion(s32[488]{0:T(512)S(1)} %copy-done.9, pred[488]{0:T(512)(128)(4,1)S(1)} %copy-done.10), kind=kLoop, calls=%fused_computation.16 | loop fusion | flops 163968 | bytes 111752 | tf_op jit(solution)/shard_map/convert_element_type | solution.py:285
  39.5 1.5 %concatenate.53.core_ref = f32[256,1280]{1,0:T(8,128)} concatenate(f32[256,64]{1,0:T(8,128)S(1)} %bitcast.38, f32[256,1024]{1,0:T(8,128)S(1)} %copy-done, f32[256,64]{1,0:T(8,128)S(1)} %bitcast.37, f32[256,128]{1,0:T(8,128)S(1)} %broadcast_in_dim.44), dimensions={1} | concatenate | bytes 2621440 | tf_op jit(solution)/shard_map/concatenate | solution.py:251
  41.6 1.5 %slice.145.yl_ref = f32[16,1280]{1,0:T(8,128)} slice(f32[32,1280]{1,0:T(8,128)} %copy-done.6), slice={[16:32], [0:1280]} | slice | bytes 163840 | tf_op jit(solution)/shard_map/slice | solution.py:186
  43.1 0.9 %slice.163 = bf16[24,1280]{1,0:T(8,128)(2,1)S(1)} slice(f32[42,1280]{1,0:T(8,128)} %collective-permute-done.5), slice={[0:24], [0:1280]} | slice | bytes 122880 | tf_op jit(solution)/shard_map/slice | solution.py:186
  45.5 4.2 %fusion = f32[1,10,10,10,64]{4,0,3,2,1:T(1,128)S(1)} fusion(bf16[1,12,12,12,64]{4,3,2,1,0:T(8,128)(2,1)S(1)} %fusion.6, bf16[64,3,3,3,64]{4,3,2,1,0:T(4,128)(2,1)S(1)} %reshape.133), kind=kOutput, calls=%fused_computation.2 | convolution fusion | flops 221184000 | bytes 698368 | tf_op jit(solution)/shard_map/conv_general_dilated | solution.py:157
  50.7 0.7 pad.14.hid_ref
  51.4 1.6 %slice.148.xh_ref = f32[18,1280]{1,0:T(8,128)} slice(f32[42,1280]{1,0:T(8,128)} %collective-permute-done.5), slice={[24:42], [0:1280]} | slice | bytes 184320 | tf_op jit(solution)/shard_map/slice | solution.py:186
  53.6 15.4 %shard_map.84 = bf16[256,1024]{1,0:T(8,128)(2,1)} custom-call(bf16[112,640]{1,0:T(8,128)(2,1)} %pad.14.hid_ref, bf16[488,112]{1,0:T(8,128)(2,1)} %fusion.9.spread_ref, f32[256,1280]{1,0:T(8,128)} %concatenate.53.core_ref, f32[16,1280]{1,0:T(8,128)} %slice.145.yl_ref, f32[16,1280]{1,0:T(8,128)} %slice.146.yh_ref, f32[18,1280]{1,0:T(8,128)} %slice.147.xl_ref, ...), custom_call_target="tpu_custom_call" | custom-call | tf_op jit(solution)/shard_map/pallas_call | solution.py:143
  (77 shorter events, 8.4 us)
Async XLA Ops:
  2.4 13.5 %collective-permute-start = (bf16[8,4,1280]{2,1,0:T(4,128)(2,1)S(1)}, bf16[8,4,1280]{2,1,0:T(4,128)(2,1)}, u32[]{:S(2)}, u32[]{:S(2)}) collective-permute-start(bf16[8,4,1280]{2,1,0:T(4,128)(2,1)S(1)} %concatenate.40), channel_id=1, source_target_pairs={{0,1},{1,0},{2,3},{3,2},{4,5},{5,4},{6,7},{7,6},{8,9},{9,8},{10,11... | collective-permute-start | bytes 245768 | tf_op jit(solution)/shard_map/ppermute | solution.py:226
  6.8 3.9 %copy-start.1 = (bf16[64,1728]{1,0:T(8,128)(2,1)S(1)}, bf16[64,1728]{1,0:T(8,128)(2,1)}, u32[]{:S(2)}) copy-start(bf16[64,1728]{1,0:T(8,128)(2,1)} %param.12) | copy-start | bytes 663556
  8.8 6.2 %collective-permute-start.1 = (f32[16,16,64]{2,0,1:T(8,128)S(1)}, f32[16,16,64]{2,0,1:T(8,128)S(1)}, u32[]{:S(2)}, u32[]{:S(2)}) collective-permute-start(f32[16,16,64]{2,0,1:T(8,128)S(1)} %slice_select_fusion), channel_id=1, source_target_pairs={{0,1},{1,0},{2,3},{3,2},{4,5},{5,4},{6,7},{7,6},{8,9},{9,8},{10,11... | collective-permute-start | bytes 196616 | tf_op jit(solution)/shard_map/ppermute | solution.py:249
  19.9 8.6 %collective-permute-start.3 = (f32[32,1280]{1,0:T(8,128)S(1)}, f32[32,1280]{1,0:T(8,128)S(1)}, u32[]{:S(2)}, u32[]{:S(2)}) collective-permute-start(f32[32,1280]{1,0:T(8,128)S(1)} %pad_maximum_fusion.4), channel_id=1, source_target_pairs={{2,0},{3,1},{6,4},{7,5},{10,8},{11,9},{14,12},{15,13},{18,16},{19,... | collective-permute-start | bytes 491528 | tf_op jit(solution)/shard_map/ppermute | solution.py:189
  21.2 8.5 %collective-permute-start.2 = (f32[32,1280]{1,0:T(8,128)S(1)}, f32[32,1280]{1,0:T(8,128)S(1)}, u32[]{:S(2)}, u32[]{:S(2)}) collective-permute-start(f32[32,1280]{1,0:T(8,128)S(1)} %pad_maximum_fusion.3), channel_id=1, source_target_pairs={{0,2},{1,3},{4,6},{5,7},{8,10},{9,11},{12,14},{13,15},{16,18},{17,... | collective-permute-start | bytes 491528 | tf_op jit(solution)/shard_map/ppermute | solution.py:188
  26.2 12.3 %copy-start.9 = (s32[488]{0:T(512)S(1)}, s32[488]{0:T(512)}, u32[]{:S(2)}) copy-start(s32[488]{0:T(512)} %fusion.29) | copy-start | bytes 5860
  26.2 12.3 %copy-start.10 = (pred[488]{0:T(512)(128)(4,1)S(1)}, pred[488]{0:T(512)(128)(4,1)}, u32[]{:S(2)}) copy-start(pred[488]{0:T(512)(128)(4,1)} %compare_and_fusion) | copy-start | bytes 1468
  28.5 1.2 %copy-start.4 = (f32[32,1280]{1,0:T(8,128)}, f32[32,1280]{1,0:T(8,128)S(1)}, u32[]{:S(2)}) copy-start(f32[32,1280]{1,0:T(8,128)S(1)} %collective-permute-done.3) | copy-start | bytes 491524
  29.7 0.7 copy-start.6
  30.4 9.1 %copy-start = (f32[256,1024]{1,0:T(8,128)S(1)}, f32[256,1024]{1,0:T(8,128)}, u32[]{:S(2)}) copy-start(f32[256,1024]{1,0:T(8,128)} %get-tuple-element.9) | copy-start | bytes 3145732
  32.2 10.9 %collective-permute-start.5 = (f32[42,1280]{1,0:T(8,128)S(1)}, f32[42,1280]{1,0:T(8,128)}, u32[]{:S(2)}, u32[]{:S(2)}) collective-permute-start(f32[42,1280]{1,0:T(8,128)S(1)} %pad_maximum_fusion.2), channel_id=1, source_target_pairs={{4,0},{8,4},{12,8},{5,1},{9,5},{13,9},{6,2},{10,6},{14,10},{7,3},{... | collective-permute-start | bytes 645128 | tf_op jit(solution)/shard_map/ppermute | solution.py:189
  33.5 10.5 %collective-permute-start.4 = (f32[42,1280]{1,0:T(8,128)S(1)}, f32[42,1280]{1,0:T(8,128)S(1)}, u32[]{:S(2)}, u32[]{:S(2)}) collective-permute-start(f32[42,1280]{1,0:T(8,128)S(1)} %pad_maximum_fusion.1), channel_id=1, source_target_pairs={{0,4},{4,8},{8,12},{1,5},{5,9},{9,13},{2,6},{6,10},{10,14},{3,7},{... | collective-permute-start | bytes 645128 | tf_op jit(solution)/shard_map/ppermute | solution.py:188
  39.5 1.5 %copy-start.5 = (f32[32,1280]{1,0:T(8,128)S(1)}, f32[32,1280]{1,0:T(8,128)}, u32[]{:S(2)}) copy-start(f32[32,1280]{1,0:T(8,128)} %copy-done.4) | copy-start | bytes 491524
  44.1 0.7 %copy-start.2 = (f32[42,1280]{1,0:T(8,128)}, f32[42,1280]{1,0:T(8,128)S(1)}, u32[]{:S(2)}) copy-start(f32[42,1280]{1,0:T(8,128)S(1)} %collective-permute-done.4) | copy-start | bytes 645124
  45.5 4.2 %copy-start.7 = (pred[12,12,20]{2,1,0:T(8,128)(4,1)S(1)}, pred[12,12,20]{2,1,0:T(8,128)(4,1)}, u32[]{:S(2)}) copy-start(pred[12,12,20]{2,1,0:T(8,128)(4,1)} %get-tuple-element.27) | copy-start | bytes 8644
  45.5 4.2 %copy-start.8 = (pred[12,12,20]{2,1,0:T(8,128)(4,1)S(1)}, pred[12,12,20]{2,1,0:T(8,128)(4,1)}, u32[]{:S(2)}) copy-start(pred[12,12,20]{2,1,0:T(8,128)(4,1)} %get-tuple-element.28) | copy-start | bytes 8644
  50.0 2.9 %copy-start.3 = (f32[42,1280]{1,0:T(8,128)S(1)}, f32[42,1280]{1,0:T(8,128)}, u32[]{:S(2)}) copy-start(f32[42,1280]{1,0:T(8,128)} %copy-done.2) | copy-start | bytes 645124

commit v10 on v8

--- a/solution.py
+++ b/solution.py
@@ -57,10 +57,11 @@
         keep = select((128, 128), lambda r, c: (r >> 6) == (c >> 6))
         tiles.append(jnp.where(keep, tall, 0.0).astype(jnp.bfloat16))
     live = live_ref[...]
+    swap = select((256, 256), lambda r, c: c == (r & 15) * 16 + (r >> 4)).astype(jnp.bfloat16)
+    swapped = jnp.dot(swap, field_ref[...], preferred_element_type=jnp.float32).astype(jnp.bfloat16)
     for k in range(field_ref.shape[1] // 128):
         lanes = slice(128 * k, 128 * k + 128)
-        x = field_ref[:, lanes]
-        for tile, out in zip(tiles, (ga_ref, gb_ref)):
+        for tile, out, x in zip(tiles, (ga_ref, gb_ref), (swapped[:, lanes], field_ref[:, lanes])):
             v = jnp.dot(x, tile, preferred_element_type=jnp.float32)
             out[:, lanes] = live / (1.0 + jnp.exp(-v))
 
@@ -202,7 +203,7 @@
     cells_z = flat_z // channels
     edge = field.shape[0]
     half = edge // 2
-    assert lax.axis_size("gz") == 2 and rows_x == half and 2 * rows_y == half
+    assert lax.axis_size("gz") == 2 and rows_x == half and 2 * rows_y == half and edge == 16
     lanes = 256
     zside = lax.axis_index("gz")
     first = zside == 0
@@ -237,7 +238,7 @@
 
     live_row = jnp.broadcast_to(live.astype(jnp.float32), (1, 128))
     gate_a, gate_b = gate_stage(field.reshape(edge * edge, -1), mod_weight, live_row)
-    gate_a = gate_a.reshape(field.shape)
+    gate_a = gate_a.reshape(field.shape).transpose(1, 0, 2)
     width = edge * channels
     face = jnp.where(first, gate_a[:, :, width - channels :], gate_a[:, :, :channels])
     face = lax.ppermute(face, "gz", [(0, 1), (1, 0)])

time: 62.8 us -> 63 us (level)
  other arithmetic: 5.55 us -> 6.61 us
    reshape x1 -> x0, local copies, waits for them, and re-layouts: 1.84 us -> none  [body(): gate_a = gate_a.reshape(field.shape)]
    reshape x1, local copies, waits for them, and re-layouts: 0.34 us -> 1.53 us  [convolve(): weight.reshape(channels, 3, 3, 3, channels).transpose(1, 2, 3, 0, 4)]
    select_n x1, other arithmetic: 0.1 us -> 1.16 us  [body(): jnp.where(first, gate_a[:, :, width - channels:], gate_a[:, :, :channels])]
  transfers between devices with their start and end apart: 6 -> 6, of which waited for: 3 -> 2; matrix products, arithmetic and copies ran while one was open for 10% -> 10% of each run, Pallas kernels for 12% -> 12%
where the time goes in v10:
time: 63 us; the launch traced here: 62.6 us
  Pallas kernels  22.7 us (36%)
  starting transfers between devices  13.5 us (21%)
  local copies, waits for them, and re-layouts  9.4 us (15%)
  other arithmetic  6.61 us (10%)
  matrix products  4.22 us (7%)
  waiting for transfers between devices  3.66 us (6%)
  between operations  2.42 us (4%)
    pallas_call x1, Pallas kernels, fine_stage(): pl.pallas_call(fine_kernel, out_shape=jax.ShapeDtypeStruct(gate_b.shape,...  15.3 us
    ppermute x2, starting transfers between devices, grow_both(): lax.ppermute(pack(cells_tail, gate_tail), axis, shift_pairs(count, True))  10.3 us
    conv_general_dilated x1, matrix products, convolve(): lax.conv_general_dilated(padded[None], kernel, (1, 1, 1), 'VALID', dimens...  4.22 us
    pallas_call x1, Pallas kernels, band_stage(): pl.pallas_call(band_kernel, out_shape=(shape, shape), cost_estimate=pl.Co...  3.92 us
    pallas_call x1, Pallas kernels, gate_stage(): pl.pallas_call(gate_kernel, out_shape=(shape, shape))  3.52 us
    ppermute x2, starting transfers between devices, grow_both(): lax.ppermute(pack(cells_head, gate_head), axis, shift_pairs(count, False))  2.58 us
    ppermute x2, waiting for transfers between devices, grow_both(): lax.ppermute(pack(cells_head, gate_head), axis, shift_pairs(count, False))  2.57 us
    reshape x1, local copies, waits for them, and re-layouts, convolve(): weight.reshape(channels, 3, 3, 3, channels).transpose(1, 2, 3, 0, 4)  1.53 us
  transfers between devices with their start and end apart: 6, of which 2 were waited for; matrix products, arithmetic and copies ran while one was open for 10% of the time, Pallas kernels for 12%

profile of v10, /device:TPU:0, one launch (start us, length us, event | category | flops | bytes accessed | tf_op | source)
XLA Modules:
  0.0 62.6 jit_solution(11164329529136405621)
XLA Ops:
  0.7 0.7 %convert_element_type.57 = bf16[8,4,16]{2,1,0:T(4,128)(2,1)S(1)} convert(s32[8,4,16]{2,1,0:T(4,128)} %param.9) | non-fusion elementwise | flops 512 | bytes 3072 | tf_op jit(solution)/shard_map/convert_element_type | solution.py:214
  1.4 1.0 %concatenate.39 = bf16[8,4,1280]{2,1,0:T(4,128)(2,1)S(1)} concatenate(bf16[8,4,1024]{2,1,0:T(4,128)(2,1)} %param.8, bf16[8,4,16]{2,1,0:T(4,128)(2,1)S(1)} %convert_element_type.57, bf16[8,4,1]{2,1,0:T(4,128)(2,1)S(1)} %broadcast_in_dim.33, bf16[8,4,239]{2,1,0:T(4,128)(2,1)S(1)} %broadcast_in_dim.34), dimensions={2} | concatenate | bytes 163840 | tf_op jit(solution)/shard_map/concatenate | solution.py:220
  2.9 0.6 broadcast_in_dim.39.live_ref
  3.5 3.5 %shard_map.82 = (f32[256,1024]{1,0:T(8,128)}, f32[256,1024]{1,0:T(8,128)}) custom-call(bf16[256,1024]{1,0:T(8,128)(2,1)} %bitcast.43, bf16[64,128]{1,0:T(8,128)(2,1)} %mw_ref.1, f32[1,128]{1,0:T(1,128)} %broadcast_in_dim.39.live_ref), custom_call_target="tpu_custom_call" | custom-call | tf_op jit(solution)/shard_map/pallas_call | solution.py:71
  7.0 1.2 %slice_select_fusion = f32[16,16,64]{2,0,1:T(8,128)S(1)} fusion(f32[16,16,1024]{2,0,1:T(8,128)} %bitcast.41, pred[]{:T(512)S(6)} %eq.18), kind=kLoop, calls=%fused_computation.25 | loop fusion | flops 16384 | bytes 196609 | tf_op jit(solution)/shard_map/jit(_where)/select_n | solution.py:243
  8.3 0.6 %iota_compare_fusion.1 = (pred[12,12,20]{2,1,0:T(8,128)(4,1)}, pred[12,12,20]{2,1,0:T(8,128)(4,1)}) fusion(), kind=kLoop, calls=%fused_computation.23 | loop fusion | flops 5760 | bytes 5760 | tf_op jit(solution)/shard_map/jit(_pad)/pad | solution.py:261
  8.9 1.5 %reshape.160 = bf16[64,3,3,3,64]{4,3,2,1,0:T(4,128)(2,1)S(1)} reshape(bf16[64,1728]{1,0:T(8,128)(2,1)} %param.12) | data formatting | bytes 442368 | tf_op jit(solution)/shard_map/reshape | solution.py:145
  10.6 0.8 %concatenate.43 = f32[16,16,1280]{2,0,1:T(8,128)S(1)} concatenate(f32[16,16,64]{2,0,1:T(8,128)S(1)} %get-tuple-element.22, f32[16,16,1024]{2,0,1:T(8,128)S(1)} %bitcast.42, f32[16,16,64]{2,0,1:T(8,128)S(1)} %get-tuple-element.21, f32[16,16,128]{2,0,1:T(8,128)S(1)} %broadcast_in_dim.40), dimensions={2} | concatenate | bytes 2621440 | tf_op jit(solution)/shard_map/concatenate | solution.py:246
  11.4 0.6 slice.106
  13.8 1.3 %collective-permute-start.3 = (f32[32,1280]{1,0:T(8,128)S(1)}, f32[32,1280]{1,0:T(8,128)S(1)}, u32[]{:S(2)}, u32[]{:S(2)}) collective-permute-start(f32[32,1280]{1,0:T(8,128)S(1)} %pad_maximum_fusion.5), channel_id=1, source_target_pairs={{2,0},{3,1},{6,4},{7,5},{10,8},{11,9},{14,12},{15,13},{18,16},{19,... | collective-permute-start | bytes 491528 | tf_op jit(solution)/shard_map/ppermute | solution.py:181
  15.1 4.9 %collective-permute-start.2 = (f32[32,1280]{1,0:T(8,128)S(1)}, f32[32,1280]{1,0:T(8,128)S(1)}, u32[]{:S(2)}, u32[]{:S(2)}) collective-permute-start(f32[32,1280]{1,0:T(8,128)S(1)} %pad_maximum_fusion.4), channel_id=1, source_target_pairs={{0,2},{1,3},{4,6},{5,7},{8,10},{9,11},{12,14},{13,15},{16,18},{17,... | collective-permute-start | bytes 491528 | tf_op jit(solution)/shard_map/ppermute | solution.py:180
  20.0 3.9 %shard_map.83 = (bf16[9,384,256]{2,1,0:T(8,128)(2,1)}, bf16[9,384,256]{2,1,0:T(8,128)(2,1)}) custom-call(bf16[64,1728]{1,0:T(8,128)(2,1)} %wa_raw.1, bf16[64,1728]{1,0:T(8,128)(2,1)} %wb_raw.1), custom_call_target="tpu_custom_call" | custom-call | flops 905969664 | bytes 3538944 | tf_op jit(solution)/shard_map/pallas_call | solution.py:86
  23.9 0.6 %iota_add_fusion = s32[12,12,10]{2,1,0:T(8,128)} fusion(s32[]{:T(128)S(6)} %select_n.96), kind=kLoop, calls=%fused_computation.30 | loop fusion | flops 1440 | bytes 5764 | tf_op jit(solution)/shard_map/dynamic_slice | solution.py:262
  25.0 1.3 %collective-permute-start.5 = (f32[42,1280]{1,0:T(8,128)S(1)}, f32[42,1280]{1,0:T(8,128)S(1)}, u32[]{:S(2)}, u32[]{:S(2)}) collective-permute-start(f32[42,1280]{1,0:T(8,128)S(1)} %pad_maximum_fusion.3), channel_id=1, source_target_pairs={{4,0},{8,4},{12,8},{5,1},{9,5},{13,9},{6,2},{10,6},{14,10},{7,3},{... | collective-permute-start | bytes 645128 | tf_op jit(solution)/shard_map/ppermute | solution.py:181
  26.3 5.5 %collective-permute-start.4 = (f32[42,1280]{1,0:T(8,128)S(1)}, f32[42,1280]{1,0:T(8,128)S(1)}, u32[]{:S(2)}, u32[]{:S(2)}) collective-permute-start(f32[42,1280]{1,0:T(8,128)S(1)} %pad_maximum_fusion.2), channel_id=1, source_target_pairs={{0,4},{4,8},{8,12},{1,5},{5,9},{9,13},{2,6},{6,10},{10,14},{3,7},{... | collective-permute-start | bytes 645128 | tf_op jit(solution)/shard_map/ppermute | solution.py:180
  31.8 0.9 %fusion.9.spread_ref = bf16[488,112]{1,0:T(8,128)(2,1)} fusion(s32[488]{0:T(512)S(1)} %fusion.29, pred[488]{0:T(512)(128)(4,1)S(1)} %compare_and_fusion), kind=kLoop, calls=%fused_computation.17 | loop fusion | flops 163968 | bytes 111752 | tf_op jit(solution)/shard_map/convert_element_type | solution.py:277
  32.6 2.6 %collective-permute-done.5 = f32[42,1280]{1,0:T(8,128)S(1)} collective-permute-done((f32[42,1280]{1,0:T(8,128)S(1)}, f32[42,1280]{1,0:T(8,128)S(1)}, u32[]{:S(2)}, u32[]{:S(2)}) %collective-permute-start.5) | collective-permute-done | bytes 215072 | tf_op jit(solution)/shard_map/ppermute | solution.py:181
  35.3 1.1 %collective-permute-done.4 = f32[42,1280]{1,0:T(8,128)S(1)} collective-permute-done((f32[42,1280]{1,0:T(8,128)S(1)}, f32[42,1280]{1,0:T(8,128)S(1)}, u32[]{:S(2)}, u32[]{:S(2)}) %collective-permute-start.4) | collective-permute-done | bytes 215072 | tf_op jit(solution)/shard_map/ppermute | solution.py:180
  36.4 0.7 %reshape.162 = f32[1,18,1280]{2,0,1:T(1,128)} reshape(f32[18,1280]{1,0:T(8,128)S(1)} %slice.121) | data formatting | bytes 184320 | tf_op jit(solution)/shard_map/reshape | solution.py:178
  37.8 1.2 %pad_maximum_fusion = f32[18,18,1280]{2,0,1:T(8,128)S(1)} fusion(f32[1,18,1280]{2,0,1:T(1,128)S(1)} %reshape.163, f32[16,1,1280]{2,0,1:T(8,128)S(1)} %slice_bitcast_fusion, f32[16,16,1280]{2,0,1:T(8,128)S(1)} %concatenate.43, f32[16,1,1280]{2,0,1:T(8,128)S(1)} %slice_bitcast_fusion.1, f32[1,18,1280]{2,0,1:T(1,128)} %reshape.162), kind=kLoop, calls=%fused_computation | loop fusion | flops 1658880 | bytes 3317760 | tf_op jit(solution)/shard_map/concatenate | solution.py:184
  39.6 1.5 %pad.19.clone = f32[18,24,1280]{2,1,0:T(8,128)} pad(f32[18,18,1280]{2,1,0:T(8,128)S(1)} %copy.25, f32[]{:T(128)} %constant.55.clone.1), padding=0_0x0_6x0_0 | pad | bytes 3870724 | tf_op jit(solution)/shard_map/jit(_pad)/pad | solution.py:271
  41.4 4.2 %fusion = f32[1,10,10,10,64]{4,0,3,2,1:T(1,128)S(1)} fusion(bf16[1,12,12,12,64]{4,3,2,1,0:T(8,128)(2,1)S(1)} %fusion.6, bf16[64,3,3,3,64]{4,3,2,1,0:T(4,128)(2,1)S(1)} %reshape.160), kind=kOutput, calls=%fused_computation.3 | convolution fusion | flops 221184000 | bytes 698368 | tf_op jit(solution)/shard_map/conv_general_dilated | solution.py:146
  46.6 0.7 %pad.18.hid_ref = bf16[112,640]{1,0:T(8,128)(2,1)} pad(bf16[100,640]{1,0:T(8,128)(2,1)S(1)} %reshape.161, bf16[]{:T(256)} %constant.53.clone.1), padding=0_12x0_0 | pad | bytes 271362 | tf_op jit(solution)/shard_map/jit(_pad)/pad | solution.py:269
  47.3 15.3 %shard_map.84 = bf16[256,1024]{1,0:T(8,128)(2,1)} custom-call(bf16[112,640]{1,0:T(8,128)(2,1)} %pad.18.hid_ref, bf16[488,112]{1,0:T(8,128)(2,1)} %fusion.9.spread_ref, f32[432,1280]{1,0:T(8,128)} %bitcast.40, f32[256,1024]{1,0:T(8,128)} %get-tuple-element.10.gb_ref, bf16[9,384,256]{2,1,0:T(8,128)(2,1)} %get-tuple-element.11.wa_ref, ...), custom_call_target="tpu_custom_call" | custom-call | tf_op jit(solution)/shard_map/pallas_call | solution.py:133
  (61 shorter events, 4.1 us)
Async XLA Ops:
  2.4 9.0 %collective-permute-start = (bf16[8,4,1280]{2,1,0:T(4,128)(2,1)S(1)}, bf16[8,4,1280]{2,1,0:T(4,128)(2,1)S(1)}, u32[]{:S(2)}, u32[]{:S(2)}) collective-permute-start(bf16[8,4,1280]{2,1,0:T(4,128)(2,1)S(1)} %concatenate.39), channel_id=1, source_target_pairs={{0,1},{1,0},{2,3},{3,2},{4,5},{5,4},{6,7},{7,6},{8,9},{9,8},{10,11... | collective-permute-start | bytes 245768 | tf_op jit(solution)/shard_map/ppermute | solution.py:221
  7.0 3.6 %copy-start = (f32[256,1024]{1,0:T(8,128)S(1)}, f32[256,1024]{1,0:T(8,128)}, u32[]{:S(2)}) copy-start(f32[256,1024]{1,0:T(8,128)} %get-tuple-element.9) | copy-start | bytes 3145732
  8.2 2.3 %collective-permute-start.1 = (f32[16,16,64]{2,0,1:T(8,128)S(1)}, f32[16,16,64]{2,0,1:T(8,128)S(1)}, u32[]{:S(2)}, u32[]{:S(2)}) collective-permute-start(f32[16,16,64]{2,0,1:T(8,128)S(1)} %slice_select_fusion), channel_id=1, source_target_pairs={{0,1},{1,0},{2,3},{3,2},{4,5},{5,4},{6,7},{7,6},{8,9},{9,8},{10,11... | collective-permute-start | bytes 196616 | tf_op jit(solution)/shard_map/ppermute | solution.py:244
  13.8 10.8 %collective-permute-start.3 = (f32[32,1280]{1,0:T(8,128)S(1)}, f32[32,1280]{1,0:T(8,128)S(1)}, u32[]{:S(2)}, u32[]{:S(2)}) collective-permute-start(f32[32,1280]{1,0:T(8,128)S(1)} %pad_maximum_fusion.5), channel_id=1, source_target_pairs={{2,0},{3,1},{6,4},{7,5},{10,8},{11,9},{14,12},{15,13},{18,16},{19,... | collective-permute-start | bytes 491528 | tf_op jit(solution)/shard_map/ppermute | solution.py:181
  15.1 9.5 %collective-permute-start.2 = (f32[32,1280]{1,0:T(8,128)S(1)}, f32[32,1280]{1,0:T(8,128)S(1)}, u32[]{:S(2)}, u32[]{:S(2)}) collective-permute-start(f32[32,1280]{1,0:T(8,128)S(1)} %pad_maximum_fusion.4), channel_id=1, source_target_pairs={{0,2},{1,3},{4,6},{5,7},{8,10},{9,11},{12,14},{13,15},{16,18},{17,... | collective-permute-start | bytes 491528 | tf_op jit(solution)/shard_map/ppermute | solution.py:180
  25.0 10.2 %collective-permute-start.5 = (f32[42,1280]{1,0:T(8,128)S(1)}, f32[42,1280]{1,0:T(8,128)S(1)}, u32[]{:S(2)}, u32[]{:S(2)}) collective-permute-start(f32[42,1280]{1,0:T(8,128)S(1)} %pad_maximum_fusion.3), channel_id=1, source_target_pairs={{4,0},{8,4},{12,8},{5,1},{9,5},{13,9},{6,2},{10,6},{14,10},{7,3},{... | collective-permute-start | bytes 645128 | tf_op jit(solution)/shard_map/ppermute | solution.py:181
  26.3 10.1 %collective-permute-start.4 = (f32[42,1280]{1,0:T(8,128)S(1)}, f32[42,1280]{1,0:T(8,128)S(1)}, u32[]{:S(2)}, u32[]{:S(2)}) collective-permute-start(f32[42,1280]{1,0:T(8,128)S(1)} %pad_maximum_fusion.2), channel_id=1, source_target_pairs={{0,4},{4,8},{8,12},{1,5},{5,9},{9,13},{2,6},{6,10},{10,14},{3,7},{... | collective-permute-start | bytes 645128 | tf_op jit(solution)/shard_map/ppermute | solution.py:180
  41.4 4.3 %copy-start.1 = (s32[12,12,10]{2,1,0:T(8,128)S(1)}, s32[12,12,10]{2,1,0:T(8,128)}, u32[]{:S(2)}) copy-start(s32[12,12,10]{2,1,0:T(8,128)} %iota_add_fusion) | copy-start | bytes 17284
  41.4 4.3 %copy-start.2 = (pred[12,12,20]{2,1,0:T(8,128)(4,1)S(1)}, pred[12,12,20]{2,1,0:T(8,128)(4,1)}, u32[]{:S(2)}) copy-start(pred[12,12,20]{2,1,0:T(8,128)(4,1)} %get-tuple-element.23) | copy-start | bytes 8644
  41.4 4.3 %copy-start.3 = (pred[12,12,20]{2,1,0:T(8,128)(4,1)S(1)}, pred[12,12,20]{2,1,0:T(8,128)(4,1)}, u32[]{:S(2)}) copy-start(pred[12,12,20]{2,1,0:T(8,128)(4,1)} %get-tuple-element.24) | copy-start | bytes 8644

commit v11 on v8

--- a/solution.py
+++ b/solution.py
@@ -74,19 +74,17 @@
     return v / (1.0 + jnp.exp(-v))
 
 
-def band_kernel(wa_raw, wb_raw, wa_ref, wb_ref):
-    build_bands(wa_raw, wa_ref)
-    build_bands(wb_raw, wb_ref)
-
-
-def band_stage(weight_a, weight_b):
-    shape = jax.ShapeDtypeStruct((9, 384, 256), jnp.bfloat16)
-    flops = 2 * 27 * 2 * (64 * 128 * 256 + 384 * 64 * 256)
+def band_kernel(w_raw, w_ref):
+    build_bands(w_raw, w_ref)
+
+
+def band_stage(weight):
+    flops = 27 * 2 * 64 * 128 * 256
     return pl.pallas_call(
         band_kernel,
-        out_shape=(shape, shape),
-        cost_estimate=pl.CostEstimate(flops=flops, transcendentals=0, bytes_accessed=4 * 9 * 384 * 256),
-    )(weight_a, weight_b)
+        out_shape=jax.ShapeDtypeStruct((9, 384, 256), jnp.bfloat16),
+        cost_estimate=pl.CostEstimate(flops=flops, transcendentals=0, bytes_accessed=2 * 9 * 384 * 256),
+    )(weight)
 
 
 def fine_kernel(hid_ref, spread_ref, ga_ref, gb_ref, wa_ref, wb_ref, out_ref, fin_ref, lvl_ref):
@@ -252,6 +250,7 @@
         axis=2,
     )
     region, gate_a = grow_both(packed, gate_a, "gy", 1, (2, 1))
+    late_weight, region = lax.optimization_barrier((fine_weight_b, region))
     region, gate_a = grow_both(region, gate_a, "gx", 0, (2, 1))
     size = region.shape[0]
     volume = region[:, :, :flat_z].reshape(size, size, cells_z, channels)
@@ -276,7 +275,7 @@
     spread = (inside[:, None] & (source[:, None] == jnp.arange(ROWS_C)[None, :])).astype(
         jnp.bfloat16
     )
-    band_a, band_b = band_stage(fine_weight_a, fine_weight_b)
+    band_a, band_b = band_stage(fine_weight_a), band_stage(late_weight)
     out = fine_stage(hid, spread, gate_a, gate_b, band_a, band_b)
     return out.reshape(field.shape)
 

time: 62.8 us -> 63.6 us (1.013)
  other arithmetic: 5.55 us -> 2.49 us
  local copies, waits for them, and re-layouts: 10 us -> 12.3 us
  Pallas kernels: 22.6 us -> 24.8 us
    pallas_call x1 -> x2, Pallas kernels: 3.93 us -> 6.09 us  [band_stage(): pl.pallas_call(band_kernel, out_shape=jax.ShapeDtypeStruct((9, 384, 256),...]
    slice x2, local copies, waits for them, and re-layouts: 0.02 us -> 1.82 us  [unpack(): m[split:].reshape(gate_head.shape)]
    slice x4, local copies, waits for them, and re-layouts: 0.03 us -> 1.83 us  [unpack(): m[:split].reshape(cells_head.shape).astype(cells.dtype)]
    ppermute x2, waiting for transfers between devices: 1.08 us -> 0.01 us  [grow_both(): lax.ppermute(pack(cells_tail, gate_tail), axis, shift_pairs(count, True))]
    concatenate x1, local copies, waits for them, and re-layouts: 0.96 us -> 0.14 us  [body(): mine = jnp.concatenate([coarse, extra], axis=2)]
    concatenate x1 -> x2, other arithmetic: 1.19 us -> 0.46 us  [grow_both(): jnp.concatenate([low[1], gate, high[1]], axis=dim)]
    convert_element_type x1, other arithmetic: 0.72 us -> 0.01 us  [body(): coarse_mask.astype(jnp.bfloat16)]
    dynamic_slice x1 -> x0, other arithmetic: 0.65 us -> none  [body(): lax.dynamic_slice_in_dim(keep, zside * half + 1, half + 2, axis=2)]
  transfers between devices with their start and end apart: 6 -> 6, of which waited for: 3 -> 2; matrix products, arithmetic and copies ran while one was open for 10% -> 5% of each run, Pallas kernels for 12% -> 10%
where the time goes in v11:
time: 63.6 us; the launch traced here: 63.2 us
  Pallas kernels  24.8 us (39%)
  starting transfers between devices  13.2 us (21%)
  local copies, waits for them, and re-layouts  12.3 us (19%)
  matrix products  4.21 us (7%)
  waiting for transfers between devices  3.78 us (6%)
  other arithmetic  2.49 us (4%)
  between operations  2.4 us (4%)
    pallas_call x1, Pallas kernels, fine_stage(): pl.pallas_call(fine_kernel, out_shape=jax.ShapeDtypeStruct(gate_b.shape,...  15.3 us
    ppermute x2, starting transfers between devices, grow_both(): lax.ppermute(pack(cells_tail, gate_tail), axis, shift_pairs(count, True))  10 us
    pallas_call x2, Pallas kernels, band_stage(): pl.pallas_call(band_kernel, out_shape=jax.ShapeDtypeStruct((9, 384, 256),...  6.09 us
    conv_general_dilated x1, matrix products, convolve(): lax.conv_general_dilated(padded[None], kernel, (1, 1, 1), 'VALID', dimens...  4.21 us
    pallas_call x1, Pallas kernels, gate_stage(): pl.pallas_call(gate_kernel, out_shape=(shape, shape))  3.42 us
    ppermute x2, waiting for transfers between devices, grow_both(): lax.ppermute(pack(cells_head, gate_head), axis, shift_pairs(count, False))  3.09 us
    ppermute x2, starting transfers between devices, grow_both(): lax.ppermute(pack(cells_head, gate_head), axis, shift_pairs(count, False))  2.58 us
    reshape x1, local copies, waits for them, and re-layouts, body(): gate_a = gate_a.reshape(field.shape)  1.84 us
  transfers between devices with their start and end apart: 6, of which 2 were waited for; matrix products, arithmetic and copies ran while one was open for 5% of the time, Pallas kernels for 10%

profile of v11, /device:TPU:0, one launch (start us, length us, event | category | flops | bytes accessed | tf_op | source)
XLA Modules:
  0.0 63.2 jit_solution(768065277471070494)
XLA Ops:
  0.7 0.6 broadcast_in_dim.39.live_ref
  1.3 3.4 %shard_map.82 = (f32[256,1024]{1,0:T(8,128)}, f32[256,1024]{1,0:T(8,128)}) custom-call(bf16[256,1024]{1,0:T(8,128)(2,1)} %bitcast.40, bf16[64,128]{1,0:T(8,128)(2,1)} %mw_ref.1, f32[1,128]{1,0:T(1,128)} %broadcast_in_dim.39.live_ref), custom_call_target="tpu_custom_call" | custom-call | tf_op jit(solution)/shard_map/pallas_call | solution.py:70
  4.7 1.8 %copy.23 = f32[16,16,1024]{2,0,1:T(8,128)S(1)} copy(f32[16,16,1024]{2,1,0:T(8,128)} %bitcast.39) | data formatting | bytes 2097152 | tf_op jit(solution)/shard_map/reshape | solution.py:238
  6.7 0.5 collective-permute-start.1
  7.5 0.7 %collective-permute-done.1 = f32[16,16,64]{2,0,1:T(8,128)S(1)} collective-permute-done((f32[16,16,64]{2,0,1:T(8,128)S(1)}, f32[16,16,64]{2,0,1:T(8,128)S(1)}, u32[]{:S(2)}, u32[]{:S(2)}) %collective-permute-start.1) | collective-permute-done | bytes 65568 | tf_op jit(solution)/shard_map/ppermute | solution.py:241
  8.2 0.8 %concatenate.43 = f32[16,16,1280]{2,0,1:T(8,128)S(1)} concatenate(f32[16,16,64]{2,0,1:T(8,128)S(1)} %get-tuple-element.22, f32[16,16,1024]{2,0,1:T(8,128)S(1)} %copy.23, f32[16,16,64]{2,0,1:T(8,128)S(1)} %get-tuple-element.21, f32[16,16,128]{2,0,1:T(8,128)S(1)} %broadcast_in_dim.40), dimensions={2} | concatenate | bytes 2621440 | tf_op jit(solution)/shard_map/concatenate | solution.py:243
  9.0 0.6 slice.106
  11.4 4.8 %collective-permute-start.2 = (f32[32,1280]{1,0:T(8,128)S(1)}, f32[32,1280]{1,0:T(8,128)S(1)}, u32[]{:S(2)}, u32[]{:S(2)}) collective-permute-start(f32[32,1280]{1,0:T(8,128)S(1)} %pad_maximum_fusion.4), channel_id=1, source_target_pairs={{0,2},{1,3},{4,6},{5,7},{8,10},{9,11},{12,14},{13,15},{16,18},{17,... | collective-permute-start | bytes 491528 | tf_op jit(solution)/shard_map/ppermute | solution.py:177
  16.2 1.3 %collective-permute-start.3 = (f32[32,1280]{1,0:T(8,128)S(1)}, f32[32,1280]{1,0:T(8,128)S(1)}, u32[]{:S(2)}, u32[]{:S(2)}) collective-permute-start(f32[32,1280]{1,0:T(8,128)S(1)} %pad_maximum_fusion.5), channel_id=1, source_target_pairs={{2,0},{3,1},{6,4},{7,5},{10,8},{11,9},{14,12},{15,13},{18,16},{19,... | collective-permute-start | bytes 491528 | tf_op jit(solution)/shard_map/ppermute | solution.py:178
  17.9 3.0 %shard_map.83.wa_ref = bf16[9,384,256]{2,1,0:T(8,128)(2,1)} custom-call(bf16[64,1728]{1,0:T(8,128)(2,1)} %w_raw.1), custom_call_target="tpu_custom_call" | custom-call | flops 113246208 | bytes 1769472 | tf_op jit(solution)/shard_map/pallas_call | solution.py:83
  21.0 3.1 %collective-permute-done.3 = f32[32,1280]{1,0:T(8,128)S(1)} collective-permute-done((f32[32,1280]{1,0:T(8,128)S(1)}, f32[32,1280]{1,0:T(8,128)S(1)}, u32[]{:S(2)}, u32[]{:S(2)}) %collective-permute-start.3) | collective-permute-done | bytes 163872 | tf_op jit(solution)/shard_map/ppermute | solution.py:178
  24.6 1.3 %collective-permute-start.5 = (f32[42,1280]{1,0:T(8,128)S(1)}, f32[42,1280]{1,0:T(8,128)}, u32[]{:S(2)}, u32[]{:S(2)}) collective-permute-start(f32[42,1280]{1,0:T(8,128)S(1)} %pad_maximum_fusion.3), channel_id=1, source_target_pairs={{4,0},{8,4},{12,8},{5,1},{9,5},{13,9},{6,2},{10,6},{14,10},{7,3},{... | collective-permute-start | bytes 645128 | tf_op jit(solution)/shard_map/ppermute | solution.py:178
  25.9 5.2 %collective-permute-start.4 = (f32[42,1280]{1,0:T(8,128)S(1)}, f32[42,1280]{1,0:T(8,128)}, u32[]{:S(2)}, u32[]{:S(2)}) collective-permute-start(f32[42,1280]{1,0:T(8,128)S(1)} %pad_maximum_fusion.2), channel_id=1, source_target_pairs={{0,4},{4,8},{8,12},{1,5},{5,9},{9,13},{2,6},{6,10},{10,14},{3,7},{... | collective-permute-start | bytes 645128 | tf_op jit(solution)/shard_map/ppermute | solution.py:177
  31.2 0.9 %fusion.9.spread_ref = bf16[488,112]{1,0:T(8,128)(2,1)} fusion(s32[488]{0:T(512)S(1)} %fusion.17, pred[488]{0:T(512)(128)(4,1)S(1)} %compare_and_fusion), kind=kLoop, calls=%fused_computation.17 | loop fusion | flops 163968 | bytes 111752 | tf_op jit(solution)/shard_map/convert_element_type | solution.py:275
  32.1 3.1 %shard_map.84.wb_ref = bf16[9,384,256]{2,1,0:T(8,128)(2,1)} custom-call(bf16[64,1728]{1,0:T(8,128)(2,1)} %w_raw.2), custom_call_target="tpu_custom_call" | custom-call | flops 113246208 | bytes 1769472 | tf_op jit(solution)/shard_map/pallas_call | solution.py:83
  35.1 0.9 %slice.138 = bf16[24,1280]{1,0:T(8,128)(2,1)S(1)} slice(f32[42,1280]{1,0:T(8,128)} %collective-permute-done.5), slice={[0:24], [0:1280]} | slice | bytes 122880 | tf_op jit(solution)/shard_map/slice | solution.py:175
  36.1 0.9 %slice.139 = bf16[24,1280]{1,0:T(8,128)(2,1)S(1)} slice(f32[42,1280]{1,0:T(8,128)} %collective-permute-done.4), slice={[0:24], [0:1280]} | slice | bytes 122880 | tf_op jit(solution)/shard_map/slice | solution.py:175
  37.1 0.9 %slice.122 = f32[18,1280]{1,0:T(8,128)S(1)} slice(f32[42,1280]{1,0:T(8,128)} %collective-permute-done.5), slice={[24:42], [0:1280]} | slice | bytes 184320 | tf_op jit(solution)/shard_map/slice | solution.py:175
  38.1 0.9 %slice.121 = f32[18,1280]{1,0:T(8,128)S(1)} slice(f32[42,1280]{1,0:T(8,128)} %collective-permute-done.4), slice={[24:42], [0:1280]} | slice | bytes 184320 | tf_op jit(solution)/shard_map/slice | solution.py:175
  39.4 0.6 copy.34
  40.0 1.5 %pad.19.clone = f32[18,24,1280]{2,1,0:T(8,128)} pad(f32[18,18,1280]{2,1,0:T(8,128)S(1)} %copy.34, f32[]{:T(128)} %constant.55.clone.1), padding=0_0x0_6x0_0 | pad | bytes 3870724 | tf_op jit(solution)/shard_map/jit(_pad)/pad | solution.py:269
  42.2 4.2 %fusion = f32[1,10,10,10,64]{4,0,3,2,1:T(1,128)S(1)} fusion(bf16[1,12,12,12,64]{4,3,2,1,0:T(8,128)(2,1)S(1)} %fusion.6, bf16[64,3,3,3,64]{4,3,2,1,0:T(4,128)(2,1)S(1)} %reshape.160), kind=kOutput, calls=%fused_computation.3 | convolution fusion | flops 221184000 | bytes 698368 | tf_op jit(solution)/shard_map/conv_general_dilated | solution.py:143
  47.2 0.7 %pad.18.hid_ref = bf16[112,640]{1,0:T(8,128)(2,1)} pad(bf16[100,640]{1,0:T(8,128)(2,1)S(1)} %reshape.161, bf16[]{:T(256)} %constant.53.clone.1), padding=0_12x0_0 | pad | bytes 271362 | tf_op jit(solution)/shard_map/jit(_pad)/pad | solution.py:267
  47.9 15.3 %shard_map.85 = bf16[256,1024]{1,0:T(8,128)(2,1)} custom-call(bf16[112,640]{1,0:T(8,128)(2,1)} %pad.18.hid_ref, bf16[488,112]{1,0:T(8,128)(2,1)} %fusion.9.spread_ref, f32[432,1280]{1,0:T(8,128)} %bitcast.38, f32[256,1024]{1,0:T(8,128)} %get-tuple-element.11.gb_ref, bf16[9,384,256]{2,1,0:T(8,128)(2,1)} %shard_map.83.wa_ref, ...), custom_call_target="tpu_custom_call" | custom-call | tf_op jit(solution)/shard_map/pallas_call | solution.py:130
  (63 shorter events, 3.8 us)
Async XLA Ops:
  0.0 7.2 %copy-start.2 = (s32[8,4,16]{2,1,0:T(4,128)S(1)}, s32[8,4,16]{2,1,0:T(4,128)}, u32[]{:S(2)}) copy-start(s32[8,4,16]{2,1,0:T(4,128)} %param.9) | copy-start | bytes 6148
  0.0 7.2 %copy-start.1 = (bf16[8,4,1024]{2,1,0:T(4,128)(2,1)S(1)}, bf16[8,4,1024]{2,1,0:T(4,128)(2,1)}, u32[]{:S(2)}) copy-start(bf16[8,4,1024]{2,1,0:T(4,128)(2,1)} %param.8) | copy-start | bytes 196612
  6.7 1.5 %collective-permute-start.1 = (f32[16,16,64]{2,0,1:T(8,128)S(1)}, f32[16,16,64]{2,0,1:T(8,128)S(1)}, u32[]{:S(2)}, u32[]{:S(2)}) collective-permute-start(f32[16,16,64]{2,0,1:T(8,128)S(1)} %slice_select_fusion), channel_id=1, source_target_pairs={{0,1},{1,0},{2,3},{3,2},{4,5},{5,4},{6,7},{7,6},{8,9},{9,8},{10,11... | collective-permute-start | bytes 196616 | tf_op jit(solution)/shard_map/ppermute | solution.py:241
  7.4 1.7 %collective-permute-start = (bf16[8,4,1280]{2,1,0:T(4,128)(2,1)S(1)}, bf16[8,4,1280]{2,1,0:T(4,128)(2,1)S(1)}, u32[]{:S(2)}, u32[]{:S(2)}) collective-permute-start(bf16[8,4,1280]{2,1,0:T(4,128)(2,1)S(1)} %concatenate.39), channel_id=1, source_target_pairs={{0,1},{1,0},{2,3},{3,2},{4,5},{5,4},{6,7},{7,6},{8,9},{9,8},{10,11... | collective-permute-start | bytes 245768 | tf_op jit(solution)/shard_map/ppermute | solution.py:218
  8.2 9.4 %copy-start = (bf16[64,1728]{1,0:T(8,128)(2,1)S(1)}, bf16[64,1728]{1,0:T(8,128)(2,1)}, u32[]{:S(2)}) copy-start(bf16[64,1728]{1,0:T(8,128)(2,1)} %param.12) | copy-start | bytes 663556
  11.4 9.6 %collective-permute-start.2 = (f32[32,1280]{1,0:T(8,128)S(1)}, f32[32,1280]{1,0:T(8,128)S(1)}, u32[]{:S(2)}, u32[]{:S(2)}) collective-permute-start(f32[32,1280]{1,0:T(8,128)S(1)} %pad_maximum_fusion.4), channel_id=1, source_target_pairs={{0,2},{1,3},{4,6},{5,7},{8,10},{9,11},{12,14},{13,15},{16,18},{17,... | collective-permute-start | bytes 491528 | tf_op jit(solution)/shard_map/ppermute | solution.py:177
  16.2 7.9 %collective-permute-start.3 = (f32[32,1280]{1,0:T(8,128)S(1)}, f32[32,1280]{1,0:T(8,128)S(1)}, u32[]{:S(2)}, u32[]{:S(2)}) collective-permute-start(f32[32,1280]{1,0:T(8,128)S(1)} %pad_maximum_fusion.5), channel_id=1, source_target_pairs={{2,0},{3,1},{6,4},{7,5},{10,8},{11,9},{14,12},{15,13},{18,16},{19,... | collective-permute-start | bytes 491528 | tf_op jit(solution)/shard_map/ppermute | solution.py:178
  24.6 10.5 %collective-permute-start.5 = (f32[42,1280]{1,0:T(8,128)S(1)}, f32[42,1280]{1,0:T(8,128)}, u32[]{:S(2)}, u32[]{:S(2)}) collective-permute-start(f32[42,1280]{1,0:T(8,128)S(1)} %pad_maximum_fusion.3), channel_id=1, source_target_pairs={{4,0},{8,4},{12,8},{5,1},{9,5},{13,9},{6,2},{10,6},{14,10},{7,3},{... | collective-permute-start | bytes 645128 | tf_op jit(solution)/shard_map/ppermute | solution.py:178
  25.9 10.1 %collective-permute-start.4 = (f32[42,1280]{1,0:T(8,128)S(1)}, f32[42,1280]{1,0:T(8,128)}, u32[]{:S(2)}, u32[]{:S(2)}) collective-permute-start(f32[42,1280]{1,0:T(8,128)S(1)} %pad_maximum_fusion.2), channel_id=1, source_target_pairs={{0,4},{4,8},{8,12},{1,5},{5,9},{9,13},{2,6},{6,10},{10,14},{3,7},{... | collective-permute-start | bytes 645128 | tf_op jit(solution)/shard_map/ppermute | solution.py:177

commit v12 on v8

--- a/solution.py
+++ b/solution.py
@@ -101,21 +101,25 @@
     shift = (r == c + 64).astype(jnp.bfloat16)
     lvl_ref[ROWS_A:, :] = jnp.zeros((ROWS_L - ROWS_A, LANES_A), jnp.float32)
 
-    def conv(src, weights, rows, chunk):
-        acc = jnp.zeros((rows, 256), jnp.float32)
+    def conv(src, weights, rows, chunk, cells=4):
+        acc = jnp.zeros((rows, 64 * cells), jnp.float32)
         centre = None
         for t in range(9):
             dx, dy = divmod(t, 3)
             off = dx * STRIDE + dy
-            a = src[off : off + rows, 256 * chunk : 256 * chunk + 384].astype(jnp.bfloat16)
-            acc = acc + jnp.dot(a, weights[t], preferred_element_type=jnp.float32)
+            a = src[off : off + rows, 256 * chunk : 256 * chunk + 64 * cells + 128]
+            a = a.astype(jnp.bfloat16)
+            band = weights[t, : 64 * cells + 128, : 64 * cells]
+            acc = acc + jnp.dot(a, band, preferred_element_type=jnp.float32)
             if t == 4:
-                centre = jnp.dot(a, shift, preferred_element_type=jnp.float32)
+                picked = shift[: 64 * cells + 128, : 64 * cells]
+                centre = jnp.dot(a, picked, preferred_element_type=jnp.float32)
         return centre, acc
 
     for k in range(LANES_A // 256):
-        centre, acc = conv(fin_ref, wa_ref, ROWS_A, k)
-        lanes = slice(256 * k, 256 * k + 256)
+        cells = 4 if k < LANES_A // 256 - 1 else 2
+        centre, acc = conv(fin_ref, wa_ref, ROWS_A, k, cells)
+        lanes = slice(256 * k, 256 * k + 64 * cells)
         step = centre + silu(acc) * ga_ref[:, lanes]
         lvl_ref[:ROWS_A, lanes] = step.astype(jnp.bfloat16).astype(jnp.float32)
     for k in range(LANES_B // 256):

time: 62.8 us -> 62.1 us (0.989)
  Pallas kernels: 22.6 us -> 21.9 us
    pallas_call x1, Pallas kernels: 15.3 us -> 14.6 us  [fine_stage(): pl.pallas_call(fine_kernel, out_shape=jax.ShapeDtypeStruct(gate_b.shape,...]
where the time goes in v12:
time: 62.1 us; the launch traced here: 61.7 us
  Pallas kernels  21.9 us (35%)
  starting transfers between devices  13.3 us (21%)
  local copies, waits for them, and re-layouts  10 us (16%)
  other arithmetic  5.55 us (9%)
  waiting for transfers between devices  4.23 us (7%)
  matrix products  4.22 us (7%)
  between operations  2.45 us (4%)
    pallas_call x1, Pallas kernels, fine_stage(): pl.pallas_call(fine_kernel, out_shape=jax.ShapeDtypeStruct(gate_b.shape,...  14.6 us
    ppermute x2, starting transfers between devices, grow_both(): lax.ppermute(pack(cells_tail, gate_tail), axis, shift_pairs(count, True))  10 us
    conv_general_dilated x1, matrix products, convolve(): lax.conv_general_dilated(padded[None], kernel, (1, 1, 1), 'VALID', dimens...  4.22 us
    pallas_call x1, Pallas kernels, band_stage(): pl.pallas_call(band_kernel, out_shape=(shape, shape), cost_estimate=pl.Co...  3.93 us
    pallas_call x1, Pallas kernels, gate_stage(): pl.pallas_call(gate_kernel, out_shape=(shape, shape))  3.42 us
    ppermute x2, waiting for transfers between devices, grow_both(): lax.ppermute(pack(cells_head, gate_head), axis, shift_pairs(count, False))  2.87 us
    ppermute x2, starting transfers between devices, grow_both(): lax.ppermute(pack(cells_head, gate_head), axis, shift_pairs(count, False))  2.58 us
    reshape x1, local copies, waits for them, and re-layouts, body(): gate_a = gate_a.reshape(field.shape)  1.84 us
  transfers between devices with their start and end apart: 6, of which 3 were waited for; matrix products, arithmetic and copies ran while one was open for 10% of the time, Pallas kernels for 12%

profile of v12, /device:TPU:0, one launch (start us, length us, event | category | flops | bytes accessed | tf_op | source)
XLA Modules:
  0.0 61.7 jit_solution(6625244622832619768)
XLA Ops:
  0.7 0.7 %convert_element_type.57 = bf16[8,4,16]{2,1,0:T(4,128)(2,1)S(1)} convert(s32[8,4,16]{2,1,0:T(4,128)} %param.9) | non-fusion elementwise | flops 512 | bytes 3072 | tf_op jit(solution)/shard_map/convert_element_type | solution.py:217
  1.4 1.0 %concatenate.39 = bf16[8,4,1280]{2,1,0:T(4,128)(2,1)S(1)} concatenate(bf16[8,4,1024]{2,1,0:T(4,128)(2,1)} %param.8, bf16[8,4,16]{2,1,0:T(4,128)(2,1)S(1)} %convert_element_type.57, bf16[8,4,1]{2,1,0:T(4,128)(2,1)S(1)} %broadcast_in_dim.33, bf16[8,4,239]{2,1,0:T(4,128)(2,1)S(1)} %broadcast_in_dim.34), dimensions={2} | concatenate | bytes 163840 | tf_op jit(solution)/shard_map/concatenate | solution.py:223
  2.9 0.6 broadcast_in_dim.39.live_ref
  3.5 3.4 %shard_map.82 = (f32[256,1024]{1,0:T(8,128)}, f32[256,1024]{1,0:T(8,128)}) custom-call(bf16[256,1024]{1,0:T(8,128)(2,1)} %bitcast.40, bf16[64,128]{1,0:T(8,128)(2,1)} %mw_ref.1, f32[1,128]{1,0:T(1,128)} %broadcast_in_dim.39.live_ref), custom_call_target="tpu_custom_call" | custom-call | tf_op jit(solution)/shard_map/pallas_call | solution.py:70
  6.9 1.8 %copy.23 = f32[16,16,1024]{2,0,1:T(8,128)S(1)} copy(f32[16,16,1024]{2,1,0:T(8,128)} %bitcast.39) | data formatting | bytes 2097152 | tf_op jit(solution)/shard_map/reshape | solution.py:244
  9.0 0.6 %iota_compare_fusion.1 = (pred[12,12,20]{2,1,0:T(8,128)(4,1)}, pred[12,12,20]{2,1,0:T(8,128)(4,1)}) fusion(), kind=kLoop, calls=%fused_computation.23 | loop fusion | flops 5760 | bytes 5760 | tf_op jit(solution)/shard_map/jit(_pad)/pad | solution.py:264
  10.3 0.8 %concatenate.43 = f32[16,16,1280]{2,0,1:T(8,128)S(1)} concatenate(f32[16,16,64]{2,0,1:T(8,128)S(1)} %get-tuple-element.22, f32[16,16,1024]{2,0,1:T(8,128)S(1)} %copy.23, f32[16,16,64]{2,0,1:T(8,128)S(1)} %get-tuple-element.21, f32[16,16,128]{2,0,1:T(8,128)S(1)} %broadcast_in_dim.40), dimensions={2} | concatenate | bytes 2621440 | tf_op jit(solution)/shard_map/concatenate | solution.py:249
  11.2 0.6 slice.106
  13.6 1.3 %collective-permute-start.3 = (f32[32,1280]{1,0:T(8,128)S(1)}, f32[32,1280]{1,0:T(8,128)S(1)}, u32[]{:S(2)}, u32[]{:S(2)}) collective-permute-start(f32[32,1280]{1,0:T(8,128)S(1)} %pad_maximum_fusion.5), channel_id=1, source_target_pairs={{2,0},{3,1},{6,4},{7,5},{10,8},{11,9},{14,12},{15,13},{18,16},{19,... | collective-permute-start | bytes 491528 | tf_op jit(solution)/shard_map/ppermute | solution.py:184
  14.9 4.6 %collective-permute-start.2 = (f32[32,1280]{1,0:T(8,128)S(1)}, f32[32,1280]{1,0:T(8,128)S(1)}, u32[]{:S(2)}, u32[]{:S(2)}) collective-permute-start(f32[32,1280]{1,0:T(8,128)S(1)} %pad_maximum_fusion.4), channel_id=1, source_target_pairs={{0,2},{1,3},{4,6},{5,7},{8,10},{9,11},{12,14},{13,15},{16,18},{17,... | collective-permute-start | bytes 491528 | tf_op jit(solution)/shard_map/ppermute | solution.py:183
  19.5 3.9 %shard_map.83 = (bf16[9,384,256]{2,1,0:T(8,128)(2,1)}, bf16[9,384,256]{2,1,0:T(8,128)(2,1)}) custom-call(bf16[64,1728]{1,0:T(8,128)(2,1)} %wa_raw.1, bf16[64,1728]{1,0:T(8,128)(2,1)} %wb_raw.1), custom_call_target="tpu_custom_call" | custom-call | flops 905969664 | bytes 3538944 | tf_op jit(solution)/shard_map/pallas_call | solution.py:85
  23.4 0.6 %iota_add_fusion = s32[12,12,10]{2,1,0:T(8,128)} fusion(s32[]{:T(128)S(6)} %select_n.96), kind=kLoop, calls=%fused_computation.30 | loop fusion | flops 1440 | bytes 5764 | tf_op jit(solution)/shard_map/dynamic_slice | solution.py:265
  24.5 1.3 %collective-permute-start.5 = (f32[42,1280]{1,0:T(8,128)S(1)}, f32[42,1280]{1,0:T(8,128)S(1)}, u32[]{:S(2)}, u32[]{:S(2)}) collective-permute-start(f32[42,1280]{1,0:T(8,128)S(1)} %pad_maximum_fusion.3), channel_id=1, source_target_pairs={{4,0},{8,4},{12,8},{5,1},{9,5},{13,9},{6,2},{10,6},{14,10},{7,3},{... | collective-permute-start | bytes 645128 | tf_op jit(solution)/shard_map/ppermute | solution.py:184
  25.9 5.4 %collective-permute-start.4 = (f32[42,1280]{1,0:T(8,128)S(1)}, f32[42,1280]{1,0:T(8,128)S(1)}, u32[]{:S(2)}, u32[]{:S(2)}) collective-permute-start(f32[42,1280]{1,0:T(8,128)S(1)} %pad_maximum_fusion.2), channel_id=1, source_target_pairs={{0,4},{4,8},{8,12},{1,5},{5,9},{9,13},{2,6},{6,10},{10,14},{3,7},{... | collective-permute-start | bytes 645128 | tf_op jit(solution)/shard_map/ppermute | solution.py:183
  31.3 0.9 %fusion.9.spread_ref = bf16[488,112]{1,0:T(8,128)(2,1)} fusion(s32[488]{0:T(512)S(1)} %fusion.29, pred[488]{0:T(512)(128)(4,1)S(1)} %compare_and_fusion), kind=kLoop, calls=%fused_computation.17 | loop fusion | flops 163968 | bytes 111752 | tf_op jit(solution)/shard_map/convert_element_type | solution.py:280
  32.2 2.9 %collective-permute-done.5 = f32[42,1280]{1,0:T(8,128)S(1)} collective-permute-done((f32[42,1280]{1,0:T(8,128)S(1)}, f32[42,1280]{1,0:T(8,128)S(1)}, u32[]{:S(2)}, u32[]{:S(2)}) %collective-permute-start.5) | collective-permute-done | bytes 215072 | tf_op jit(solution)/shard_map/ppermute | solution.py:184
  35.2 1.1 %collective-permute-done.4 = f32[42,1280]{1,0:T(8,128)S(1)} collective-permute-done((f32[42,1280]{1,0:T(8,128)S(1)}, f32[42,1280]{1,0:T(8,128)S(1)}, u32[]{:S(2)}, u32[]{:S(2)}) %collective-permute-start.4) | collective-permute-done | bytes 215072 | tf_op jit(solution)/shard_map/ppermute | solution.py:183
  36.3 0.7 %reshape.162 = f32[1,18,1280]{2,0,1:T(1,128)} reshape(f32[18,1280]{1,0:T(8,128)S(1)} %slice.121) | data formatting | bytes 184320 | tf_op jit(solution)/shard_map/reshape | solution.py:181
  37.6 1.2 %pad_maximum_fusion = f32[18,18,1280]{2,0,1:T(8,128)S(1)} fusion(f32[1,18,1280]{2,0,1:T(1,128)S(1)} %reshape.163, f32[16,1,1280]{2,0,1:T(8,128)S(1)} %slice_bitcast_fusion, f32[16,16,1280]{2,0,1:T(8,128)S(1)} %concatenate.43, f32[16,1,1280]{2,0,1:T(8,128)S(1)} %slice_bitcast_fusion.1, f32[1,18,1280]{2,0,1:T(1,128)} %reshape.162), kind=kLoop, calls=%fused_computation | loop fusion | flops 1658880 | bytes 3317760 | tf_op jit(solution)/shard_map/concatenate | solution.py:187
  38.8 0.6 copy.34
  39.4 1.5 %pad.19.clone = f32[18,24,1280]{2,1,0:T(8,128)} pad(f32[18,18,1280]{2,1,0:T(8,128)S(1)} %copy.34, f32[]{:T(128)} %constant.55.clone.1), padding=0_0x0_6x0_0 | pad | bytes 3870724 | tf_op jit(solution)/shard_map/jit(_pad)/pad | solution.py:274
  41.2 4.2 %fusion = f32[1,10,10,10,64]{4,0,3,2,1:T(1,128)S(1)} fusion(bf16[1,12,12,12,64]{4,3,2,1,0:T(8,128)(2,1)S(1)} %fusion.6, bf16[64,3,3,3,64]{4,3,2,1,0:T(4,128)(2,1)S(1)} %reshape.160), kind=kOutput, calls=%fused_computation.3 | convolution fusion | flops 221184000 | bytes 698368 | tf_op jit(solution)/shard_map/conv_general_dilated | solution.py:149
  46.4 0.7 %pad.18.hid_ref = bf16[112,640]{1,0:T(8,128)(2,1)} pad(bf16[100,640]{1,0:T(8,128)(2,1)S(1)} %reshape.161, bf16[]{:T(256)} %constant.53.clone.1), padding=0_12x0_0 | pad | bytes 271362 | tf_op jit(solution)/shard_map/jit(_pad)/pad | solution.py:272
  47.1 14.6 %shard_map.84 = bf16[256,1024]{1,0:T(8,128)(2,1)} custom-call(bf16[112,640]{1,0:T(8,128)(2,1)} %pad.18.hid_ref, bf16[488,112]{1,0:T(8,128)(2,1)} %fusion.9.spread_ref, f32[432,1280]{1,0:T(8,128)} %bitcast.38, f32[256,1024]{1,0:T(8,128)} %get-tuple-element.10.gb_ref, bf16[9,384,256]{2,1,0:T(8,128)(2,1)} %get-tuple-element.11.wa_ref, ...), custom_call_target="tpu_custom_call" | custom-call | tf_op jit(solution)/shard_map/pallas_call | solution.py:136
  (62 shorter events, 4.3 us)
Async XLA Ops:
  0.0 9.7 %copy-start.1 = (bf16[64,1728]{1,0:T(8,128)(2,1)S(1)}, bf16[64,1728]{1,0:T(8,128)(2,1)}, u32[]{:S(2)}) copy-start(bf16[64,1728]{1,0:T(8,128)(2,1)} %param.12) | copy-start | bytes 663556
  2.4 8.7 %collective-permute-start = (bf16[8,4,1280]{2,1,0:T(4,128)(2,1)S(1)}, bf16[8,4,1280]{2,1,0:T(4,128)(2,1)S(1)}, u32[]{:S(2)}, u32[]{:S(2)}) collective-permute-start(bf16[8,4,1280]{2,1,0:T(4,128)(2,1)S(1)} %concatenate.39), channel_id=1, source_target_pairs={{0,1},{1,0},{2,3},{3,2},{4,5},{5,4},{6,7},{7,6},{8,9},{9,8},{10,11... | collective-permute-start | bytes 245768 | tf_op jit(solution)/shard_map/ppermute | solution.py:224
  8.9 1.4 %collective-permute-start.1 = (f32[16,16,64]{2,0,1:T(8,128)S(1)}, f32[16,16,64]{2,0,1:T(8,128)S(1)}, u32[]{:S(2)}, u32[]{:S(2)}) collective-permute-start(f32[16,16,64]{2,0,1:T(8,128)S(1)} %slice_select_fusion), channel_id=1, source_target_pairs={{0,1},{1,0},{2,3},{3,2},{4,5},{5,4},{6,7},{7,6},{8,9},{9,8},{10,11... | collective-permute-start | bytes 196616 | tf_op jit(solution)/shard_map/ppermute | solution.py:247
  13.6 10.5 %collective-permute-start.3 = (f32[32,1280]{1,0:T(8,128)S(1)}, f32[32,1280]{1,0:T(8,128)S(1)}, u32[]{:S(2)}, u32[]{:S(2)}) collective-permute-start(f32[32,1280]{1,0:T(8,128)S(1)} %pad_maximum_fusion.5), channel_id=1, source_target_pairs={{2,0},{3,1},{6,4},{7,5},{10,8},{11,9},{14,12},{15,13},{18,16},{19,... | collective-permute-start | bytes 491528 | tf_op jit(solution)/shard_map/ppermute | solution.py:184
  14.9 9.2 %collective-permute-start.2 = (f32[32,1280]{1,0:T(8,128)S(1)}, f32[32,1280]{1,0:T(8,128)S(1)}, u32[]{:S(2)}, u32[]{:S(2)}) collective-permute-start(f32[32,1280]{1,0:T(8,128)S(1)} %pad_maximum_fusion.4), channel_id=1, source_target_pairs={{0,2},{1,3},{4,6},{5,7},{8,10},{9,11},{12,14},{13,15},{16,18},{17,... | collective-permute-start | bytes 491528 | tf_op jit(solution)/shard_map/ppermute | solution.py:183
  24.5 10.5 %collective-permute-start.5 = (f32[42,1280]{1,0:T(8,128)S(1)}, f32[42,1280]{1,0:T(8,128)S(1)}, u32[]{:S(2)}, u32[]{:S(2)}) collective-permute-start(f32[42,1280]{1,0:T(8,128)S(1)} %pad_maximum_fusion.3), channel_id=1, source_target_pairs={{4,0},{8,4},{12,8},{5,1},{9,5},{13,9},{6,2},{10,6},{14,10},{7,3},{... | collective-permute-start | bytes 645128 | tf_op jit(solution)/shard_map/ppermute | solution.py:184
  25.9 10.4 %collective-permute-start.4 = (f32[42,1280]{1,0:T(8,128)S(1)}, f32[42,1280]{1,0:T(8,128)S(1)}, u32[]{:S(2)}, u32[]{:S(2)}) collective-permute-start(f32[42,1280]{1,0:T(8,128)S(1)} %pad_maximum_fusion.2), channel_id=1, source_target_pairs={{0,4},{4,8},{8,12},{1,5},{5,9},{9,13},{2,6},{6,10},{10,14},{3,7},{... | collective-permute-start | bytes 645128 | tf_op jit(solution)/shard_map/ppermute | solution.py:183
  41.2 4.3 %copy-start = (s32[12,12,10]{2,1,0:T(8,128)S(1)}, s32[12,12,10]{2,1,0:T(8,128)}, u32[]{:S(2)}) copy-start(s32[12,12,10]{2,1,0:T(8,128)} %iota_add_fusion) | copy-start | bytes 17284
  41.2 4.3 %copy-start.2 = (pred[12,12,20]{2,1,0:T(8,128)(4,1)S(1)}, pred[12,12,20]{2,1,0:T(8,128)(4,1)}, u32[]{:S(2)}) copy-start(pred[12,12,20]{2,1,0:T(8,128)(4,1)} %get-tuple-element.23) | copy-start | bytes 8644
  41.2 4.3 %copy-start.3 = (pred[12,12,20]{2,1,0:T(8,128)(4,1)S(1)}, pred[12,12,20]{2,1,0:T(8,128)(4,1)}, u32[]{:S(2)}) copy-start(pred[12,12,20]{2,1,0:T(8,128)(4,1)} %get-tuple-element.24) | copy-start | bytes 8644

commit v13 on v12

--- a/solution.py
+++ b/solution.py
@@ -13,7 +13,7 @@
 ROWS_A = 432
 ROWS_B = 384
 ROWS_L = 440
-LANES_F = 1408
+LANES_F = 1280
 LANES_A = 1280
 LANES_B = 1024
 

time: 62.1 us -> 62 us (level)
  no operation moved by 1% of the time
where the time goes in v13:
time: 62 us; the launch traced here: 61.6 us
  Pallas kernels  21.8 us (35%)
  starting transfers between devices  13.3 us (21%)
  local copies, waits for them, and re-layouts  10 us (16%)
  other arithmetic  5.55 us (9%)
  waiting for transfers between devices  4.23 us (7%)
  matrix products  4.22 us (7%)
  between operations  2.45 us (4%)
    pallas_call x1, Pallas kernels, fine_stage(): pl.pallas_call(fine_kernel, out_shape=jax.ShapeDtypeStruct(gate_b.shape,...  14.4 us
    ppermute x2, starting transfers between devices, grow_both(): lax.ppermute(pack(cells_tail, gate_tail), axis, shift_pairs(count, True))  10 us
    conv_general_dilated x1, matrix products, convolve(): lax.conv_general_dilated(padded[None], kernel, (1, 1, 1), 'VALID', dimens...  4.22 us
    pallas_call x1, Pallas kernels, band_stage(): pl.pallas_call(band_kernel, out_shape=(shape, shape), cost_estimate=pl.Co...  3.93 us
    pallas_call x1, Pallas kernels, gate_stage(): pl.pallas_call(gate_kernel, out_shape=(shape, shape))  3.42 us
    ppermute x2, waiting for transfers between devices, grow_both(): lax.ppermute(pack(cells_head, gate_head), axis, shift_pairs(count, False))  2.87 us
    ppermute x2, starting transfers between devices, grow_both(): lax.ppermute(pack(cells_head, gate_head), axis, shift_pairs(count, False))  2.58 us
    reshape x1, local copies, waits for them, and re-layouts, body(): gate_a = gate_a.reshape(field.shape)  1.84 us
  transfers between devices with their start and end apart: 6, of which 3 were waited for; matrix products, arithmetic and copies ran while one was open for 10% of the time, Pallas kernels for 12%

profile of v13, /device:TPU:0, one launch (start us, length us, event | category | flops | bytes accessed | tf_op | source)
XLA Modules:
  0.0 61.6 jit_solution(469411418397915585)
XLA Ops:
  0.7 0.7 %convert_element_type.57 = bf16[8,4,16]{2,1,0:T(4,128)(2,1)S(1)} convert(s32[8,4,16]{2,1,0:T(4,128)} %param.9) | non-fusion elementwise | flops 512 | bytes 3072 | tf_op jit(solution)/shard_map/convert_element_type | solution.py:217
  1.4 1.0 %concatenate.39 = bf16[8,4,1280]{2,1,0:T(4,128)(2,1)S(1)} concatenate(bf16[8,4,1024]{2,1,0:T(4,128)(2,1)} %param.8, bf16[8,4,16]{2,1,0:T(4,128)(2,1)S(1)} %convert_element_type.57, bf16[8,4,1]{2,1,0:T(4,128)(2,1)S(1)} %broadcast_in_dim.33, bf16[8,4,239]{2,1,0:T(4,128)(2,1)S(1)} %broadcast_in_dim.34), dimensions={2} | concatenate | bytes 163840 | tf_op jit(solution)/shard_map/concatenate | solution.py:223
  2.9 0.6 broadcast_in_dim.39.live_ref
  3.5 3.4 %shard_map.82 = (f32[256,1024]{1,0:T(8,128)}, f32[256,1024]{1,0:T(8,128)}) custom-call(bf16[256,1024]{1,0:T(8,128)(2,1)} %bitcast.40, bf16[64,128]{1,0:T(8,128)(2,1)} %mw_ref.1, f32[1,128]{1,0:T(1,128)} %broadcast_in_dim.39.live_ref), custom_call_target="tpu_custom_call" | custom-call | tf_op jit(solution)/shard_map/pallas_call | solution.py:70
  6.9 1.8 %copy.23 = f32[16,16,1024]{2,0,1:T(8,128)S(1)} copy(f32[16,16,1024]{2,1,0:T(8,128)} %bitcast.39) | data formatting | bytes 2097152 | tf_op jit(solution)/shard_map/reshape | solution.py:244
  9.0 0.6 %iota_compare_fusion.1 = (pred[12,12,20]{2,1,0:T(8,128)(4,1)}, pred[12,12,20]{2,1,0:T(8,128)(4,1)}) fusion(), kind=kLoop, calls=%fused_computation.23 | loop fusion | flops 5760 | bytes 5760 | tf_op jit(solution)/shard_map/jit(_pad)/pad | solution.py:264
  10.3 0.8 %concatenate.43 = f32[16,16,1280]{2,0,1:T(8,128)S(1)} concatenate(f32[16,16,64]{2,0,1:T(8,128)S(1)} %get-tuple-element.22, f32[16,16,1024]{2,0,1:T(8,128)S(1)} %copy.23, f32[16,16,64]{2,0,1:T(8,128)S(1)} %get-tuple-element.21, f32[16,16,128]{2,0,1:T(8,128)S(1)} %broadcast_in_dim.40), dimensions={2} | concatenate | bytes 2621440 | tf_op jit(solution)/shard_map/concatenate | solution.py:249
  11.2 0.6 slice.106
  13.6 1.3 %collective-permute-start.3 = (f32[32,1280]{1,0:T(8,128)S(1)}, f32[32,1280]{1,0:T(8,128)S(1)}, u32[]{:S(2)}, u32[]{:S(2)}) collective-permute-start(f32[32,1280]{1,0:T(8,128)S(1)} %pad_maximum_fusion.5), channel_id=1, source_target_pairs={{2,0},{3,1},{6,4},{7,5},{10,8},{11,9},{14,12},{15,13},{18,16},{19,... | collective-permute-start | bytes 491528 | tf_op jit(solution)/shard_map/ppermute | solution.py:184
  14.9 4.6 %collective-permute-start.2 = (f32[32,1280]{1,0:T(8,128)S(1)}, f32[32,1280]{1,0:T(8,128)S(1)}, u32[]{:S(2)}, u32[]{:S(2)}) collective-permute-start(f32[32,1280]{1,0:T(8,128)S(1)} %pad_maximum_fusion.4), channel_id=1, source_target_pairs={{0,2},{1,3},{4,6},{5,7},{8,10},{9,11},{12,14},{13,15},{16,18},{17,... | collective-permute-start | bytes 491528 | tf_op jit(solution)/shard_map/ppermute | solution.py:183
  19.5 3.9 %shard_map.83 = (bf16[9,384,256]{2,1,0:T(8,128)(2,1)}, bf16[9,384,256]{2,1,0:T(8,128)(2,1)}) custom-call(bf16[64,1728]{1,0:T(8,128)(2,1)} %wa_raw.1, bf16[64,1728]{1,0:T(8,128)(2,1)} %wb_raw.1), custom_call_target="tpu_custom_call" | custom-call | flops 905969664 | bytes 3538944 | tf_op jit(solution)/shard_map/pallas_call | solution.py:85
  23.4 0.6 %iota_add_fusion = s32[12,12,10]{2,1,0:T(8,128)} fusion(s32[]{:T(128)S(6)} %select_n.96), kind=kLoop, calls=%fused_computation.30 | loop fusion | flops 1440 | bytes 5764 | tf_op jit(solution)/shard_map/dynamic_slice | solution.py:265
  24.5 1.3 %collective-permute-start.5 = (f32[42,1280]{1,0:T(8,128)S(1)}, f32[42,1280]{1,0:T(8,128)S(1)}, u32[]{:S(2)}, u32[]{:S(2)}) collective-permute-start(f32[42,1280]{1,0:T(8,128)S(1)} %pad_maximum_fusion.3), channel_id=1, source_target_pairs={{4,0},{8,4},{12,8},{5,1},{9,5},{13,9},{6,2},{10,6},{14,10},{7,3},{... | collective-permute-start | bytes 645128 | tf_op jit(solution)/shard_map/ppermute | solution.py:184
  25.9 5.4 %collective-permute-start.4 = (f32[42,1280]{1,0:T(8,128)S(1)}, f32[42,1280]{1,0:T(8,128)S(1)}, u32[]{:S(2)}, u32[]{:S(2)}) collective-permute-start(f32[42,1280]{1,0:T(8,128)S(1)} %pad_maximum_fusion.2), channel_id=1, source_target_pairs={{0,4},{4,8},{8,12},{1,5},{5,9},{9,13},{2,6},{6,10},{10,14},{3,7},{... | collective-permute-start | bytes 645128 | tf_op jit(solution)/shard_map/ppermute | solution.py:183
  31.3 0.9 %fusion.9.spread_ref = bf16[488,112]{1,0:T(8,128)(2,1)} fusion(s32[488]{0:T(512)S(1)} %fusion.29, pred[488]{0:T(512)(128)(4,1)S(1)} %compare_and_fusion), kind=kLoop, calls=%fused_computation.17 | loop fusion | flops 163968 | bytes 111752 | tf_op jit(solution)/shard_map/convert_element_type | solution.py:280
  32.2 2.9 %collective-permute-done.5 = f32[42,1280]{1,0:T(8,128)S(1)} collective-permute-done((f32[42,1280]{1,0:T(8,128)S(1)}, f32[42,1280]{1,0:T(8,128)S(1)}, u32[]{:S(2)}, u32[]{:S(2)}) %collective-permute-start.5) | collective-permute-done | bytes 215072 | tf_op jit(solution)/shard_map/ppermute | solution.py:184
  35.2 1.1 %collective-permute-done.4 = f32[42,1280]{1,0:T(8,128)S(1)} collective-permute-done((f32[42,1280]{1,0:T(8,128)S(1)}, f32[42,1280]{1,0:T(8,128)S(1)}, u32[]{:S(2)}, u32[]{:S(2)}) %collective-permute-start.4) | collective-permute-done | bytes 215072 | tf_op jit(solution)/shard_map/ppermute | solution.py:183
  36.3 0.7 %reshape.162 = f32[1,18,1280]{2,0,1:T(1,128)} reshape(f32[18,1280]{1,0:T(8,128)S(1)} %slice.121) | data formatting | bytes 184320 | tf_op jit(solution)/shard_map/reshape | solution.py:181
  37.6 1.2 %pad_maximum_fusion = f32[18,18,1280]{2,0,1:T(8,128)S(1)} fusion(f32[1,18,1280]{2,0,1:T(1,128)S(1)} %reshape.163, f32[16,1,1280]{2,0,1:T(8,128)S(1)} %slice_bitcast_fusion, f32[16,16,1280]{2,0,1:T(8,128)S(1)} %concatenate.43, f32[16,1,1280]{2,0,1:T(8,128)S(1)} %slice_bitcast_fusion.1, f32[1,18,1280]{2,0,1:T(1,128)} %reshape.162), kind=kLoop, calls=%fused_computation | loop fusion | flops 1658880 | bytes 3317760 | tf_op jit(solution)/shard_map/concatenate | solution.py:187
  38.8 0.6 copy.34
  39.4 1.5 %pad.19.clone = f32[18,24,1280]{2,1,0:T(8,128)} pad(f32[18,18,1280]{2,1,0:T(8,128)S(1)} %copy.34, f32[]{:T(128)} %constant.55.clone.1), padding=0_0x0_6x0_0 | pad | bytes 3870724 | tf_op jit(solution)/shard_map/jit(_pad)/pad | solution.py:274
  41.2 4.2 %fusion = f32[1,10,10,10,64]{4,0,3,2,1:T(1,128)S(1)} fusion(bf16[1,12,12,12,64]{4,3,2,1,0:T(8,128)(2,1)S(1)} %fusion.6, bf16[64,3,3,3,64]{4,3,2,1,0:T(4,128)(2,1)S(1)} %reshape.160), kind=kOutput, calls=%fused_computation.3 | convolution fusion | flops 221184000 | bytes 698368 | tf_op jit(solution)/shard_map/conv_general_dilated | solution.py:149
  46.4 0.7 %pad.18.hid_ref = bf16[112,640]{1,0:T(8,128)(2,1)} pad(bf16[100,640]{1,0:T(8,128)(2,1)S(1)} %reshape.161, bf16[]{:T(256)} %constant.53.clone.1), padding=0_12x0_0 | pad | bytes 271362 | tf_op jit(solution)/shard_map/jit(_pad)/pad | solution.py:272
  47.1 14.4 %shard_map.84 = bf16[256,1024]{1,0:T(8,128)(2,1)} custom-call(bf16[112,640]{1,0:T(8,128)(2,1)} %pad.18.hid_ref, bf16[488,112]{1,0:T(8,128)(2,1)} %fusion.9.spread_ref, f32[432,1280]{1,0:T(8,128)} %bitcast.38, f32[256,1024]{1,0:T(8,128)} %get-tuple-element.10.gb_ref, bf16[9,384,256]{2,1,0:T(8,128)(2,1)} %get-tuple-element.11.wa_ref, ...), custom_call_target="tpu_custom_call" | custom-call | tf_op jit(solution)/shard_map/pallas_call | solution.py:136
  (62 shorter events, 4.3 us)
Async XLA Ops:
  0.0 9.7 %copy-start.1 = (bf16[64,1728]{1,0:T(8,128)(2,1)S(1)}, bf16[64,1728]{1,0:T(8,128)(2,1)}, u32[]{:S(2)}) copy-start(bf16[64,1728]{1,0:T(8,128)(2,1)} %param.12) | copy-start | bytes 663556
  2.4 8.7 %collective-permute-start = (bf16[8,4,1280]{2,1,0:T(4,128)(2,1)S(1)}, bf16[8,4,1280]{2,1,0:T(4,128)(2,1)S(1)}, u32[]{:S(2)}, u32[]{:S(2)}) collective-permute-start(bf16[8,4,1280]{2,1,0:T(4,128)(2,1)S(1)} %concatenate.39), channel_id=1, source_target_pairs={{0,1},{1,0},{2,3},{3,2},{4,5},{5,4},{6,7},{7,6},{8,9},{9,8},{10,11... | collective-permute-start | bytes 245768 | tf_op jit(solution)/shard_map/ppermute | solution.py:224
  8.9 1.4 %collective-permute-start.1 = (f32[16,16,64]{2,0,1:T(8,128)S(1)}, f32[16,16,64]{2,0,1:T(8,128)S(1)}, u32[]{:S(2)}, u32[]{:S(2)}) collective-permute-start(f32[16,16,64]{2,0,1:T(8,128)S(1)} %slice_select_fusion), channel_id=1, source_target_pairs={{0,1},{1,0},{2,3},{3,2},{4,5},{5,4},{6,7},{7,6},{8,9},{9,8},{10,11... | collective-permute-start | bytes 196616 | tf_op jit(solution)/shard_map/ppermute | solution.py:247
  13.6 10.5 %collective-permute-start.3 = (f32[32,1280]{1,0:T(8,128)S(1)}, f32[32,1280]{1,0:T(8,128)S(1)}, u32[]{:S(2)}, u32[]{:S(2)}) collective-permute-start(f32[32,1280]{1,0:T(8,128)S(1)} %pad_maximum_fusion.5), channel_id=1, source_target_pairs={{2,0},{3,1},{6,4},{7,5},{10,8},{11,9},{14,12},{15,13},{18,16},{19,... | collective-permute-start | bytes 491528 | tf_op jit(solution)/shard_map/ppermute | solution.py:184
  14.9 9.2 %collective-permute-start.2 = (f32[32,1280]{1,0:T(8,128)S(1)}, f32[32,1280]{1,0:T(8,128)S(1)}, u32[]{:S(2)}, u32[]{:S(2)}) collective-permute-start(f32[32,1280]{1,0:T(8,128)S(1)} %pad_maximum_fusion.4), channel_id=1, source_target_pairs={{0,2},{1,3},{4,6},{5,7},{8,10},{9,11},{12,14},{13,15},{16,18},{17,... | collective-permute-start | bytes 491528 | tf_op jit(solution)/shard_map/ppermute | solution.py:183
  24.5 10.5 %collective-permute-start.5 = (f32[42,1280]{1,0:T(8,128)S(1)}, f32[42,1280]{1,0:T(8,128)S(1)}, u32[]{:S(2)}, u32[]{:S(2)}) collective-permute-start(f32[42,1280]{1,0:T(8,128)S(1)} %pad_maximum_fusion.3), channel_id=1, source_target_pairs={{4,0},{8,4},{12,8},{5,1},{9,5},{13,9},{6,2},{10,6},{14,10},{7,3},{... | collective-permute-start | bytes 645128 | tf_op jit(solution)/shard_map/ppermute | solution.py:184
  25.9 10.4 %collective-permute-start.4 = (f32[42,1280]{1,0:T(8,128)S(1)}, f32[42,1280]{1,0:T(8,128)S(1)}, u32[]{:S(2)}, u32[]{:S(2)}) collective-permute-start(f32[42,1280]{1,0:T(8,128)S(1)} %pad_maximum_fusion.2), channel_id=1, source_target_pairs={{0,4},{4,8},{8,12},{1,5},{5,9},{9,13},{2,6},{6,10},{10,14},{3,7},{... | collective-permute-start | bytes 645128 | tf_op jit(solution)/shard_map/ppermute | solution.py:183
  41.2 4.3 %copy-start = (s32[12,12,10]{2,1,0:T(8,128)S(1)}, s32[12,12,10]{2,1,0:T(8,128)}, u32[]{:S(2)}) copy-start(s32[12,12,10]{2,1,0:T(8,128)} %iota_add_fusion) | copy-start | bytes 17284
  41.2 4.3 %copy-start.2 = (pred[12,12,20]{2,1,0:T(8,128)(4,1)S(1)}, pred[12,12,20]{2,1,0:T(8,128)(4,1)}, u32[]{:S(2)}) copy-start(pred[12,12,20]{2,1,0:T(8,128)(4,1)} %get-tuple-element.23) | copy-start | bytes 8644
  41.2 4.3 %copy-start.3 = (pred[12,12,20]{2,1,0:T(8,128)(4,1)S(1)}, pred[12,12,20]{2,1,0:T(8,128)(4,1)}, u32[]{:S(2)}) copy-start(pred[12,12,20]{2,1,0:T(8,128)(4,1)} %get-tuple-element.24) | copy-start | bytes 8644
